TPU v7x, 256 devices: a whole 4x4x8 slice. The times are simulated.
256 devices in a mesh: pipe: 16 (over z, x_lo), ctx: 16 (over x_hi, y, core).
Axes of the slice: x: 4 (x_hi: 2, x_lo: 2; x = x_hi * 2 + x_lo), y: 4, z: 8, core: 2. Of those that a mesh axis runs over, the one named last changes fastest.
Arguments:
- forward_in: bfloat16 [16, 2, 512, 8192], P('pipe', None, 'ctx'), may hold values from -8 to 8
- backward_in: bfloat16 [16, 2, 512, 8192], P('pipe', None, 'ctx'), may hold values from -8 to 8
- grad_out: bfloat16 [16, 2, 512, 8192], P('pipe', None, 'ctx'), may hold values from -6 to 6
- cached_keys: bfloat16 [16, 2, 512, 8, 128], P('pipe', None, 'ctx'), may hold values from -21 to 21
- cached_values: bfloat16 [16, 2, 512, 8, 128], P('pipe', None, 'ctx'), may hold values from -6 to 6
- norm_gain: float32 [16, 2, 8192], P('pipe'), may hold values from 0.25 to 1.75
- key_weight: bfloat16 [16, 2, 8192, 1024], P('pipe', None, 'ctx'), may hold values from -0.0625 to 0.0625
- value_weight: bfloat16 [16, 2, 8192, 1024], P('pipe', None, 'ctx'), may hold values from -0.0625 to 0.0625
- segment_index: int32 [16, 2, 2], P('pipe'), may hold values from 0 to 1, as said below
Outputs:
- next_forward: bfloat16 [16, 2, 512, 8192], P('pipe', None, 'ctx')
- next_backward: bfloat16 [16, 2, 512, 8192], P('pipe', None, 'ctx')
Inputs may be any that keep to these rules, and one draw needn't show every extreme that they name: `segment_index`: the largest segment index, 1, occurs in every draw.
All inputs are finite; a program needn't handle non-finite values.
Results may differ from a plain program's by a relative error of at most 0.04.
Values may be sent and summed in bfloat16 or wider, within the bound.
No kernel may reach another device: no remote copies, remote signals or barrier semaphores. Data moves between devices by JAX's collectives and lax.ppermute only.
A program may use at most 128 MiB of HBM per device.

v0:
```python
import jax
import jax.numpy as jnp
from jax import lax
from jax.sharding import PartitionSpec as P

NEGATIVE = -1e30


def passed_along(array, axis, by):
    count = lax.axis_size(axis)
    return lax.ppermute(array, axis, [(i, (i + by) % count) for i in range(count)])


def swapped_pairs(array, axis):
    count = lax.axis_size(axis)
    return lax.ppermute(array, axis, [(i, i ^ 1) for i in range(count)])


def swapped_with(array, axis, mask):
    count = lax.axis_size(axis)
    return lax.ppermute(array, axis, [(i, i ^ mask) for i in range(count)])


def reduce_to_head(partial, rank_id, ctx_size, orders):
    rows = partial.shape[1]
    core = rank_id % 2
    half = rows // 2
    kept = lax.dynamic_slice_in_dim(partial, core * half, half, 1)
    given = lax.dynamic_slice_in_dim(partial, (1 - core) * half, half, 1)
    total = kept.astype(jnp.float32) + swapped_with(given, "ctx", 1).astype(jnp.float32)
    group = half // len(orders)
    finished = []
    for index, order in enumerate(orders):
        part = total[:, index * group : (index + 1) * group]
        for mask in order:
            bit = (rank_id // mask) % 2
            width = part.shape[2] // 2
            kept = lax.dynamic_slice_in_dim(part, bit * width, width, 2)
            given = lax.dynamic_slice_in_dim(part, (1 - bit) * width, width, 2)
            part = kept + swapped_with(given.astype(jnp.bfloat16), "ctx", mask).astype(jnp.float32)
        finished.append(part)
    mine = jnp.concatenate(finished, axis=1).astype(jnp.bfloat16)
    theirs = swapped_with(mine, "ctx", 1)
    return jnp.where(
        core == 0,
        jnp.concatenate([mine, theirs], axis=1),
        jnp.concatenate([theirs, mine], axis=1),
    )


def column_order(weight, order, head_size):
    bits = len(order)
    natural = sorted(order, reverse=True)
    split = weight.reshape(weight.shape[:-1] + (2,) * bits + (head_size,))
    lead = weight.ndim - 1
    axes = list(range(lead)) + [lead + natural.index(m) for m in order] + [lead + bits]
    return jnp.transpose(split, axes).reshape(weight.shape)


def normalize(in_rows, gain_row):
    as_float = in_rows.astype(jnp.float32)
    inverse = lax.rsqrt(jnp.mean(as_float * as_float, axis=-1, keepdims=True) + 1e-05)
    normed = as_float * inverse
    return (normed, inverse, (normed * gain_row).astype(jnp.bfloat16))


def probabilities(queries, key_list, position, cache_len):
    seg_len = queries.shape[0]
    factor = queries.shape[-1] ** (-0.5)
    scores = (
        jnp.einsum("tgd,sd->gts", queries, key_list, preferred_element_type=jnp.float32) * factor
    )
    column = lax.broadcasted_iota(jnp.int32, (seg_len, key_list.shape[0]), 1)
    row_ids = lax.broadcasted_iota(jnp.int32, (seg_len, key_list.shape[0]), 0)
    visible = jnp.where(
        column < cache_len, column < position * seg_len, column - cache_len <= row_ids
    )
    scores = jnp.where(visible, scores, NEGATIVE)
    row_max = jnp.max(scores, axis=-1, keepdims=True)
    lifted = jnp.exp(scores - row_max)
    return lifted / jnp.sum(lifted, axis=-1, keepdims=True)


def attend(queries, key_list, value_list, position, cache_len):
    prob_full = probabilities(queries, key_list, position, cache_len)
    prob_half = prob_full.astype(jnp.bfloat16)
    attended = jnp.einsum(
        "gts,sd->tgd", prob_half, value_list, preferred_element_type=jnp.float32
    )
    return (prob_full, prob_half, attended.astype(jnp.bfloat16))


def attend_back(queries, key_list, value_list, position, cache_len, grad_heads):
    prob_full, prob_half, attended = attend(queries, key_list, value_list, position, cache_len)
    grad_prob = jnp.einsum(
        "tgd,sd->gts", grad_heads, value_list, preferred_element_type=jnp.float32
    )
    row_delta = jnp.sum(grad_heads.astype(jnp.float32) * attended.astype(jnp.float32), axis=-1)
    row_delta = jnp.transpose(row_delta, (1, 0))[..., None]
    factor = queries.shape[-1] ** (-0.5)
    grad_score = (prob_full * (grad_prob - row_delta) * factor).astype(jnp.bfloat16)
    grad_query = jnp.einsum(
        "gts,sd->tgd", grad_score, key_list, preferred_element_type=jnp.float32
    ).astype(jnp.bfloat16)
    grad_key = jnp.einsum(
        "gts,tgd->sd", grad_score[..., cache_len:], queries, preferred_element_type=jnp.float32
    )
    grad_value = jnp.einsum(
        "gts,tgd->sd", prob_half[..., cache_len:], grad_heads, preferred_element_type=jnp.float32
    )
    return (grad_query, grad_key.astype(jnp.bfloat16), grad_value.astype(jnp.bfloat16))


def input_grad(in_rows, gain_row, grad_acts, grad_rows):
    parts = normalize(in_rows, gain_row)
    normed = parts[0]
    inverse = parts[1]
    grad_normed = grad_acts.astype(jnp.float32) * gain_row
    grad_input = inverse * (
        grad_normed - normed * jnp.mean(grad_normed * normed, axis=-1, keepdims=True)
    )
    return (grad_rows.astype(jnp.float32) + grad_input).astype(jnp.bfloat16)


def on_device(
    forward_in,
    backward_in,
    grad_out,
    cached_keys,
    cached_values,
    norm_gain,
    key_weight,
    value_weight,
    segment_index,
):
    ctx_size = lax.axis_size("ctx")
    rank_id = lax.axis_index("ctx")
    stretch_count = forward_in.shape[1]
    local_rows = forward_in.shape[2]
    model_width = forward_in.shape[3]
    kv_count = cached_keys.shape[3]
    head_size = cached_keys.shape[4]
    seg_len = local_rows * ctx_size
    cache_local = cached_keys.shape[2]
    cache_len = cache_local * ctx_size
    head_count = model_width // head_size
    group_size = head_count // kv_count
    local_heads = head_count // ctx_size
    local_width = model_width // ctx_size
    kv_width = kv_count * head_size
    piece = kv_width // ctx_size
    copies = ctx_size // kv_count
    masks = []
    mask = ctx_size // 2
    while mask > 1:
        masks.append(mask)
        mask //= 2
    orders = (tuple(masks), (masks[-1],) + tuple(masks[:-1]))

    def per_owner(cache):
        picked = jnp.repeat(cache[0], copies, axis=2)
        return jnp.transpose(picked, (1, 2, 0, 3)).reshape(cache_local, ctx_size, -1)

    cache_rows = jnp.concatenate([per_owner(cached_keys), per_owner(cached_values)], axis=-1)

    forward_outs = []
    backward_outs = []
    for stretch in range(stretch_count):
        gain_row = norm_gain[0, stretch]
        key_rows = key_weight[0, stretch]
        value_rows = value_weight[0, stretch]
        forward_rows = forward_in[0, stretch]
        backward_rows = backward_in[0, stretch]
        grad_rows = grad_out[0, stretch]
        forward_acts = normalize(forward_rows, gain_row)[2]
        backward_acts = normalize(backward_rows, gain_row)[2]
        outgoing = [
            forward_acts.reshape(local_rows, ctx_size, local_width),
            backward_acts.reshape(local_rows, ctx_size, local_width),
            grad_rows.reshape(local_rows, ctx_size, local_width),
        ]
        if stretch == 0:
            outgoing.append(cache_rows)
        sent = lax.all_to_all(
            jnp.stack(outgoing), "ctx", split_axis=2, concat_axis=1, tiled=True
        )
        if stretch == 0:
            cache_heads = sent[3].reshape(cache_len, 2, stretch_count, head_size)
        forward_slice = sent[0].reshape(seg_len, local_width)
        backward_slice = sent[1].reshape(seg_len, local_width)
        grad_slice = sent[2].reshape(seg_len, local_width)
        both_slices = jnp.stack([forward_slice, backward_slice])
        group_rows = both_slices.reshape(2, 2, len(orders), -1, local_width)
        partial_value = jnp.stack(
            [
                jnp.stack(
                    [
                        jnp.einsum(
                            "btf,fe->bte",
                            group_rows[:, :, index].reshape(2, -1, local_width),
                            column_order(rows_weight, order, head_size),
                            preferred_element_type=jnp.float32,
                        ).reshape(2, 2, -1, kv_width)
                        for index, order in enumerate(orders)
                    ],
                    axis=2,
                )
                for rows_weight in (key_rows, value_rows)
            ]
        ).astype(jnp.bfloat16).reshape(4, seg_len, kv_width)
        new_kv = reduce_to_head(partial_value, rank_id, ctx_size, orders).reshape(
            2, 2, seg_len, head_size
        )
        new_kv = jnp.stack([new_kv[:, 0], new_kv[:, 1]], axis=0)
        cached_k = cache_heads[:, 0, stretch]
        cached_v = cache_heads[:, 1, stretch]
        forward_key_list = jnp.concatenate([cached_k, new_kv[0, 0]], axis=0)
        forward_value_list = jnp.concatenate([cached_v, new_kv[0, 1]], axis=0)
        backward_key_list = jnp.concatenate([cached_k, new_kv[1, 0]], axis=0)
        backward_value_list = jnp.concatenate([cached_v, new_kv[1, 1]], axis=0)
        attended = attend(
            forward_slice.reshape(seg_len, local_heads, head_size),
            forward_key_list,
            forward_value_list,
            segment_index[0, stretch, 0],
            cache_len,
        )[2]
        grad_query, grad_key, grad_value = attend_back(
            backward_slice.reshape(seg_len, local_heads, head_size),
            backward_key_list,
            backward_value_list,
            segment_index[0, stretch, 1],
            cache_len,
            grad_slice.reshape(seg_len, local_heads, head_size),
        )
        run_sums = jnp.stack([grad_key, grad_value])
        other_run = swapped_pairs(run_sums, "ctx")
        head_grads = (run_sums.astype(jnp.float32) + other_run.astype(jnp.float32)).astype(
            jnp.bfloat16
        )
        half_rows = seg_len // 2
        my_half = lax.dynamic_slice_in_dim(head_grads, (rank_id % 2) * half_rows, half_rows, 1)
        every_half = lax.all_gather(my_half, "ctx", axis=0, tiled=False)
        every_half = every_half.reshape(kv_count, 2, 2, half_rows, head_size)
        key_rows_heads = key_rows.reshape(local_width, kv_count, head_size)
        value_rows_heads = value_rows.reshape(local_width, kv_count, head_size)
        back_rows = jnp.einsum(
            "jhtd,fjd->htf", every_half[:, :, 0], key_rows_heads, preferred_element_type=jnp.float32
        )
        back_rows = back_rows + jnp.einsum(
            "jhtd,fjd->htf",
            every_half[:, :, 1],
            value_rows_heads,
            preferred_element_type=jnp.float32,
        )
        grad_acts = (
            grad_query.reshape(seg_len, -1).astype(jnp.float32) + back_rows.reshape(seg_len, -1)
        ).astype(jnp.bfloat16)
        returned = lax.all_to_all(
            jnp.stack([attended.reshape(ctx_size, local_rows, -1), grad_acts.reshape(ctx_size, local_rows, -1)]),
            "ctx",
            split_axis=1,
            concat_axis=3,
            tiled=True,
        )
        attn_rows = returned[0].reshape(local_rows, model_width)
        section_out = (forward_rows.astype(jnp.float32) + attn_rows.astype(jnp.float32)).astype(
            jnp.bfloat16
        )
        section_grad = input_grad(
            backward_rows, gain_row, returned[1].reshape(local_rows, model_width), grad_rows
        )
        forward_outs.append(passed_along(section_out, "pipe", 1))
        backward_outs.append(passed_along(section_grad, "pipe", -1))
    pipe_rank = lax.axis_index("pipe")
    arrived = jnp.stack(forward_outs)
    next_forward = jnp.where(pipe_rank == 0, jnp.roll(arrived, 1, axis=0), arrived)
    came_back = jnp.stack(backward_outs)
    next_backward = jnp.where(
        pipe_rank == lax.axis_size("pipe") - 1, jnp.roll(came_back, -1, axis=0), came_back
    )
    return (next_forward[None], next_backward[None])


def solution(mesh):
    in_specs = (
        P("pipe", None, "ctx", None),
        P("pipe", None, "ctx", None),
        P("pipe", None, "ctx", None),
        P("pipe", None, "ctx", None, None),
        P("pipe", None, "ctx", None, None),
        P("pipe", None, None),
        P("pipe", None, "ctx", None),
        P("pipe", None, "ctx", None),
        P("pipe", None, None),
    )
    out_specs = (P("pipe", None, "ctx", None), P("pipe", None, "ctx", None))
    return jax.shard_map(
        on_device, mesh=mesh, in_specs=in_specs, out_specs=out_specs, check_vma=False
    )
```

profile of v0, /device:TPU:1, one launch (start us, length us, event | category | flops | bytes accessed | tf_op | source)
XLA Modules:
  0.0 425.7 jit_solution(8083838282504881984)
XLA Ops:
  7.2 1.7 fusion.126
  8.9 2.3 slice_convert_fusion.4
  15.5 2.0 copy.267
  17.5 9.1 %all-to-all-start.1 = ((bf16[3,32,16,512]{3,1,0,2:T(8,128)(2,1)}), bf16[3,32,16,512]{3,1,0,2:T(8,128)(2,1)S(1)}, u32[]{:S(2)}, u32[]{:S(2)}) async-start(bf16[3,32,16,512]{3,1,0,2:T(8,128)(2,1)} %copy.267), calls=%async_computation.1 | async-start | bytes 3145728 | tf_op jit(solution)/shard_map/all_to_all | solution.py:184
  26.8 1.8 copy.383
  28.7 3.2 copy.382
  38.9 2.5 copy.264
  41.4 2.5 slice_bitcast_fusion.15
  43.9 1.8 reshape_squeeze.44
  45.7 1.7 copy.304
  47.4 2.6 reshape.645
  50.0 3.9 slice_bitcast_fusion.14
  54.0 1.8 reshape_squeeze.45
  55.8 1.7 copy.305
  57.5 2.7 reshape.647
  63.4 2.6 copy.392
  67.4 1.8 reshape_squeeze.19
  69.2 1.7 copy.271
  70.8 2.6 reshape.629
  73.4 1.8 reshape_squeeze.20
  75.2 1.7 copy.272
  76.9 2.8 reshape.631
  79.8 2.5 copy.389
  84.6 7.2 %all-to-all-start = ((bf16[4,32,16,512]{3,1,0,2:T(8,128)(2,1)}), bf16[4,32,16,512]{3,1,0,2:T(8,128)(2,1)S(1)}, u32[]{:S(2)}, u32[]{:S(2)}) async-start(bf16[4,32,16,512]{3,1,0,2:T(8,128)(2,1)} %copy.264), calls=%async_computation | async-start | bytes 4194304 | tf_op jit(solution)/shard_map/all_to_all | solution.py:184
  91.9 1.7 copy.487
  99.6 2.0 copy-done
  101.6 1.6 constant_dynamic-slice_fusion.1
  103.3 17.0 %all-to-all-done = bf16[4,32,16,512]{3,1,0,2:T(8,128)(2,1)S(1)} async-done(((bf16[4,32,16,512]{3,1,0,2:T(8,128)(2,1)}), bf16[4,32,16,512]{3,1,0,2:T(8,128)(2,1)S(1)}, u32[]{:S(2)}, u32[]{:S(2)}) %all-to-all-start) | async-done | bytes 2097184 | tf_op jit(solution)/shard_map/all_to_all | solution.py:184
  127.3 2.0 copy-done.1
  131.8 3.0 fusion.41
  143.3 3.1 convert_add_fusion.1
  148.6 2.5 convert_add_fusion
  151.8 1.8 collective-permute-start.11
  155.3 7.0 %collective-permute-done.1 = bf16[4,128,512]{2,1,0:T(8,128)(2,1)S(1)} collective-permute-done((bf16[4,128,512]{2,1,0:T(8,128)(2,1)S(1)}, bf16[4,128,512]{2,1,0:T(8,128)(2,1)S(1)}, u32[]{:S(2)}, u32[]{:S(2)}) %collective-permute-start.1) | collective-permute-done | bytes 524320 | tf_op jit(solution)/shard_map/ppermute | solution.py:21
  164.4 17.4 %collective-permute-done.2 = bf16[4,128,256]{2,1,0:T(8,128)(2,1)S(1)} collective-permute-done((bf16[4,128,256]{2,1,0:T(8,128)(2,1)S(1)}, bf16[4,128,256]{2,1,0:T(8,128)(2,1)S(1)}, u32[]{:S(2)}, u32[]{:S(2)}) %collective-permute-start.2) | collective-permute-done | bytes 262176 | tf_op jit(solution)/shard_map/ppermute | solution.py:21
  182.4 3.4 collective-permute-done.3
  185.8 1.7 collective-permute-done.6
  187.6 2.7 collective-permute-start.7
  191.3 2.1 collective-permute-start.12
  196.8 7.8 %fusion.279 = (f32[4,512]{1,0:T(4,128)S(1)}, f32[4,512,1024]{1,2,0:T(8,128)}) fusion(pred[512,1024]{0,1:T(8,128)(4,1)} %get-tuple-element.74, bf16[512,4,128]{2,1,0:T(4,128)(2,1)} %reshape_reshape_squeeze.33, bf16[512,128]{1,0:T(8,128)(2,1)} %bitcast.662, bf16[512,128]{1,0:T(8,128)(2,1)} %get-tuple-element.60), kind=kOutput, calls=%fused_computation.365 | convolution fusion | flops 545784832 | bytes 9707520 | tf_op jit(solution)/shard_map/sub | solution.py:80
  204.6 4.8 %fusion.28 = bf16[4,512,1024]{1,2,0:T(8,128)(2,1)S(1)} fusion(f32[4,512,1024]{1,2,0:T(8,128)} %get-tuple-element.80, f32[4,512]{1,0:T(4,128)S(1)} %get-tuple-element.79), kind=kLoop, calls=%fused_computation.46 | loop fusion | flops 4194304 | bytes 12591104 | tf_op jit(solution)/shard_map/convert_element_type | solution.py:86
  210.5 2.3 fusion.9
  218.6 1.8 collective-permute-start.16
  221.3 4.4 %collective-permute-done.16 = bf16[4,128,128]{2,1,0:T(8,128)(2,1)S(1)} collective-permute-done((bf16[4,128,128]{2,1,0:T(8,128)(2,1)S(1)}, bf16[4,128,128]{2,1,0:T(8,128)(2,1)S(1)}, u32[]{:S(2)}, u32[]{:S(2)}) %collective-permute-start.16) | collective-permute-done | bytes 131104 | tf_op jit(solution)/shard_map/ppermute | solution.py:21
  228.2 6.5 %fusion.297 = (f32[4,512]{1,0:T(4,128)S(1)}, f32[4,512,1024]{1,2,0:T(8,128)}) fusion(pred[512,1024]{0,1:T(8,128)(4,1)S(1)} %copy-done.50, bf16[512,4,128]{2,1,0:T(4,128)(2,1)S(1)} %copy-done.43, bf16[512,128]{1,0:T(8,128)(2,1)S(1)} %bitcast.656, bf16[512,128]{1,0:T(8,128)(2,1)S(1)} %get-tuple-element.64), kind=kOutput, calls=%fused_computation.367 | convolution fusion | flops 545784832 | bytes 9707520 | tf_op jit(solution)/shard_map/sub | solution.py:80
  234.7 4.8 %fusion.29 = bf16[4,512,1024]{1,2,0:T(8,128)(2,1)S(1)} fusion(f32[4,512,1024]{1,2,0:T(8,128)} %get-tuple-element.84, f32[4,512]{1,0:T(4,128)S(1)} %get-tuple-element.83), kind=kLoop, calls=%fused_computation.47 | loop fusion | flops 4194304 | bytes 12591104 | tf_op jit(solution)/shard_map/convert_element_type | solution.py:86
  241.0 2.3 fusion.6
  243.4 1.9 copy-done.19
  246.8 6.5 %fusion.288 = (f32[4,512]{1,0:T(4,128)S(1)}, f32[4,512,1024]{1,2,0:T(8,128)}) fusion(pred[512,1024]{0,1:T(8,128)(4,1)S(1)} %copy-done.49, bf16[512,4,128]{2,1,0:T(4,128)(2,1)S(1)} %copy-done.42, bf16[512,128]{1,0:T(8,128)(2,1)S(1)} %bitcast.663, bf16[512,128]{1,0:T(8,128)(2,1)S(1)} %get-tuple-element.58), kind=kOutput, calls=%fused_computation.366 | convolution fusion | flops 545784832 | bytes 9707520 | tf_op jit(solution)/shard_map/sub | solution.py:80
  254.0 4.2 fusion.66
  259.5 3.0 fusion.58
  263.3 7.5 %fusion.306 = (f32[4,512]{1,0:T(4,128)S(1)}, f32[4,512,1024]{1,2,0:T(8,128)}) fusion(pred[512,1024]{0,1:T(8,128)(4,1)} %get-tuple-element.73, bf16[512,4,128]{2,1,0:T(4,128)(2,1)S(1)} %copy-done.41, bf16[512,128]{1,0:T(8,128)(2,1)S(1)} %bitcast.657, bf16[512,128]{1,0:T(8,128)(2,1)S(1)} %get-tuple-element.62), kind=kOutput, calls=%fused_computation.368 | convolution fusion | flops 545784832 | bytes 9707520 | tf_op jit(solution)/shard_map/sub | solution.py:80
  270.9 4.2 fusion.67
  276.4 3.0 fusion.63
  280.8 1.8 fusion.272
  285.9 4.4 %all-to-all-start.2 = ((bf16[2,16,32,512]{3,2,0,1:T(8,128)(2,1)}), bf16[2,16,32,512]{3,2,0,1:T(8,128)(2,1)S(1)}, u32[]{:S(2)}, u32[]{:S(2)}) async-start(bf16[2,16,32,512]{3,2,0,1:T(8,128)(2,1)} %copy.299), calls=%async_computation.2 | async-start | bytes 2097152 | tf_op jit(solution)/shard_map/all_to_all | solution.py:259
  290.2 49.1 %all-gather.7.cloned.1.call-done = bf16[32,256,128]{2,1,0:T(8,128)(2,1)} async-done(((bf16[2,256,128]{2,1,0:T(8,128)(2,1)}), bf16[32,256,128]{2,1,0:T(8,128)(2,1)}) %all-gather.7.cloned.1.call-update) | async-done | bytes 2097168 | tf_op jit(solution)/shard_map/all_gather | solution.py:243
  339.4 1.8 fusion.273
  344.2 4.3 %all-to-all-start.3 = ((bf16[2,16,32,512]{3,2,0,1:T(8,128)(2,1)}), bf16[2,16,32,512]{3,2,0,1:T(8,128)(2,1)}, u32[]{:S(2)}, u32[]{:S(2)}) async-start(bf16[2,16,32,512]{3,2,0,1:T(8,128)(2,1)} %copy.332), calls=%async_computation.3 | async-start | bytes 2097152 | tf_op jit(solution)/shard_map/all_to_all | solution.py:259
  353.1 12.8 %all-to-all-done.3 = bf16[2,16,32,512]{3,2,0,1:T(8,128)(2,1)} async-done(((bf16[2,16,32,512]{3,2,0,1:T(8,128)(2,1)}), bf16[2,16,32,512]{3,2,0,1:T(8,128)(2,1)}, u32[]{:S(2)}, u32[]{:S(2)}) %all-to-all-start.3) | async-done | bytes 1048608 | tf_op jit(solution)/shard_map/all_to_all | solution.py:259
  365.9 1.9 copy.488
  369.9 3.6 collective-permute-start.20
  375.9 29.0 %collective-permute-done.20 = bf16[32,8192]{1,0:T(8,128)(2,1)S(1)} collective-permute-done((bf16[32,8192]{1,0:T(8,128)(2,1)S(1)}, bf16[32,8192]{1,0:T(8,128)(2,1)S(1)}, u32[]{:S(2)}, u32[]{:S(2)}) %collective-permute-start.20) | collective-permute-done | bytes 524320 | tf_op jit(solution)/shard_map/ppermute | solution.py:11
  404.9 11.2 %collective-permute-done.21 = bf16[32,8192]{1,0:T(8,128)(2,1)S(1)} collective-permute-done((bf16[32,8192]{1,0:T(8,128)(2,1)S(1)}, bf16[32,8192]{1,0:T(8,128)(2,1)S(1)}, u32[]{:S(2)}, u32[]{:S(2)}) %collective-permute-start.21) | collective-permute-done | bytes 524320 | tf_op jit(solution)/shard_map/ppermute | solution.py:11
  (319 shorter events, 86.8 us)
Async XLA Ops:
  7.2 4.0 copy-start.4
  7.2 5.5 %copy-start.58 = (f32[1,2,8192]{2,1,0:T(2,128)S(1)}, f32[1,2,8192]{2,1,0:T(2,128)}, u32[]{:S(2)}) copy-start(f32[1,2,8192]{2,1,0:T(2,128)} %param.14) | copy-start | bytes 196612
  7.2 6.1 %copy-start.11 = (bf16[1,2,32,8192]{3,2,1,0:T(8,128)(2,1)S(1)}, bf16[1,2,32,8192]{3,2,1,0:T(8,128)(2,1)}, u32[]{:S(2)}) copy-start(bf16[1,2,32,8192]{3,2,1,0:T(8,128)(2,1)} %param.11) | copy-start | bytes 3145732
  14.8 22.3 %copy-start.61 = (f32[32]{0:T(128)}, f32[32]{0:T(128)S(1)}, u32[]{:S(2)}) copy-start(f32[32]{0:T(128)S(1)} %get-tuple-element.94) | copy-start | bytes 388
  17.5 15.3 %copy-start.57 = (bf16[1,2,32,8,128]{4,3,2,1,0:T(8,128)(2,1)S(1)}, bf16[1,2,32,8,128]{4,3,2,1,0:T(8,128)(2,1)}, u32[]{:S(2)}) copy-start(bf16[1,2,32,8,128]{4,3,2,1,0:T(8,128)(2,1)} %param.12) | copy-start | bytes 393220
  17.5 66.0 %all-to-all-start.1 = ((bf16[3,32,16,512]{3,1,0,2:T(8,128)(2,1)}), bf16[3,32,16,512]{3,1,0,2:T(8,128)(2,1)S(1)}, u32[]{:S(2)}, u32[]{:S(2)}) async-start(bf16[3,32,16,512]{3,1,0,2:T(8,128)(2,1)} %copy.267), calls=%async_computation.1 | async-start | bytes 3145728 | tf_op jit(solution)/shard_map/all_to_all | solution.py:184
  26.8 10.3 %copy-start.53 = (f32[16,512]{1,0:T(8,128)}, f32[16,512]{1,0:T(8,128)S(1)}, u32[]{:S(2)}) copy-start(f32[16,512]{1,0:T(8,128)S(1)} %mul.365) | copy-start | bytes 98308
  28.6 10.0 %copy-start.8 = (f32[4,8,16,512]{3,2,1,0:T(8,128)}, f32[4,8,16,512]{3,2,1,0:T(8,128)S(1)}, u32[]{:S(2)}) copy-start(f32[4,8,16,512]{3,2,1,0:T(8,128)S(1)} %copy.383) | copy-start | bytes 3145732
  32.8 5.8 %copy-start.32 = (bf16[4,8,16,512]{3,2,1,0:T(8,128)(2,1)S(1)}, bf16[4,8,16,512]{3,2,1,0:T(8,128)(2,1)}, u32[]{:S(2)}) copy-start(bf16[4,8,16,512]{3,2,1,0:T(8,128)(2,1)} %copy.384) | copy-start | bytes 1572868
  54.0 6.2 %copy-start.63 = (s32[1,2,2]{2,1,0:T(2,128)S(1)}, s32[1,2,2]{2,1,0:T(2,128)}, u32[]{:S(2)}) copy-start(s32[1,2,2]{2,1,0:T(2,128)} %param.17) | copy-start | bytes 52
  57.5 8.5 %copy-start.22 = (bf16[64,8,8,128]{3,1,2,0:T(8,128)(2,1)S(1)}, bf16[64,8,8,128]{3,1,2,0:T(8,128)(2,1)}, u32[]{:S(2)}) copy-start(bf16[64,8,8,128]{3,1,2,0:T(8,128)(2,1)} %get-tuple-element.15) | copy-start | bytes 3145732
  76.9 5.3 %copy-start.20 = (bf16[64,8,8,128]{3,1,2,0:T(8,128)(2,1)S(1)}, bf16[64,8,8,128]{3,1,2,0:T(8,128)(2,1)}, u32[]{:S(2)}) copy-start(bf16[64,8,8,128]{3,1,2,0:T(8,128)(2,1)} %get-tuple-element.14) | copy-start | bytes 3145732
  84.6 35.7 %all-to-all-start = ((bf16[4,32,16,512]{3,1,0,2:T(8,128)(2,1)}), bf16[4,32,16,512]{3,1,0,2:T(8,128)(2,1)S(1)}, u32[]{:S(2)}, u32[]{:S(2)}) async-start(bf16[4,32,16,512]{3,1,0,2:T(8,128)(2,1)} %copy.264), calls=%async_computation | async-start | bytes 4194304 | tf_op jit(solution)/shard_map/all_to_all | solution.py:184
  91.9 188.9 %all-gather.5.cloned.1.call-start = ((), (), s32[]{:S(2)}) async-start(), calls=%async_computation.4 | async-start | bytes 2228224 | tf_op jit(solution)/shard_map/all_gather | solution.py:243
  103.2 40.1 %collective-permute-start = (bf16[4,256,1024]{2,1,0:T(8,128)(2,1)}, bf16[4,256,1024]{2,1,0:T(8,128)(2,1)}, u32[]{:S(2)}, u32[]{:S(2)}) collective-permute-start(bf16[4,256,1024]{2,1,0:T(8,128)(2,1)} %constant_dynamic-slice_fusion.1), channel_id=1, source_target_pairs={{0,1},{1,0},{2,3},{3,2},{4,5},{5,4},{6,7},{7,6},{8,9},{9,8},{10,11... | collective-permute-start | bytes 6291464 | tf_op jit(solution)/shard_map/ppermute | solution.py:21
  129.3 7.3 %copy-start.28 = (bf16[1,16,32,1,512]{4,2,1,3,0:T(8,128)(2,1)S(1)}, bf16[1,16,32,1,512]{4,2,1,3,0:T(8,128)(2,1)}, u32[]{:S(2)}) copy-start(bf16[1,16,32,1,512]{4,2,1,3,0:T(8,128)(2,1)} %get-tuple-element.30) | copy-start | bytes 1572868
  130.8 17.6 %collective-permute-start.10 = (bf16[4,256,1024]{2,1,0:T(8,128)(2,1)}, bf16[4,256,1024]{2,1,0:T(8,128)(2,1)}, u32[]{:S(2)}, u32[]{:S(2)}) collective-permute-start(bf16[4,256,1024]{2,1,0:T(8,128)(2,1)} %constant_dynamic-slice_fusion), channel_id=1, source_target_pairs={{0,1},{1,0},{2,3},{3,2},{4,5},{5,4},{6,7},{7,6},{8,9},{9,8},{10,11... | collective-permute-start | bytes 6291464 | tf_op jit(solution)/shard_map/ppermute | solution.py:21
  136.6 4.9 %copy-start.31 = (bf16[1,16,32,1,512]{4,2,1,3,0:T(8,128)(2,1)S(1)}, bf16[1,16,32,1,512]{4,2,1,3,0:T(8,128)(2,1)}, u32[]{:S(2)}) copy-start(bf16[1,16,32,1,512]{4,2,1,3,0:T(8,128)(2,1)} %get-tuple-element.26) | copy-start | bytes 1572868
  147.1 15.1 %collective-permute-start.1 = (bf16[4,128,512]{2,1,0:T(8,128)(2,1)S(1)}, bf16[4,128,512]{2,1,0:T(8,128)(2,1)S(1)}, u32[]{:S(2)}, u32[]{:S(2)}) collective-permute-start(bf16[4,128,512]{2,1,0:T(8,128)(2,1)S(1)} %dynamic-slice_convert_fusion.3), channel_id=1, source_target_pairs={{0,8},{1,9},{2,10},{3,11},{4,12},{5,13},{6,14},{7,15},{8,0},{9,1},... | collective-permute-start | bytes 1572872 | tf_op jit(solution)/shard_map/ppermute | solution.py:21
  148.2 14.4 %collective-permute-start.4 = (bf16[4,128,512]{2,1,0:T(8,128)(2,1)S(1)}, bf16[4,128,512]{2,1,0:T(8,128)(2,1)S(1)}, u32[]{:S(2)}, u32[]{:S(2)}) collective-permute-start(bf16[4,128,512]{2,1,0:T(8,128)(2,1)S(1)} %dynamic-slice_convert_fusion.2), channel_id=1, source_target_pairs={{0,2},{1,3},{2,0},{3,1},{4,6},{5,7},{6,4},{7,5},{8,10},{9,11},{10,... | collective-permute-start | bytes 1572872 | tf_op jit(solution)/shard_map/ppermute | solution.py:21
  151.8 38.5 %collective-permute-start.11 = (bf16[4,128,512]{2,1,0:T(8,128)(2,1)S(1)}, bf16[4,128,512]{2,1,0:T(8,128)(2,1)S(1)}, u32[]{:S(2)}, u32[]{:S(2)}) collective-permute-start(bf16[4,128,512]{2,1,0:T(8,128)(2,1)S(1)} %dynamic-slice_convert_fusion.1), channel_id=1, source_target_pairs={{0,8},{1,9},{2,10},{3,11},{4,12},{5,13},{6,14},{7,15},{8,0},{9,1},... | collective-permute-start | bytes 1572872 | tf_op jit(solution)/shard_map/ppermute | solution.py:21
  153.7 39.6 %collective-permute-start.14 = (bf16[4,128,512]{2,1,0:T(8,128)(2,1)S(1)}, bf16[4,128,512]{2,1,0:T(8,128)(2,1)S(1)}, u32[]{:S(2)}, u32[]{:S(2)}) collective-permute-start(bf16[4,128,512]{2,1,0:T(8,128)(2,1)S(1)} %dynamic-slice_convert_fusion), channel_id=1, source_target_pairs={{0,2},{1,3},{2,0},{3,1},{4,6},{5,7},{6,4},{7,5},{8,10},{9,11},{10,... | collective-permute-start | bytes 1572872 | tf_op jit(solution)/shard_map/ppermute | solution.py:21
  162.5 19.2 %collective-permute-start.2 = (bf16[4,128,256]{2,1,0:T(8,128)(2,1)S(1)}, bf16[4,128,256]{2,1,0:T(8,128)(2,1)S(1)}, u32[]{:S(2)}, u32[]{:S(2)}) collective-permute-start(bf16[4,128,256]{2,1,0:T(8,128)(2,1)S(1)} %dynamic-slice_convert_fusion.7), channel_id=1, source_target_pairs={{0,4},{1,5},{2,6},{3,7},{4,0},{5,1},{6,2},{7,3},{8,12},{9,13},{10,... | collective-permute-start | bytes 786440 | tf_op jit(solution)/shard_map/ppermute | solution.py:21
  162.9 19.1 %collective-permute-start.5 = (bf16[4,128,256]{2,1,0:T(8,128)(2,1)S(1)}, bf16[4,128,256]{2,1,0:T(8,128)(2,1)S(1)}, u32[]{:S(2)}, u32[]{:S(2)}) collective-permute-start(bf16[4,128,256]{2,1,0:T(8,128)(2,1)S(1)} %dynamic-slice_convert_fusion.6), channel_id=1, source_target_pairs={{0,8},{1,9},{2,10},{3,11},{4,12},{5,13},{6,14},{7,15},{8,0},{9,1},... | collective-permute-start | bytes 786440 | tf_op jit(solution)/shard_map/ppermute | solution.py:21
  181.9 3.9 collective-permute-start.3
  182.1 5.4 %collective-permute-start.6 = (bf16[4,128,128]{2,1,0:T(8,128)(2,1)S(1)}, bf16[4,128,128]{2,1,0:T(8,128)(2,1)S(1)}, u32[]{:S(2)}, u32[]{:S(2)}) collective-permute-start(bf16[4,128,128]{2,1,0:T(8,128)(2,1)S(1)} %dynamic-slice_convert_fusion.10), channel_id=1, source_target_pairs={{0,4},{1,5},{2,6},{3,7},{4,0},{5,1},{6,2},{7,3},{8,12},{9,13},{10,... | collective-permute-start | bytes 393224 | tf_op jit(solution)/shard_map/ppermute | solution.py:21
  187.6 8.2 %collective-permute-start.7 = (bf16[4,256,128]{2,1,0:T(8,128)(2,1)S(1)}, bf16[4,256,128]{2,1,0:T(8,128)(2,1)S(1)}, u32[]{:S(2)}, u32[]{:S(2)}) collective-permute-start(bf16[4,256,128]{2,1,0:T(8,128)(2,1)S(1)} %pad_maximum_fusion.22), channel_id=1, source_target_pairs={{0,1},{1,0},{2,3},{3,2},{4,5},{5,4},{6,7},{7,6},{8,9},{9,8},{10,11... | collective-permute-start | bytes 786440 | tf_op jit(solution)/shard_map/ppermute | solution.py:21
  191.3 23.8 %collective-permute-start.12 = (bf16[4,128,256]{2,1,0:T(8,128)(2,1)}, bf16[4,128,256]{2,1,0:T(8,128)(2,1)}, u32[]{:S(2)}, u32[]{:S(2)}) collective-permute-start(bf16[4,128,256]{2,1,0:T(8,128)(2,1)} %dynamic-slice_convert_fusion.5), channel_id=1, source_target_pairs={{0,4},{1,5},{2,6},{3,7},{4,0},{5,1},{6,2},{7,3},{8,12},{9,13},{10,... | collective-permute-start | bytes 786440 | tf_op jit(solution)/shard_map/ppermute | solution.py:21
  194.3 23.3 %collective-permute-start.15 = (bf16[4,128,256]{2,1,0:T(8,128)(2,1)}, bf16[4,128,256]{2,1,0:T(8,128)(2,1)}, u32[]{:S(2)}, u32[]{:S(2)}) collective-permute-start(bf16[4,128,256]{2,1,0:T(8,128)(2,1)} %dynamic-slice_convert_fusion.4), channel_id=1, source_target_pairs={{0,8},{1,9},{2,10},{3,11},{4,12},{5,13},{6,14},{7,15},{8,0},{9,1},... | collective-permute-start | bytes 786440 | tf_op jit(solution)/shard_map/ppermute | solution.py:21
  204.6 5.6 %slice-start.2 = ((s8[8388608]{0:T(1024)(128)(4,1)}), s8[4194304]{0:T(1024)(128)(4,1)S(1)}, s32[]{:S(2)}) async-start(s8[8388608]{0:T(1024)(128)(4,1)} %bitcast.592), calls=%async_computation.8 | async-start | bytes 8388608
  204.6 4.8 %copy-start.39 = (bf16[512,1,1,128]{3,0,2,1:T(8,128)(2,1)S(1)}, bf16[512,1,1,128]{3,0,2,1:T(8,128)(2,1)}, u32[]{:S(2)}) copy-start(bf16[512,1,1,128]{3,0,2,1:T(8,128)(2,1)} %copy.493) | copy-start | bytes 393220
  204.6 4.8 %copy-start.48 = (bf16[512,128]{1,0:T(8,128)(2,1)S(1)}, bf16[512,128]{1,0:T(8,128)(2,1)}, u32[]{:S(2)}) copy-start(bf16[512,128]{1,0:T(8,128)(2,1)} %get-tuple-element.59) | copy-start | bytes 393220
  204.6 6.0 %slice-start.3 = ((s8[8388608]{0:T(1024)(128)(4,1)}), s8[4194304]{0:T(1024)(128)(4,1)S(1)}, s32[]{:S(2)}) async-start(s8[8388608]{0:T(1024)(128)(4,1)} %bitcast.592), calls=%async_computation.9 | async-start | bytes 8388608
  214.3 12.4 %collective-permute-start.8 = (bf16[2,512,128]{2,1,0:T(8,128)(2,1)S(1)}, bf16[2,512,128]{2,1,0:T(8,128)(2,1)S(1)}, u32[]{:S(2)}, u32[]{:S(2)}) collective-permute-start(bf16[2,512,128]{2,1,0:T(8,128)(2,1)S(1)} %pad_maximum_fusion.16), channel_id=1, source_target_pairs={{0,1},{1,0},{2,3},{3,2},{4,5},{5,4},{6,7},{7,6},{8,9},{9,8},{10,11... | collective-permute-start | bytes 786440 | tf_op jit(solution)/shard_map/ppermute | solution.py:16
  216.1 5.2 %collective-permute-start.13 = (bf16[4,128,128]{2,1,0:T(8,128)(2,1)S(1)}, bf16[4,128,128]{2,1,0:T(8,128)(2,1)S(1)}, u32[]{:S(2)}, u32[]{:S(2)}) collective-permute-start(bf16[4,128,128]{2,1,0:T(8,128)(2,1)S(1)} %dynamic-slice_convert_fusion.9), channel_id=1, source_target_pairs={{0,2},{1,3},{2,0},{3,1},{4,6},{5,7},{6,4},{7,5},{8,10},{9,11},{10,... | collective-permute-start | bytes 393224 | tf_op jit(solution)/shard_map/ppermute | solution.py:21
  218.6 9.6 %copy-start.43 = (bf16[512,4,128]{2,1,0:T(4,128)(2,1)S(1)}, bf16[512,4,128]{2,1,0:T(4,128)(2,1)}, u32[]{:S(2)}) copy-start(bf16[512,4,128]{2,1,0:T(4,128)(2,1)} %reshape_reshape_squeeze.38) | copy-start | bytes 1572868
  218.6 9.6 %copy-start.50 = (pred[512,1024]{0,1:T(8,128)(4,1)S(1)}, pred[512,1024]{0,1:T(8,128)(4,1)}, u32[]{:S(2)}) copy-start(pred[512,1024]{0,1:T(8,128)(4,1)} %get-tuple-element.72) | copy-start | bytes 1572868
  218.6 7.1 %collective-permute-start.16 = (bf16[4,128,128]{2,1,0:T(8,128)(2,1)S(1)}, bf16[4,128,128]{2,1,0:T(8,128)(2,1)S(1)}, u32[]{:S(2)}, u32[]{:S(2)}) collective-permute-start(bf16[4,128,128]{2,1,0:T(8,128)(2,1)S(1)} %dynamic-slice_convert_fusion.8), channel_id=1, source_target_pairs={{0,4},{1,5},{2,6},{3,7},{4,0},{5,1},{6,2},{7,3},{8,12},{9,13},{10,... | collective-permute-start | bytes 393224 | tf_op jit(solution)/shard_map/ppermute | solution.py:21
  225.8 2.1 collective-permute-start.17
  227.5 111.9 %all-gather.7.cloned.1.call-start = ((), (), s32[]{:S(2)}) async-start(), calls=%async_computation.5 | async-start | bytes 2228224 | tf_op jit(solution)/shard_map/all_gather | solution.py:243
  228.2 6.5 %copy-start.46 = (bf16[512,128]{1,0:T(8,128)(2,1)}, bf16[512,128]{1,0:T(8,128)(2,1)S(1)}, u32[]{:S(2)}) copy-start(bf16[512,128]{1,0:T(8,128)(2,1)S(1)} %get-tuple-element.64) | copy-start | bytes 393220
  234.7 6.3 %slice-start = ((s8[8388608]{0:T(1024)(128)(4,1)}), s8[4194304]{0:T(1024)(128)(4,1)S(1)}, s32[]{:S(2)}) async-start(s8[8388608]{0:T(1024)(128)(4,1)} %bitcast.590), calls=%async_computation.6 | async-start | bytes 8388608
  234.7 5.6 %copy-start.37 = (bf16[512,1,1,128]{3,0,2,1:T(8,128)(2,1)S(1)}, bf16[512,1,1,128]{3,0,2,1:T(8,128)(2,1)}, u32[]{:S(2)}) copy-start(bf16[512,1,1,128]{3,0,2,1:T(8,128)(2,1)} %copy.491) | copy-start | bytes 393220
  234.7 6.3 %slice-start.1 = ((s8[8388608]{0:T(1024)(128)(4,1)}), s8[4194304]{0:T(1024)(128)(4,1)S(1)}, s32[]{:S(2)}) async-start(s8[8388608]{0:T(1024)(128)(4,1)} %bitcast.590), calls=%async_computation.7 | async-start | bytes 8388608
  246.1 7.2 %collective-permute-start.18 = (bf16[2,512,128]{2,1,0:T(8,128)(2,1)S(1)}, bf16[2,512,128]{2,1,0:T(8,128)(2,1)S(1)}, u32[]{:S(2)}, u32[]{:S(2)}) collective-permute-start(bf16[2,512,128]{2,1,0:T(8,128)(2,1)S(1)} %pad_maximum_fusion.21), channel_id=1, source_target_pairs={{0,1},{1,0},{2,3},{3,2},{4,5},{5,4},{6,7},{7,6},{8,9},{9,8},{10,11... | collective-permute-start | bytes 786440 | tf_op jit(solution)/shard_map/ppermute | solution.py:16
  246.8 7.2 %copy-start.40 = (bf16[512,1,1,128]{3,0,2,1:T(8,128)(2,1)S(1)}, bf16[512,1,1,128]{3,0,2,1:T(8,128)(2,1)}, u32[]{:S(2)}) copy-start(bf16[512,1,1,128]{3,0,2,1:T(8,128)(2,1)} %copy.493) | copy-start | bytes 393220
  254.0 5.5 %copy-start.45 = (bf16[512,128]{1,0:T(8,128)(2,1)S(1)}, bf16[512,128]{1,0:T(8,128)(2,1)}, u32[]{:S(2)}) copy-start(bf16[512,128]{1,0:T(8,128)(2,1)} %get-tuple-element.60) | copy-start | bytes 393220
  270.9 5.5 %copy-start.47 = (bf16[512,128]{1,0:T(8,128)(2,1)S(1)}, bf16[512,128]{1,0:T(8,128)(2,1)}, u32[]{:S(2)}) copy-start(bf16[512,128]{1,0:T(8,128)(2,1)} %copy-done.46) | copy-start | bytes 393220
  285.9 58.3 %all-to-all-start.2 = ((bf16[2,16,32,512]{3,2,0,1:T(8,128)(2,1)}), bf16[2,16,32,512]{3,2,0,1:T(8,128)(2,1)S(1)}, u32[]{:S(2)}, u32[]{:S(2)}) async-start(bf16[2,16,32,512]{3,2,0,1:T(8,128)(2,1)} %copy.299), calls=%async_computation.2 | async-start | bytes 2097152 | tf_op jit(solution)/shard_map/all_to_all | solution.py:259
  290.2 51.8 %copy-start.33 = (bf16[64,8,8,128]{3,2,1,0:T(8,128)(2,1)S(1)}, bf16[64,8,8,128]{3,2,1,0:T(8,128)(2,1)}, u32[]{:S(2)}) copy-start(bf16[64,8,8,128]{3,2,1,0:T(8,128)(2,1)} %copy.391) | copy-start | bytes 3145732
  344.2 21.7 %all-to-all-start.3 = ((bf16[2,16,32,512]{3,2,0,1:T(8,128)(2,1)}), bf16[2,16,32,512]{3,2,0,1:T(8,128)(2,1)}, u32[]{:S(2)}, u32[]{:S(2)}) async-start(bf16[2,16,32,512]{3,2,0,1:T(8,128)(2,1)} %copy.332), calls=%async_computation.3 | async-start | bytes 2097152 | tf_op jit(solution)/shard_map/all_to_all | solution.py:259
  351.0 17.0 %copy-start.9 = (f32[4,8,16,512]{3,2,1,0:T(8,128)S(1)}, f32[4,8,16,512]{3,2,1,0:T(8,128)}, u32[]{:S(2)}) copy-start(f32[4,8,16,512]{3,2,1,0:T(8,128)} %copy-done.8) | copy-start | bytes 3145732
  351.0 17.0 %copy-start.54 = (f32[16,512]{1,0:T(8,128)S(1)}, f32[16,512]{1,0:T(8,128)}, u32[]{:S(2)}) copy-start(f32[16,512]{1,0:T(8,128)} %copy-done.53) | copy-start | bytes 98308
  351.0 17.0 %copy-start.62 = (f32[32]{0:T(128)S(1)}, f32[32]{0:T(128)}, u32[]{:S(2)}) copy-start(f32[32]{0:T(128)} %copy-done.61) | copy-start | bytes 388
  353.1 16.1 %copy-start.3 = (bf16[1,2,32,8192]{3,2,1,0:T(8,128)(2,1)S(1)}, bf16[1,2,32,8192]{3,2,1,0:T(8,128)(2,1)}, u32[]{:S(2)}) copy-start(bf16[1,2,32,8192]{3,2,1,0:T(8,128)(2,1)} %param.10) | copy-start | bytes 3145732
  353.1 16.1 %copy-start.12 = (bf16[1,2,32,8192]{3,2,1,0:T(8,128)(2,1)S(1)}, bf16[1,2,32,8192]{3,2,1,0:T(8,128)(2,1)}, u32[]{:S(2)}) copy-start(bf16[1,2,32,8192]{3,2,1,0:T(8,128)(2,1)} %param.11) | copy-start | bytes 3145732
  353.1 16.1 %copy-start.55 = (f32[1,1,8192]{2,1,0:T(1,128)S(1)}, f32[1,1,8192]{2,1,0:T(1,128)}, u32[]{:S(2)}) copy-start(f32[1,1,8192]{2,1,0:T(1,128)} %get-tuple-element.65) | copy-start | bytes 98308
  353.1 16.1 %copy-start.56 = (f32[1,1,8192]{2,1,0:T(1,128)S(1)}, f32[1,1,8192]{2,1,0:T(1,128)}, u32[]{:S(2)}) copy-start(f32[1,1,8192]{2,1,0:T(1,128)} %get-tuple-element.66) | copy-start | bytes 98308
  369.1 5.6 %copy-start.5 = (bf16[1,2,32,8192]{3,2,1,0:T(8,128)(2,1)S(1)}, bf16[1,2,32,8192]{3,2,1,0:T(8,128)(2,1)}, u32[]{:S(2)}) copy-start(bf16[1,2,32,8192]{3,2,1,0:T(8,128)(2,1)} %param.9) | copy-start | bytes 3145732
  369.1 5.6 %copy-start.21 = (f32[4,8,16,512]{3,1,2,0:T(8,128)S(1)}, f32[4,8,16,512]{3,1,2,0:T(8,128)}, u32[]{:S(2)}) copy-start(f32[4,8,16,512]{3,1,2,0:T(8,128)} %copy.390) | copy-start | bytes 3145732
  369.9 35.1 %collective-permute-start.20 = (bf16[32,8192]{1,0:T(8,128)(2,1)S(1)}, bf16[32,8192]{1,0:T(8,128)(2,1)S(1)}, u32[]{:S(2)}, u32[]{:S(2)}) collective-permute-start(bf16[32,8192]{1,0:T(8,128)(2,1)S(1)} %get-tuple-element.12), channel_id=1, source_target_pairs={{0,240},{16,0},{32,16},{48,32},{64,48},{80,64},{96,80},{112,96},{1... | collective-permute-start | bytes 1572872 | tf_op jit(solution)/shard_map/ppermute | solution.py:11
  373.4 42.7 %collective-permute-start.21 = (bf16[32,8192]{1,0:T(8,128)(2,1)S(1)}, bf16[32,8192]{1,0:T(8,128)(2,1)S(1)}, u32[]{:S(2)}, u32[]{:S(2)}) collective-permute-start(bf16[32,8192]{1,0:T(8,128)(2,1)S(1)} %get-tuple-element.13), channel_id=1, source_target_pairs={{0,240},{16,0},{32,16},{48,32},{64,48},{80,64},{96,80},{112,96},{1... | collective-permute-start | bytes 1572872 | tf_op jit(solution)/shard_map/ppermute | solution.py:11
  375.0 42.3 %collective-permute-start.19 = (bf16[32,8192]{1,0:T(8,128)(2,1)S(1)}, bf16[32,8192]{1,0:T(8,128)(2,1)S(1)}, u32[]{:S(2)}, u32[]{:S(2)}) collective-permute-start(bf16[32,8192]{1,0:T(8,128)(2,1)S(1)} %get-tuple-element.38), channel_id=1, source_target_pairs={{0,16},{16,32},{32,48},{48,64},{64,80},{80,96},{96,112},{112,128},... | collective-permute-start | bytes 1572872 | tf_op jit(solution)/shard_map/ppermute | solution.py:11
  375.8 41.5 %collective-permute-start.9 = (bf16[32,8192]{1,0:T(8,128)(2,1)S(1)}, bf16[32,8192]{1,0:T(8,128)(2,1)S(1)}, u32[]{:S(2)}, u32[]{:S(2)}) collective-permute-start(bf16[32,8192]{1,0:T(8,128)(2,1)S(1)} %get-tuple-element.37), channel_id=1, source_target_pairs={{0,16},{16,32},{32,48},{48,64},{64,80},{80,96},{96,112},{112,128},... | collective-permute-start | bytes 1572872 | tf_op jit(solution)/shard_map/ppermute | solution.py:11
  (32 other events, 69.0 us)
Sparse Core Ops, SparseCore 0:
  227.6 53.1 all-gather.4
  283.5 55.7 all-gather.6
where the time goes:
time: 431 us; the launch traced here: 426 us
  waiting for transfers between devices  155 us (36%)
  local copies, waits for them, and re-layouts  103 us (24%)
  matrix products  60.6 us (14%)
  starting transfers between devices  49.8 us (12%)
  other arithmetic  38.7 us (9%)
  between operations  18.8 us (4%)
    all_gather x2, waiting for transfers between devices, on_device(): every_half = lax.all_gather(my_half, 'ctx', axis=0, tiled=False)  49.6 us
    ppermute x4, waiting for transfers between devices, passed_along(): lax.ppermute(array, axis, [(i, (i + by) % count) for i in range(count)])  40.3 us
    unnamed x156, local copies, waits for them, and re-layouts  38 us
    ppermute x16, waiting for transfers between devices, swapped_with(): return lax.ppermute(array, axis, [(i, i ^ mask) for i in range(count)])  35 us
    sub x4, matrix products, probabilities(): lifted = jnp.exp(scores - row_max)  28.3 us
    ppermute x16, starting transfers between devices, swapped_with(): return lax.ppermute(array, axis, [(i, i ^ mask) for i in range(count)])  18 us
    all_to_all x2, waiting for transfers between devices, on_device(): lax.all_to_all(jnp.stack(outgoing), 'ctx', split_axis=2, concat_axis=1, t...  17 us
    all_to_all x2, starting transfers between devices, on_device(): lax.all_to_all(jnp.stack(outgoing), 'ctx', split_axis=2, concat_axis=1, t...  16.4 us
  transfers between devices with their start and end apart: 28, of which 13 were waited for; matrix products, arithmetic and copies ran while one was open for 42% of the time, Pallas kernels for 0%

commit v1 on v0

--- a/solution.py
+++ b/solution.py
@@ -45,6 +45,29 @@
         core == 0,
         jnp.concatenate([mine, theirs], axis=1),
         jnp.concatenate([theirs, mine], axis=1),
+    )
+
+
+def gather_heads(head_grads, rank_id, ctx_size):
+    core = rank_id % 2
+    rows = head_grads.shape[1]
+    half = rows // 2
+    held = lax.dynamic_slice_in_dim(head_grads, core * half, half, 1)[None]
+    mask = 2
+    while mask < ctx_size:
+        other = swapped_with(held, "ctx", mask)
+        bit = (rank_id // mask) % 2
+        held = jnp.where(
+            bit == 0,
+            jnp.concatenate([held, other], axis=0),
+            jnp.concatenate([other, held], axis=0),
+        )
+        mask *= 2
+    other = swapped_with(held, "ctx", 1)
+    return jnp.where(
+        core == 0,
+        jnp.concatenate([held, other], axis=2),
+        jnp.concatenate([other, held], axis=2),
     )
 
 
@@ -238,18 +261,15 @@
         head_grads = (run_sums.astype(jnp.float32) + other_run.astype(jnp.float32)).astype(
             jnp.bfloat16
         )
-        half_rows = seg_len // 2
-        my_half = lax.dynamic_slice_in_dim(head_grads, (rank_id % 2) * half_rows, half_rows, 1)
-        every_half = lax.all_gather(my_half, "ctx", axis=0, tiled=False)
-        every_half = every_half.reshape(kv_count, 2, 2, half_rows, head_size)
+        every_head = gather_heads(head_grads, rank_id, ctx_size)
         key_rows_heads = key_rows.reshape(local_width, kv_count, head_size)
         value_rows_heads = value_rows.reshape(local_width, kv_count, head_size)
         back_rows = jnp.einsum(
-            "jhtd,fjd->htf", every_half[:, :, 0], key_rows_heads, preferred_element_type=jnp.float32
+            "jtd,fjd->tf", every_head[:, 0], key_rows_heads, preferred_element_type=jnp.float32
         )
         back_rows = back_rows + jnp.einsum(
-            "jhtd,fjd->htf",
-            every_half[:, :, 1],
+            "jtd,fjd->tf",
+            every_head[:, 1],
             value_rows_heads,
             preferred_element_type=jnp.float32,
         )

time: 431 us -> 402 us (0.933)
  waiting for transfers between devices: 155 us -> 118 us
  starting transfers between devices: 49.8 us -> 66.7 us
  between operations: 18.8 us -> 5.29 us
  other arithmetic: 38.7 us -> 44.6 us
    all_gather x2 -> x0, waiting for transfers between devices: 49.6 us -> none  [on_device(): every_half = lax.all_gather(my_half, 'ctx', axis=0, tiled=False)]
    ppermute x16 -> x24, starting transfers between devices: 18 us -> 31.9 us  [swapped_with(): return lax.ppermute(array, axis, [(i, i ^ mask) for i in range(count)])]
    ppermute x16 -> x24, waiting for transfers between devices: 35 us -> 45.2 us  [swapped_with(): return lax.ppermute(array, axis, [(i, i ^ mask) for i in range(count)])]
    all_to_all x2, waiting for transfers between devices: 12.8 us -> 18.1 us  [on_device(): lax.all_to_all(jnp.stack([attended.reshape(ctx_size, local_rows, -1), gra...]
    unnamed x156 -> x164, local copies, waits for them, and re-layouts: 38 us -> 38.9 us
  transfers between devices with their start and end apart: 28 -> 34, of which waited for: 13 -> 14; matrix products, arithmetic and copies ran while one was open for 42% -> 45% of each run, Pallas kernels for 0% -> 0%
where the time goes in v1:
time: 402 us; the launch traced here: 396 us
  waiting for transfers between devices  118 us (29%)
  local copies, waits for them, and re-layouts  101 us (25%)
  starting transfers between devices  66.7 us (17%)
  matrix products  60.2 us (15%)
  other arithmetic  44.6 us (11%)
  between operations  5.29 us (1%)
    ppermute x24, waiting for transfers between devices, swapped_with(): return lax.ppermute(array, axis, [(i, i ^ mask) for i in range(count)])  45.2 us
    unnamed x164, local copies, waits for them, and re-layouts  38.9 us
    ppermute x4, waiting for transfers between devices, passed_along(): lax.ppermute(array, axis, [(i, (i + by) % count) for i in range(count)])  37.3 us
    ppermute x24, starting transfers between devices, swapped_with(): return lax.ppermute(array, axis, [(i, i ^ mask) for i in range(count)])  31.9 us
    sub x4, matrix products, probabilities(): lifted = jnp.exp(scores - row_max)  29.5 us
    all_to_all x2, waiting for transfers between devices, on_device(): lax.all_to_all(jnp.stack([attended.reshape(ctx_size, local_rows, -1), gra...  18.1 us
    all_to_all x2, waiting for transfers between devices, on_device(): lax.all_to_all(jnp.stack(outgoing), 'ctx', split_axis=2, concat_axis=1, t...  17.1 us
    all_to_all x2, starting transfers between devices, on_device(): lax.all_to_all(jnp.stack(outgoing), 'ctx', split_axis=2, concat_axis=1, t...  16.1 us
  transfers between devices with their start and end apart: 34, of which 14 were waited for; matrix products, arithmetic and copies ran while one was open for 45% of the time, Pallas kernels for 0%

profile of v1, /device:TPU:1, one launch (start us, length us, event | category | flops | bytes accessed | tf_op | source)
XLA Modules:
  0.0 395.8 jit_solution(17370217560663627197)
XLA Ops:
  2.3 2.3 slice_convert_fusion.4
  8.9 2.0 copy.189
  10.9 8.9 %all-to-all-start.1 = ((bf16[3,32,16,512]{3,1,0,2:T(8,128)(2,1)}), bf16[3,32,16,512]{3,1,0,2:T(8,128)(2,1)S(1)}, u32[]{:S(2)}, u32[]{:S(2)}) async-start(bf16[3,32,16,512]{3,1,0,2:T(8,128)(2,1)} %copy.189), calls=%async_computation.1 | async-start | bytes 3145728 | tf_op jit(solution)/shard_map/all_to_all | solution.py:207
  20.0 1.8 copy.293
  21.9 3.2 copy.292
  32.1 2.5 copy.186
  34.6 2.5 slice_bitcast_fusion.23
  37.1 1.8 reshape_squeeze.44
  40.6 2.6 reshape.577
  43.2 3.9 slice_bitcast_fusion.22
  47.2 1.8 reshape_squeeze.45
  49.0 1.7 copy.225
  50.7 2.7 reshape.579
  56.4 2.5 copy.302
  60.1 1.8 reshape_squeeze.19
  63.6 2.6 reshape.563
  66.2 1.8 reshape_squeeze.20
  69.7 3.0 reshape.565
  72.7 2.5 copy.299
  77.6 7.2 %all-to-all-start = ((bf16[4,32,16,512]{3,1,0,2:T(8,128)(2,1)}), bf16[4,32,16,512]{3,1,0,2:T(8,128)(2,1)S(1)}, u32[]{:S(2)}, u32[]{:S(2)}) async-start(bf16[4,32,16,512]{3,1,0,2:T(8,128)(2,1)} %copy.186), calls=%async_computation | async-start | bytes 4194304 | tf_op jit(solution)/shard_map/all_to_all | solution.py:207
  92.5 2.0 copy-done
  96.2 17.1 %all-to-all-done = bf16[4,32,16,512]{3,1,0,2:T(8,128)(2,1)S(1)} async-done(((bf16[4,32,16,512]{3,1,0,2:T(8,128)(2,1)}), bf16[4,32,16,512]{3,1,0,2:T(8,128)(2,1)S(1)}, u32[]{:S(2)}, u32[]{:S(2)}) %all-to-all-start) | async-done | bytes 2097184 | tf_op jit(solution)/shard_map/all_to_all | solution.py:207
  120.2 2.0 copy-done.1
  124.7 3.0 fusion.41
  135.0 3.1 convert_add_fusion.1
  140.3 2.5 convert_add_fusion
  143.5 1.8 collective-permute-start.15
  146.9 7.0 %collective-permute-done.1 = bf16[4,128,512]{2,1,0:T(8,128)(2,1)S(1)} collective-permute-done((bf16[4,128,512]{2,1,0:T(8,128)(2,1)S(1)}, bf16[4,128,512]{2,1,0:T(8,128)(2,1)S(1)}, u32[]{:S(2)}, u32[]{:S(2)}) %collective-permute-start.1) | collective-permute-done | bytes 524320 | tf_op jit(solution)/shard_map/ppermute | solution.py:21
  156.0 17.4 %collective-permute-done.2 = bf16[4,128,256]{2,1,0:T(8,128)(2,1)S(1)} collective-permute-done((bf16[4,128,256]{2,1,0:T(8,128)(2,1)S(1)}, bf16[4,128,256]{2,1,0:T(8,128)(2,1)S(1)}, u32[]{:S(2)}, u32[]{:S(2)}) %collective-permute-start.2) | collective-permute-done | bytes 262176 | tf_op jit(solution)/shard_map/ppermute | solution.py:21
  174.1 3.4 collective-permute-done.3
  179.3 2.7 collective-permute-start.7
  182.9 2.1 collective-permute-start.16
  189.1 7.7 %fusion.277 = (f32[4,512]{1,0:T(4,128)S(1)}, f32[4,512,1024]{1,2,0:T(8,128)}) fusion(pred[512,1024]{0,1:T(8,128)(4,1)} %get-tuple-element.70, bf16[512,4,128]{2,1,0:T(4,128)(2,1)} %reshape_reshape_squeeze.33, bf16[512,128]{1,0:T(8,128)(2,1)S(1)} %bitcast.658, bf16[512,128]{1,0:T(8,128)(2,1)} %get-tuple-element.56), kind=kOutput, calls=%fused_computation.369 | convolution fusion | flops 545784832 | bytes 9707520 | tf_op jit(solution)/shard_map/sub | solution.py:103
  196.9 4.8 %fusion.28 = bf16[4,512,1024]{1,2,0:T(8,128)(2,1)S(1)} fusion(f32[4,512,1024]{1,2,0:T(8,128)} %get-tuple-element.76, f32[4,512]{1,0:T(4,128)S(1)} %get-tuple-element.75), kind=kLoop, calls=%fused_computation.46 | loop fusion | flops 4194304 | bytes 12591104 | tf_op jit(solution)/shard_map/convert_element_type | solution.py:109
  203.2 2.3 fusion.9
  205.5 2.1 copy-done.19
  209.7 7.6 %fusion.286 = (f32[4,512]{1,0:T(4,128)S(1)}, f32[4,512,1024]{1,2,0:T(8,128)}) fusion(pred[512,1024]{0,1:T(8,128)(4,1)} %get-tuple-element.67, bf16[512,4,128]{2,1,0:T(4,128)(2,1)S(1)} %copy-done.40, bf16[512,128]{1,0:T(8,128)(2,1)S(1)} %bitcast.659, bf16[512,128]{1,0:T(8,128)(2,1)} %get-tuple-element.54), kind=kOutput, calls=%fused_computation.370 | convolution fusion | flops 545784832 | bytes 9707520 | tf_op jit(solution)/shard_map/sub | solution.py:103
  220.9 2.0 collective-permute-start.20
  223.7 4.4 %collective-permute-done.20 = bf16[4,128,128]{2,1,0:T(8,128)(2,1)S(1)} collective-permute-done((bf16[4,128,128]{2,1,0:T(8,128)(2,1)S(1)}, bf16[4,128,128]{2,1,0:T(8,128)(2,1)S(1)}, u32[]{:S(2)}, u32[]{:S(2)}) %collective-permute-start.20) | collective-permute-done | bytes 131104 | tf_op jit(solution)/shard_map/ppermute | solution.py:21
  229.0 4.2 %fusion.68 = bf16[512,4,128]{0,2,1:T(8,128)(2,1)S(1)} fusion(f32[4,512,1024]{1,2,0:T(8,128)} %get-tuple-element.78, f32[4,512]{1,0:T(4,128)S(1)} %get-tuple-element.77, bf16[512,128]{1,0:T(8,128)(2,1)S(1)} %bitcast.663, bf16[512,128]{1,0:T(8,128)(2,1)S(1)} %copy-done.61), kind=kOutput, calls=%fused_computation.113 | convolution fusion | flops 541851648 | bytes 9183232 | tf_op jit(solution)/shard_map/gts,sd->tgd/dot_general | solution.py:110
  234.7 6.5 %fusion.295 = (f32[4,512]{1,0:T(4,128)S(1)}, f32[4,512,1024]{1,2,0:T(8,128)}) fusion(pred[512,1024]{0,1:T(8,128)(4,1)S(1)} %copy-done.53, bf16[512,4,128]{2,1,0:T(4,128)(2,1)S(1)} %copy-done.39, bf16[512,128]{1,0:T(8,128)(2,1)S(1)} %bitcast.652, bf16[512,128]{1,0:T(8,128)(2,1)S(1)} %get-tuple-element.60), kind=kOutput, calls=%fused_computation.371 | convolution fusion | flops 545784832 | bytes 9707520 | tf_op jit(solution)/shard_map/sub | solution.py:103
  241.2 4.8 %fusion.29 = bf16[4,512,1024]{1,2,0:T(8,128)(2,1)S(1)} fusion(f32[4,512,1024]{1,2,0:T(8,128)} %get-tuple-element.80, f32[4,512]{1,0:T(4,128)S(1)} %get-tuple-element.79), kind=kLoop, calls=%fused_computation.47 | loop fusion | flops 4194304 | bytes 12591104 | tf_op jit(solution)/shard_map/convert_element_type | solution.py:109
  247.5 2.3 fusion.6
  249.9 1.9 copy-done.18
  256.8 2.2 collective-permute-start.10
  261.2 5.3 %collective-permute-done.10 = bf16[2,2,256,128]{3,2,0,1:T(8,128)(2,1)S(1)} collective-permute-done((bf16[2,2,256,128]{3,2,0,1:T(8,128)(2,1)S(1)}, bf16[2,2,256,128]{3,2,0,1:T(8,128)(2,1)S(1)}, u32[]{:S(2)}, u32[]{:S(2)}) %collective-permute-start.10) | collective-permute-done | bytes 262176 | tf_op jit(solution)/shard_map/ppermute | solution.py:21
  266.6 2.1 collective-permute-start.11
  268.7 2.5 collective-permute-start.24
  271.2 7.7 %fusion.304 = (f32[4,512]{1,0:T(4,128)S(1)}, f32[4,512,1024]{1,2,0:T(8,128)}) fusion(pred[512,1024]{0,1:T(8,128)(4,1)} %get-tuple-element.69, bf16[512,4,128]{2,1,0:T(4,128)(2,1)} %reshape_reshape_squeeze.37, bf16[512,128]{1,0:T(8,128)(2,1)S(1)} %bitcast.653, bf16[512,128]{1,0:T(8,128)(2,1)} %get-tuple-element.58), kind=kOutput, calls=%fused_computation.372 | convolution fusion | flops 545784832 | bytes 9707520 | tf_op jit(solution)/shard_map/sub | solution.py:103
  279.0 2.1 collective-permute-start.25
  281.2 1.8 collective-permute-start.12
  283.0 4.1 %fusion.69 = bf16[512,4,128]{0,2,1:T(8,128)(2,1)S(1)} fusion(f32[4,512,1024]{1,2,0:T(8,128)} %get-tuple-element.82, f32[4,512]{1,0:T(4,128)S(1)} %get-tuple-element.81, bf16[512,128]{1,0:T(8,128)(2,1)S(1)} %bitcast.657, bf16[512,128]{1,0:T(8,128)(2,1)S(1)} %get-tuple-element.57), kind=kOutput, calls=%fused_computation.114 | convolution fusion | flops 541851648 | bytes 9183232 | tf_op jit(solution)/shard_map/gts,sd->tgd/dot_general | solution.py:110
  287.2 5.2 %collective-permute-done.25 = bf16[4,2,256,128]{3,2,0,1:T(8,128)(2,1)S(1)} collective-permute-done((bf16[4,2,256,128]{3,2,0,1:T(8,128)(2,1)S(1)}, bf16[4,2,256,128]{3,2,0,1:T(8,128)(2,1)S(1)}, u32[]{:S(2)}, u32[]{:S(2)}) %collective-permute-start.25) | collective-permute-done | bytes 524320 | tf_op jit(solution)/shard_map/ppermute | solution.py:21
  292.6 2.6 collective-permute-start.26
  298.5 4.4 %all-to-all-start.2 = ((bf16[2,16,32,512]{3,2,0,1:T(8,128)(2,1)}), bf16[2,16,32,512]{3,2,0,1:T(8,128)(2,1)S(1)}, u32[]{:S(2)}, u32[]{:S(2)}) async-start(bf16[2,16,32,512]{3,2,0,1:T(8,128)(2,1)} %copy.219), calls=%async_computation.2 | async-start | bytes 2097152 | tf_op jit(solution)/shard_map/all_to_all | solution.py:279
  302.9 3.9 fusion.63
  309.7 2.2 maximum_select_fusion.1
  314.6 5.3 %all-to-all-done.2 = bf16[2,16,32,512]{3,2,0,1:T(8,128)(2,1)S(1)} async-done(((bf16[2,16,32,512]{3,2,0,1:T(8,128)(2,1)}), bf16[2,16,32,512]{3,2,0,1:T(8,128)(2,1)S(1)}, u32[]{:S(2)}, u32[]{:S(2)}) %all-to-all-start.2) | async-done | bytes 1048608 | tf_op jit(solution)/shard_map/all_to_all | solution.py:279
  320.0 5.0 %all-to-all-start.3 = ((bf16[2,16,32,512]{3,2,0,1:T(8,128)(2,1)}), bf16[2,16,32,512]{3,2,0,1:T(8,128)(2,1)}, u32[]{:S(2)}, u32[]{:S(2)}) async-start(bf16[2,16,32,512]{3,2,0,1:T(8,128)(2,1)} %copy.250), calls=%async_computation.3 | async-start | bytes 2097152 | tf_op jit(solution)/shard_map/all_to_all | solution.py:279
  329.6 12.8 %all-to-all-done.3 = bf16[2,16,32,512]{3,2,0,1:T(8,128)(2,1)} async-done(((bf16[2,16,32,512]{3,2,0,1:T(8,128)(2,1)}), bf16[2,16,32,512]{3,2,0,1:T(8,128)(2,1)}, u32[]{:S(2)}, u32[]{:S(2)}) %all-to-all-start.3) | async-done | bytes 1048608 | tf_op jit(solution)/shard_map/all_to_all | solution.py:279
  342.3 1.9 copy.382
  346.3 7.0 %collective-permute-start.28 = (bf16[32,8192]{1,0:T(8,128)(2,1)S(1)}, bf16[32,8192]{1,0:T(8,128)(2,1)S(1)}, u32[]{:S(2)}, u32[]{:S(2)}) collective-permute-start(bf16[32,8192]{1,0:T(8,128)(2,1)S(1)} %get-tuple-element.12), channel_id=1, source_target_pairs={{0,240},{16,0},{32,16},{48,32},{64,48},{80,64},{96,80},{112,96},{1... | collective-permute-start | bytes 1572872 | tf_op jit(solution)/shard_map/ppermute | solution.py:11
  355.8 7.9 %collective-permute-done.28 = bf16[32,8192]{1,0:T(8,128)(2,1)S(1)} collective-permute-done((bf16[32,8192]{1,0:T(8,128)(2,1)S(1)}, bf16[32,8192]{1,0:T(8,128)(2,1)S(1)}, u32[]{:S(2)}, u32[]{:S(2)}) %collective-permute-start.28) | collective-permute-done | bytes 524320 | tf_op jit(solution)/shard_map/ppermute | solution.py:11
  363.7 29.2 %collective-permute-done.29 = bf16[32,8192]{1,0:T(8,128)(2,1)S(1)} collective-permute-done((bf16[32,8192]{1,0:T(8,128)(2,1)S(1)}, bf16[32,8192]{1,0:T(8,128)(2,1)S(1)}, u32[]{:S(2)}, u32[]{:S(2)}) %collective-permute-start.29) | collective-permute-done | bytes 524320 | tf_op jit(solution)/shard_map/ppermute | solution.py:11
  (339 shorter events, 101.4 us)
Async XLA Ops:
  0.7 6.1 %copy-start.11 = (bf16[1,2,32,8192]{3,2,1,0:T(8,128)(2,1)S(1)}, bf16[1,2,32,8192]{3,2,1,0:T(8,128)(2,1)}, u32[]{:S(2)}) copy-start(bf16[1,2,32,8192]{3,2,1,0:T(8,128)(2,1)} %param.11) | copy-start | bytes 3145732
  8.3 22.0 %copy-start.65 = (f32[32]{0:T(128)}, f32[32]{0:T(128)S(1)}, u32[]{:S(2)}) copy-start(f32[32]{0:T(128)S(1)} %get-tuple-element.90) | copy-start | bytes 388
  10.9 15.1 %copy-start.60 = (bf16[1,2,32,8,128]{4,3,2,1,0:T(8,128)(2,1)S(1)}, bf16[1,2,32,8,128]{4,3,2,1,0:T(8,128)(2,1)}, u32[]{:S(2)}) copy-start(bf16[1,2,32,8,128]{4,3,2,1,0:T(8,128)(2,1)} %param.12) | copy-start | bytes 393220
  10.9 65.5 %all-to-all-start.1 = ((bf16[3,32,16,512]{3,1,0,2:T(8,128)(2,1)}), bf16[3,32,16,512]{3,1,0,2:T(8,128)(2,1)S(1)}, u32[]{:S(2)}, u32[]{:S(2)}) async-start(bf16[3,32,16,512]{3,1,0,2:T(8,128)(2,1)} %copy.189), calls=%async_computation.1 | async-start | bytes 3145728 | tf_op jit(solution)/shard_map/all_to_all | solution.py:207
  20.0 10.3 %copy-start.56 = (f32[16,512]{1,0:T(8,128)}, f32[16,512]{1,0:T(8,128)S(1)}, u32[]{:S(2)}) copy-start(f32[16,512]{1,0:T(8,128)S(1)} %mul.365) | copy-start | bytes 98308
  21.9 10.0 %copy-start.8 = (f32[4,8,16,512]{3,2,1,0:T(8,128)}, f32[4,8,16,512]{3,2,1,0:T(8,128)S(1)}, u32[]{:S(2)}) copy-start(f32[4,8,16,512]{3,2,1,0:T(8,128)S(1)} %copy.293) | copy-start | bytes 3145732
  26.0 5.8 %copy-start.34 = (bf16[4,8,16,512]{3,2,1,0:T(8,128)(2,1)S(1)}, bf16[4,8,16,512]{3,2,1,0:T(8,128)(2,1)}, u32[]{:S(2)}) copy-start(bf16[4,8,16,512]{3,2,1,0:T(8,128)(2,1)} %copy.294) | copy-start | bytes 1572868
  47.2 6.2 %copy-start.67 = (s32[1,2,2]{2,1,0:T(2,128)S(1)}, s32[1,2,2]{2,1,0:T(2,128)}, u32[]{:S(2)}) copy-start(s32[1,2,2]{2,1,0:T(2,128)} %param.17) | copy-start | bytes 52
  50.7 8.1 %copy-start.25 = (bf16[64,8,8,128]{3,1,2,0:T(8,128)(2,1)S(1)}, bf16[64,8,8,128]{3,1,2,0:T(8,128)(2,1)}, u32[]{:S(2)}) copy-start(bf16[64,8,8,128]{3,1,2,0:T(8,128)(2,1)} %get-tuple-element.15) | copy-start | bytes 3145732
  77.6 35.7 %all-to-all-start = ((bf16[4,32,16,512]{3,1,0,2:T(8,128)(2,1)}), bf16[4,32,16,512]{3,1,0,2:T(8,128)(2,1)S(1)}, u32[]{:S(2)}, u32[]{:S(2)}) async-start(bf16[4,32,16,512]{3,1,0,2:T(8,128)(2,1)} %copy.186), calls=%async_computation | async-start | bytes 4194304 | tf_op jit(solution)/shard_map/all_to_all | solution.py:207
  96.1 38.9 %collective-permute-start = (bf16[4,256,1024]{2,1,0:T(8,128)(2,1)}, bf16[4,256,1024]{2,1,0:T(8,128)(2,1)}, u32[]{:S(2)}, u32[]{:S(2)}) collective-permute-start(bf16[4,256,1024]{2,1,0:T(8,128)(2,1)} %constant_dynamic-slice_fusion.1), channel_id=1, source_target_pairs={{0,1},{1,0},{2,3},{3,2},{4,5},{5,4},{6,7},{7,6},{8,9},{9,8},{10,11... | collective-permute-start | bytes 6291464 | tf_op jit(solution)/shard_map/ppermute | solution.py:21
  122.3 7.3 %copy-start.31 = (bf16[1,16,32,1,512]{4,2,1,3,0:T(8,128)(2,1)S(1)}, bf16[1,16,32,1,512]{4,2,1,3,0:T(8,128)(2,1)}, u32[]{:S(2)}) copy-start(bf16[1,16,32,1,512]{4,2,1,3,0:T(8,128)(2,1)} %get-tuple-element.26) | copy-start | bytes 1572868
  123.8 16.3 %collective-permute-start.14 = (bf16[4,256,1024]{2,1,0:T(8,128)(2,1)}, bf16[4,256,1024]{2,1,0:T(8,128)(2,1)}, u32[]{:S(2)}, u32[]{:S(2)}) collective-permute-start(bf16[4,256,1024]{2,1,0:T(8,128)(2,1)} %constant_dynamic-slice_fusion), channel_id=1, source_target_pairs={{0,1},{1,0},{2,3},{3,2},{4,5},{5,4},{6,7},{7,6},{8,9},{9,8},{10,11... | collective-permute-start | bytes 6291464 | tf_op jit(solution)/shard_map/ppermute | solution.py:21
  138.8 15.1 %collective-permute-start.1 = (bf16[4,128,512]{2,1,0:T(8,128)(2,1)S(1)}, bf16[4,128,512]{2,1,0:T(8,128)(2,1)S(1)}, u32[]{:S(2)}, u32[]{:S(2)}) collective-permute-start(bf16[4,128,512]{2,1,0:T(8,128)(2,1)S(1)} %dynamic-slice_convert_fusion.3), channel_id=1, source_target_pairs={{0,8},{1,9},{2,10},{3,11},{4,12},{5,13},{6,14},{7,15},{8,0},{9,1},... | collective-permute-start | bytes 1572872 | tf_op jit(solution)/shard_map/ppermute | solution.py:21
  139.9 14.4 %collective-permute-start.4 = (bf16[4,128,512]{2,1,0:T(8,128)(2,1)S(1)}, bf16[4,128,512]{2,1,0:T(8,128)(2,1)S(1)}, u32[]{:S(2)}, u32[]{:S(2)}) collective-permute-start(bf16[4,128,512]{2,1,0:T(8,128)(2,1)S(1)} %dynamic-slice_convert_fusion.2), channel_id=1, source_target_pairs={{0,2},{1,3},{2,0},{3,1},{4,6},{5,7},{6,4},{7,5},{8,10},{9,11},{10,... | collective-permute-start | bytes 1572872 | tf_op jit(solution)/shard_map/ppermute | solution.py:21
  143.5 38.5 %collective-permute-start.15 = (bf16[4,128,512]{2,1,0:T(8,128)(2,1)S(1)}, bf16[4,128,512]{2,1,0:T(8,128)(2,1)S(1)}, u32[]{:S(2)}, u32[]{:S(2)}) collective-permute-start(bf16[4,128,512]{2,1,0:T(8,128)(2,1)S(1)} %dynamic-slice_convert_fusion.1), channel_id=1, source_target_pairs={{0,8},{1,9},{2,10},{3,11},{4,12},{5,13},{6,14},{7,15},{8,0},{9,1},... | collective-permute-start | bytes 1572872 | tf_op jit(solution)/shard_map/ppermute | solution.py:21
  145.4 39.6 %collective-permute-start.18 = (bf16[4,128,512]{2,1,0:T(8,128)(2,1)S(1)}, bf16[4,128,512]{2,1,0:T(8,128)(2,1)S(1)}, u32[]{:S(2)}, u32[]{:S(2)}) collective-permute-start(bf16[4,128,512]{2,1,0:T(8,128)(2,1)S(1)} %dynamic-slice_convert_fusion), channel_id=1, source_target_pairs={{0,2},{1,3},{2,0},{3,1},{4,6},{5,7},{6,4},{7,5},{8,10},{9,11},{10,... | collective-permute-start | bytes 1572872 | tf_op jit(solution)/shard_map/ppermute | solution.py:21
  154.2 19.3 %collective-permute-start.2 = (bf16[4,128,256]{2,1,0:T(8,128)(2,1)S(1)}, bf16[4,128,256]{2,1,0:T(8,128)(2,1)S(1)}, u32[]{:S(2)}, u32[]{:S(2)}) collective-permute-start(bf16[4,128,256]{2,1,0:T(8,128)(2,1)S(1)} %dynamic-slice_convert_fusion.7), channel_id=1, source_target_pairs={{0,4},{1,5},{2,6},{3,7},{4,0},{5,1},{6,2},{7,3},{8,12},{9,13},{10,... | collective-permute-start | bytes 786440 | tf_op jit(solution)/shard_map/ppermute | solution.py:21
  154.6 19.1 %collective-permute-start.5 = (bf16[4,128,256]{2,1,0:T(8,128)(2,1)S(1)}, bf16[4,128,256]{2,1,0:T(8,128)(2,1)S(1)}, u32[]{:S(2)}, u32[]{:S(2)}) collective-permute-start(bf16[4,128,256]{2,1,0:T(8,128)(2,1)S(1)} %dynamic-slice_convert_fusion.6), channel_id=1, source_target_pairs={{0,8},{1,9},{2,10},{3,11},{4,12},{5,13},{6,14},{7,15},{8,0},{9,1},... | collective-permute-start | bytes 786440 | tf_op jit(solution)/shard_map/ppermute | solution.py:21
  173.6 3.9 collective-permute-start.3
  173.8 5.4 %collective-permute-start.6 = (bf16[4,128,128]{2,1,0:T(8,128)(2,1)S(1)}, bf16[4,128,128]{2,1,0:T(8,128)(2,1)S(1)}, u32[]{:S(2)}, u32[]{:S(2)}) collective-permute-start(bf16[4,128,128]{2,1,0:T(8,128)(2,1)S(1)} %dynamic-slice_convert_fusion.10), channel_id=1, source_target_pairs={{0,4},{1,5},{2,6},{3,7},{4,0},{5,1},{6,2},{7,3},{8,12},{9,13},{10,... | collective-permute-start | bytes 393224 | tf_op jit(solution)/shard_map/ppermute | solution.py:21
  179.3 8.1 %collective-permute-start.7 = (bf16[4,256,128]{2,1,0:T(8,128)(2,1)S(1)}, bf16[4,256,128]{2,1,0:T(8,128)(2,1)S(1)}, u32[]{:S(2)}, u32[]{:S(2)}) collective-permute-start(bf16[4,256,128]{2,1,0:T(8,128)(2,1)S(1)} %pad_maximum_fusion.22), channel_id=1, source_target_pairs={{0,1},{1,0},{2,3},{3,2},{4,5},{5,4},{6,7},{7,6},{8,9},{9,8},{10,11... | collective-permute-start | bytes 786440 | tf_op jit(solution)/shard_map/ppermute | solution.py:21
  182.9 34.4 %collective-permute-start.16 = (bf16[4,128,256]{2,1,0:T(8,128)(2,1)}, bf16[4,128,256]{2,1,0:T(8,128)(2,1)}, u32[]{:S(2)}, u32[]{:S(2)}) collective-permute-start(bf16[4,128,256]{2,1,0:T(8,128)(2,1)} %dynamic-slice_convert_fusion.5), channel_id=1, source_target_pairs={{0,4},{1,5},{2,6},{3,7},{4,0},{5,1},{6,2},{7,3},{8,12},{9,13},{10,... | collective-permute-start | bytes 786440 | tf_op jit(solution)/shard_map/ppermute | solution.py:21
  186.0 33.9 %collective-permute-start.19 = (bf16[4,128,256]{2,1,0:T(8,128)(2,1)}, bf16[4,128,256]{2,1,0:T(8,128)(2,1)}, u32[]{:S(2)}, u32[]{:S(2)}) collective-permute-start(bf16[4,128,256]{2,1,0:T(8,128)(2,1)} %dynamic-slice_convert_fusion.4), channel_id=1, source_target_pairs={{0,8},{1,9},{2,10},{3,11},{4,12},{5,13},{6,14},{7,15},{8,0},{9,1},... | collective-permute-start | bytes 786440 | tf_op jit(solution)/shard_map/ppermute | solution.py:21
  196.8 6.3 %slice-start = ((s8[8388608]{0:T(1024)(128)(4,1)}), s8[4194304]{0:T(1024)(128)(4,1)S(1)}, s32[]{:S(2)}) async-start(s8[8388608]{0:T(1024)(128)(4,1)} %bitcast.586), calls=%async_computation.4 | async-start | bytes 8388608
  196.8 5.5 %copy-start.52 = (bf16[512,128]{1,0:T(8,128)(2,1)S(1)}, bf16[512,128]{1,0:T(8,128)(2,1)}, u32[]{:S(2)}) copy-start(bf16[512,128]{1,0:T(8,128)(2,1)} %get-tuple-element.55) | copy-start | bytes 393220
  196.9 6.3 %slice-start.1 = ((s8[8388608]{0:T(1024)(128)(4,1)}), s8[4194304]{0:T(1024)(128)(4,1)S(1)}, s32[]{:S(2)}) async-start(s8[8388608]{0:T(1024)(128)(4,1)} %bitcast.586), calls=%async_computation.5 | async-start | bytes 8388608
  202.4 6.0 %copy-start.45 = (bf16[1,512,128]{2,1,0:T(8,128)(2,1)}, bf16[1,512,128]{2,1,0:T(8,128)(2,1)S(1)}, u32[]{:S(2)}) copy-start(bf16[1,512,128]{2,1,0:T(8,128)(2,1)S(1)} %fusion.97) | copy-start | bytes 393220
  209.1 24.1 %collective-permute-start.8 = (bf16[2,512,128]{2,1,0:T(8,128)(2,1)}, bf16[2,512,128]{2,1,0:T(8,128)(2,1)}, u32[]{:S(2)}, u32[]{:S(2)}) collective-permute-start(bf16[2,512,128]{2,1,0:T(8,128)(2,1)} %pad_maximum_fusion.16), channel_id=1, source_target_pairs={{0,1},{1,0},{2,3},{3,2},{4,5},{5,4},{6,7},{7,6},{8,9},{9,8},{10,11... | collective-permute-start | bytes 786440 | tf_op jit(solution)/shard_map/ppermute | solution.py:16
  217.3 11.8 %copy-start.38 = (bf16[512,1,1,128]{3,0,2,1:T(8,128)(2,1)S(1)}, bf16[512,1,1,128]{3,0,2,1:T(8,128)(2,1)}, u32[]{:S(2)}) copy-start(bf16[512,1,1,128]{3,0,2,1:T(8,128)(2,1)} %copy.387) | copy-start | bytes 393220
  217.3 11.8 %copy-start.61 = (bf16[512,128]{1,0:T(8,128)(2,1)S(1)}, bf16[512,128]{1,0:T(8,128)(2,1)}, u32[]{:S(2)}) copy-start(bf16[512,128]{1,0:T(8,128)(2,1)} %get-tuple-element.53) | copy-start | bytes 393220
  218.4 5.2 %collective-permute-start.17 = (bf16[4,128,128]{2,1,0:T(8,128)(2,1)S(1)}, bf16[4,128,128]{2,1,0:T(8,128)(2,1)S(1)}, u32[]{:S(2)}, u32[]{:S(2)}) collective-permute-start(bf16[4,128,128]{2,1,0:T(8,128)(2,1)S(1)} %dynamic-slice_convert_fusion.9), channel_id=1, source_target_pairs={{0,2},{1,3},{2,0},{3,1},{4,6},{5,7},{6,4},{7,5},{8,10},{9,11},{10,... | collective-permute-start | bytes 393224 | tf_op jit(solution)/shard_map/ppermute | solution.py:21
  220.9 7.1 %collective-permute-start.20 = (bf16[4,128,128]{2,1,0:T(8,128)(2,1)S(1)}, bf16[4,128,128]{2,1,0:T(8,128)(2,1)S(1)}, u32[]{:S(2)}, u32[]{:S(2)}) collective-permute-start(bf16[4,128,128]{2,1,0:T(8,128)(2,1)S(1)} %dynamic-slice_convert_fusion.8), channel_id=1, source_target_pairs={{0,4},{1,5},{2,6},{3,7},{4,0},{5,1},{6,2},{7,3},{8,12},{9,13},{10,... | collective-permute-start | bytes 393224 | tf_op jit(solution)/shard_map/ppermute | solution.py:21
  228.1 6.3 %collective-permute-start.21 = (bf16[4,256,128]{2,1,0:T(8,128)(2,1)S(1)}, bf16[4,256,128]{2,1,0:T(8,128)(2,1)S(1)}, u32[]{:S(2)}, u32[]{:S(2)}) collective-permute-start(bf16[4,256,128]{2,1,0:T(8,128)(2,1)S(1)} %pad_maximum_fusion.23), channel_id=1, source_target_pairs={{0,1},{1,0},{2,3},{3,2},{4,5},{5,4},{6,7},{7,6},{8,9},{9,8},{10,11... | collective-permute-start | bytes 786440 | tf_op jit(solution)/shard_map/ppermute | solution.py:21
  234.3 21.5 %collective-permute-start.9 = (bf16[1,2,256,128]{3,2,0,1:T(8,128)(2,1)S(1)}, bf16[1,2,256,128]{3,2,0,1:T(8,128)(2,1)}, u32[]{:S(2)}, u32[]{:S(2)}) collective-permute-start(bf16[1,2,256,128]{3,2,0,1:T(8,128)(2,1)S(1)} %fusion.208), channel_id=1, source_target_pairs={{0,2},{1,3},{2,0},{3,1},{4,6},{5,7},{6,4},{7,5},{8,10},{9,11},{10,... | collective-permute-start | bytes 393224 | tf_op jit(solution)/shard_map/ppermute | solution.py:21
  234.7 6.5 %copy-start.42 = (bf16[512,128]{1,0:T(8,128)(2,1)}, bf16[512,128]{1,0:T(8,128)(2,1)S(1)}, u32[]{:S(2)}) copy-start(bf16[512,128]{1,0:T(8,128)(2,1)S(1)} %get-tuple-element.60) | copy-start | bytes 393220
  241.2 6.3 %slice-start.2 = ((s8[8388608]{0:T(1024)(128)(4,1)}), s8[4194304]{0:T(1024)(128)(4,1)S(1)}, s32[]{:S(2)}) async-start(s8[8388608]{0:T(1024)(128)(4,1)} %bitcast.588), calls=%async_computation.6 | async-start | bytes 8388608
  241.2 6.3 %slice-start.3 = ((s8[8388608]{0:T(1024)(128)(4,1)}), s8[4194304]{0:T(1024)(128)(4,1)S(1)}, s32[]{:S(2)}) async-start(s8[8388608]{0:T(1024)(128)(4,1)} %bitcast.588), calls=%async_computation.7 | async-start | bytes 8388608
  246.7 5.8 %copy-start.49 = (bf16[1,512,128]{2,1,0:T(8,128)(2,1)}, bf16[1,512,128]{2,1,0:T(8,128)(2,1)S(1)}, u32[]{:S(2)}) copy-start(bf16[1,512,128]{2,1,0:T(8,128)(2,1)S(1)} %fusion.103) | copy-start | bytes 393220
  253.3 5.7 %collective-permute-start.22 = (bf16[2,512,128]{2,1,0:T(8,128)(2,1)}, bf16[2,512,128]{2,1,0:T(8,128)(2,1)}, u32[]{:S(2)}, u32[]{:S(2)}) collective-permute-start(bf16[2,512,128]{2,1,0:T(8,128)(2,1)} %pad_maximum_fusion.21), channel_id=1, source_target_pairs={{0,1},{1,0},{2,3},{3,2},{4,5},{5,4},{6,7},{7,6},{8,9},{9,8},{10,11... | collective-permute-start | bytes 786440 | tf_op jit(solution)/shard_map/ppermute | solution.py:16
  256.8 9.7 %collective-permute-start.10 = (bf16[2,2,256,128]{3,2,0,1:T(8,128)(2,1)S(1)}, bf16[2,2,256,128]{3,2,0,1:T(8,128)(2,1)S(1)}, u32[]{:S(2)}, u32[]{:S(2)}) collective-permute-start(bf16[2,2,256,128]{3,2,0,1:T(8,128)(2,1)S(1)} %maximum_select_fusion.8), channel_id=1, source_target_pairs={{0,4},{1,5},{2,6},{3,7},{4,0},{5,1},{6,2},{7,3},{8,12},{9,13},{10,... | collective-permute-start | bytes 786440 | tf_op jit(solution)/shard_map/ppermute | solution.py:21
  260.0 8.7 %collective-permute-start.23 = (bf16[1,2,256,128]{3,2,0,1:T(8,128)(2,1)S(1)}, bf16[1,2,256,128]{3,2,0,1:T(8,128)(2,1)S(1)}, u32[]{:S(2)}, u32[]{:S(2)}) collective-permute-start(bf16[1,2,256,128]{3,2,0,1:T(8,128)(2,1)S(1)} %fusion.209), channel_id=1, source_target_pairs={{0,2},{1,3},{2,0},{3,1},{4,6},{5,7},{6,4},{7,5},{8,10},{9,11},{10,... | collective-permute-start | bytes 393224 | tf_op jit(solution)/shard_map/ppermute | solution.py:21
  266.6 14.5 %collective-permute-start.11 = (bf16[4,2,256,128]{3,2,0,1:T(8,128)(2,1)S(1)}, bf16[4,2,256,128]{3,2,0,1:T(8,128)(2,1)S(1)}, u32[]{:S(2)}, u32[]{:S(2)}) collective-permute-start(bf16[4,2,256,128]{3,2,0,1:T(8,128)(2,1)S(1)} %maximum_select_fusion.6), channel_id=1, source_target_pairs={{0,8},{1,9},{2,10},{3,11},{4,12},{5,13},{6,14},{7,15},{8,0},{9,1},... | collective-permute-start | bytes 1572872 | tf_op jit(solution)/shard_map/ppermute | solution.py:21
  268.7 10.2 %collective-permute-start.24 = (bf16[2,2,256,128]{3,2,0,1:T(8,128)(2,1)S(1)}, bf16[2,2,256,128]{3,2,0,1:T(8,128)(2,1)S(1)}, u32[]{:S(2)}, u32[]{:S(2)}) collective-permute-start(bf16[2,2,256,128]{3,2,0,1:T(8,128)(2,1)S(1)} %maximum_select_fusion.9), channel_id=1, source_target_pairs={{0,4},{1,5},{2,6},{3,7},{4,0},{5,1},{6,2},{7,3},{8,12},{9,13},{10,... | collective-permute-start | bytes 786440 | tf_op jit(solution)/shard_map/ppermute | solution.py:21
  279.0 13.5 %collective-permute-start.25 = (bf16[4,2,256,128]{3,2,0,1:T(8,128)(2,1)S(1)}, bf16[4,2,256,128]{3,2,0,1:T(8,128)(2,1)S(1)}, u32[]{:S(2)}, u32[]{:S(2)}) collective-permute-start(bf16[4,2,256,128]{3,2,0,1:T(8,128)(2,1)S(1)} %maximum_select_fusion.7), channel_id=1, source_target_pairs={{0,8},{1,9},{2,10},{3,11},{4,12},{5,13},{6,14},{7,15},{8,0},{9,1},... | collective-permute-start | bytes 1572872 | tf_op jit(solution)/shard_map/ppermute | solution.py:21
  281.2 13.9 %collective-permute-start.12 = (bf16[8,2,256,128]{3,2,0,1:T(8,128)(2,1)S(1)}, bf16[8,2,256,128]{3,2,0,1:T(8,128)(2,1)S(1)}, u32[]{:S(2)}, u32[]{:S(2)}) collective-permute-start(bf16[8,2,256,128]{3,2,0,1:T(8,128)(2,1)S(1)} %maximum_select_fusion.2), channel_id=1, source_target_pairs={{0,1},{1,0},{2,3},{3,2},{4,5},{5,4},{6,7},{7,6},{8,9},{9,8},{10,11... | collective-permute-start | bytes 3145736 | tf_op jit(solution)/shard_map/ppermute | solution.py:21
  287.2 8.6 %copy-start.36 = (bf16[64,8,8,128]{3,2,1,0:T(8,128)(2,1)S(1)}, bf16[64,8,8,128]{3,2,1,0:T(8,128)(2,1)}, u32[]{:S(2)}) copy-start(bf16[64,8,8,128]{3,2,1,0:T(8,128)(2,1)} %copy.299) | copy-start | bytes 3145732
  292.6 17.1 %collective-permute-start.26 = (bf16[8,2,256,128]{3,2,0,1:T(8,128)(2,1)S(1)}, bf16[8,2,256,128]{3,2,0,1:T(8,128)(2,1)}, u32[]{:S(2)}, u32[]{:S(2)}) collective-permute-start(bf16[8,2,256,128]{3,2,0,1:T(8,128)(2,1)S(1)} %maximum_select_fusion.3), channel_id=1, source_target_pairs={{0,1},{1,0},{2,3},{3,2},{4,5},{5,4},{6,7},{7,6},{8,9},{9,8},{10,11... | collective-permute-start | bytes 3145736 | tf_op jit(solution)/shard_map/ppermute | solution.py:21
  297.3 5.6 %copy-start.43 = (bf16[512,128]{1,0:T(8,128)(2,1)S(1)}, bf16[512,128]{1,0:T(8,128)(2,1)}, u32[]{:S(2)}) copy-start(bf16[512,128]{1,0:T(8,128)(2,1)} %copy-done.42) | copy-start | bytes 393220
  298.5 21.5 %all-to-all-start.2 = ((bf16[2,16,32,512]{3,2,0,1:T(8,128)(2,1)}), bf16[2,16,32,512]{3,2,0,1:T(8,128)(2,1)S(1)}, u32[]{:S(2)}, u32[]{:S(2)}) async-start(bf16[2,16,32,512]{3,2,0,1:T(8,128)(2,1)} %copy.219), calls=%async_computation.2 | async-start | bytes 2097152 | tf_op jit(solution)/shard_map/all_to_all | solution.py:279
  320.0 22.4 %all-to-all-start.3 = ((bf16[2,16,32,512]{3,2,0,1:T(8,128)(2,1)}), bf16[2,16,32,512]{3,2,0,1:T(8,128)(2,1)}, u32[]{:S(2)}, u32[]{:S(2)}) async-start(bf16[2,16,32,512]{3,2,0,1:T(8,128)(2,1)} %copy.250), calls=%async_computation.3 | async-start | bytes 2097152 | tf_op jit(solution)/shard_map/all_to_all | solution.py:279
  327.4 17.0 %copy-start.9 = (f32[4,8,16,512]{3,2,1,0:T(8,128)S(1)}, f32[4,8,16,512]{3,2,1,0:T(8,128)}, u32[]{:S(2)}) copy-start(f32[4,8,16,512]{3,2,1,0:T(8,128)} %copy-done.8) | copy-start | bytes 3145732
  327.4 17.0 %copy-start.57 = (f32[16,512]{1,0:T(8,128)S(1)}, f32[16,512]{1,0:T(8,128)}, u32[]{:S(2)}) copy-start(f32[16,512]{1,0:T(8,128)} %copy-done.56) | copy-start | bytes 98308
  327.4 17.0 %copy-start.66 = (f32[32]{0:T(128)S(1)}, f32[32]{0:T(128)}, u32[]{:S(2)}) copy-start(f32[32]{0:T(128)} %copy-done.65) | copy-start | bytes 388
  329.5 16.0 %copy-start.3 = (bf16[1,2,32,8192]{3,2,1,0:T(8,128)(2,1)S(1)}, bf16[1,2,32,8192]{3,2,1,0:T(8,128)(2,1)}, u32[]{:S(2)}) copy-start(bf16[1,2,32,8192]{3,2,1,0:T(8,128)(2,1)} %param.10) | copy-start | bytes 3145732
  329.5 16.1 %copy-start.12 = (bf16[1,2,32,8192]{3,2,1,0:T(8,128)(2,1)S(1)}, bf16[1,2,32,8192]{3,2,1,0:T(8,128)(2,1)}, u32[]{:S(2)}) copy-start(bf16[1,2,32,8192]{3,2,1,0:T(8,128)(2,1)} %param.11) | copy-start | bytes 3145732
  329.6 16.1 %copy-start.58 = (f32[1,1,8192]{2,1,0:T(1,128)S(1)}, f32[1,1,8192]{2,1,0:T(1,128)}, u32[]{:S(2)}) copy-start(f32[1,1,8192]{2,1,0:T(1,128)} %get-tuple-element.61) | copy-start | bytes 98308
  329.6 16.1 %copy-start.59 = (f32[1,1,8192]{2,1,0:T(1,128)S(1)}, f32[1,1,8192]{2,1,0:T(1,128)}, u32[]{:S(2)}) copy-start(f32[1,1,8192]{2,1,0:T(1,128)} %get-tuple-element.62) | copy-start | bytes 98308
  345.6 8.5 %copy-start.5 = (bf16[1,2,32,8192]{3,2,1,0:T(8,128)(2,1)S(1)}, bf16[1,2,32,8192]{3,2,1,0:T(8,128)(2,1)}, u32[]{:S(2)}) copy-start(bf16[1,2,32,8192]{3,2,1,0:T(8,128)(2,1)} %param.9) | copy-start | bytes 3145732
  345.6 8.5 %copy-start.24 = (f32[4,8,16,512]{3,1,2,0:T(8,128)S(1)}, f32[4,8,16,512]{3,1,2,0:T(8,128)}, u32[]{:S(2)}) copy-start(f32[4,8,16,512]{3,1,2,0:T(8,128)} %copy.300) | copy-start | bytes 3145732
  346.3 17.4 %collective-permute-start.28 = (bf16[32,8192]{1,0:T(8,128)(2,1)S(1)}, bf16[32,8192]{1,0:T(8,128)(2,1)S(1)}, u32[]{:S(2)}, u32[]{:S(2)}) collective-permute-start(bf16[32,8192]{1,0:T(8,128)(2,1)S(1)} %get-tuple-element.12), channel_id=1, source_target_pairs={{0,240},{16,0},{32,16},{48,32},{64,48},{80,64},{96,80},{112,96},{1... | collective-permute-start | bytes 1572872 | tf_op jit(solution)/shard_map/ppermute | solution.py:11
  353.3 39.6 %collective-permute-start.29 = (bf16[32,8192]{1,0:T(8,128)(2,1)S(1)}, bf16[32,8192]{1,0:T(8,128)(2,1)S(1)}, u32[]{:S(2)}, u32[]{:S(2)}) collective-permute-start(bf16[32,8192]{1,0:T(8,128)(2,1)S(1)} %get-tuple-element.13), channel_id=1, source_target_pairs={{0,240},{16,0},{32,16},{48,32},{64,48},{80,64},{96,80},{112,96},{1... | collective-permute-start | bytes 1572872 | tf_op jit(solution)/shard_map/ppermute | solution.py:11
  354.3 39.8 %collective-permute-start.27 = (bf16[32,8192]{1,0:T(8,128)(2,1)S(1)}, bf16[32,8192]{1,0:T(8,128)(2,1)S(1)}, u32[]{:S(2)}, u32[]{:S(2)}) collective-permute-start(bf16[32,8192]{1,0:T(8,128)(2,1)S(1)} %get-tuple-element.34), channel_id=1, source_target_pairs={{0,16},{16,32},{32,48},{48,64},{64,80},{80,96},{96,112},{112,128},... | collective-permute-start | bytes 1572872 | tf_op jit(solution)/shard_map/ppermute | solution.py:11
  355.7 38.5 %collective-permute-start.13 = (bf16[32,8192]{1,0:T(8,128)(2,1)S(1)}, bf16[32,8192]{1,0:T(8,128)(2,1)S(1)}, u32[]{:S(2)}, u32[]{:S(2)}) collective-permute-start(bf16[32,8192]{1,0:T(8,128)(2,1)S(1)} %get-tuple-element.33), channel_id=1, source_target_pairs={{0,16},{16,32},{32,48},{48,64},{64,80},{80,96},{96,112},{112,128},... | collective-permute-start | bytes 1572872 | tf_op jit(solution)/shard_map/ppermute | solution.py:11
  (42 other events, 113.5 us)

commit v2 on v1

--- a/solution.py
+++ b/solution.py
@@ -72,12 +72,15 @@
 
 
 def column_order(weight, order, head_size):
-    bits = len(order)
     natural = sorted(order, reverse=True)
-    split = weight.reshape(weight.shape[:-1] + (2,) * bits + (head_size,))
-    lead = weight.ndim - 1
-    axes = list(range(lead)) + [lead + natural.index(m) for m in order] + [lead + bits]
-    return jnp.transpose(split, axes).reshape(weight.shape)
+    blocks = []
+    for new_index in range(2 ** len(order)):
+        old_index = 0
+        for place, mask in enumerate(order):
+            bit = (new_index >> (len(order) - 1 - place)) & 1
+            old_index += bit << (len(order) - 1 - natural.index(mask))
+        blocks.append(weight[..., old_index * head_size : (old_index + 1) * head_size])
+    return jnp.concatenate(blocks, axis=-1)
 
 
 def normalize(in_rows, gain_row):

time: 402 us -> 393 us (0.978)
  local copies, waits for them, and re-layouts: 101 us -> 90 us
    reshape x4 -> x0, local copies, waits for them, and re-layouts: 10.9 us -> none  [column_order(): return jnp.transpose(split, axes).reshape(weight.shape)]
    unnamed x164 -> x198, local copies, waits for them, and re-layouts: 38.9 us -> 49.1 us
    another operation x4 -> x0, local copies, waits for them, and re-layouts: 7.16 us -> none  [column_order(): split = weight.reshape(weight.shape[:-1] + (2,) * bits + (head_size,))]
    transpose x4 -> x0, local copies, waits for them, and re-layouts: 6.8 us -> none  [column_order(): return jnp.transpose(split, axes).reshape(weight.shape)]
  transfers between devices with their start and end apart: 34 -> 34, of which waited for: 14 -> 14; matrix products, arithmetic and copies ran while one was open for 45% -> 44% of each run, Pallas kernels for 0% -> 0%
where the time goes in v2:
time: 393 us; the launch traced here: 387 us
  waiting for transfers between devices  118 us (30%)
  local copies, waits for them, and re-layouts  90 us (23%)
  starting transfers between devices  66.8 us (17%)
  matrix products  62.9 us (16%)
  other arithmetic  44.4 us (11%)
  between operations  5.27 us (1%)
    unnamed x198, local copies, waits for them, and re-layouts  49.1 us
    ppermute x24, waiting for transfers between devices, swapped_with(): return lax.ppermute(array, axis, [(i, i ^ mask) for i in range(count)])  45.7 us
    ppermute x4, waiting for transfers between devices, passed_along(): lax.ppermute(array, axis, [(i, (i + by) % count) for i in range(count)])  37.4 us
    ppermute x24, starting transfers between devices, swapped_with(): return lax.ppermute(array, axis, [(i, i ^ mask) for i in range(count)])  32 us
    sub x4, matrix products, probabilities(): lifted = jnp.exp(scores - row_max)  29.4 us
    all_to_all x2, waiting for transfers between devices, on_device(): lax.all_to_all(jnp.stack([attended.reshape(ctx_size, local_rows, -1), gra...  18.1 us
    all_to_all x2, waiting for transfers between devices, on_device(): lax.all_to_all(jnp.stack(outgoing), 'ctx', split_axis=2, concat_axis=1, t...  16.5 us
    all_to_all x2, starting transfers between devices, on_device(): lax.all_to_all(jnp.stack(outgoing), 'ctx', split_axis=2, concat_axis=1, t...  16.3 us
  transfers between devices with their start and end apart: 34, of which 14 were waited for; matrix products, arithmetic and copies ran while one was open for 44% of the time, Pallas kernels for 0%

profile of v2, /device:TPU:1, one launch (start us, length us, event | category | flops | bytes accessed | tf_op | source)
XLA Modules:
  0.0 387.0 jit_solution(674926387881831346)
XLA Ops:
  0.7 1.7 fusion.124
  2.3 2.3 slice_convert_fusion.4
  8.9 2.0 copy.177
  11.0 8.7 %all-to-all-start.1 = ((bf16[3,32,16,512]{3,1,0,2:T(8,128)(2,1)}), bf16[3,32,16,512]{3,1,0,2:T(8,128)(2,1)S(1)}, u32[]{:S(2)}, u32[]{:S(2)}) async-start(bf16[3,32,16,512]{3,1,0,2:T(8,128)(2,1)} %copy.177), calls=%async_computation.1 | async-start | bytes 3145728 | tf_op jit(solution)/shard_map/all_to_all | solution.py:210
  19.9 3.5 slice_bitcast_fusion.14
  26.2 1.9 copy.277
  28.1 3.2 copy.276
  38.4 2.5 copy.174
  57.0 1.6 slice_dynamic-update-slice_fusion.20
  60.1 1.6 slice_dynamic-update-slice_fusion.18
  63.2 1.7 slice_dynamic-update-slice_fusion.8
  65.0 1.6 slice_dynamic-update-slice_fusion
  67.8 7.6 %all-to-all-start = ((bf16[4,32,16,512]{3,1,0,2:T(8,128)(2,1)}), bf16[4,32,16,512]{3,1,0,2:T(8,128)(2,1)S(1)}, u32[]{:S(2)}, u32[]{:S(2)}) async-start(bf16[4,32,16,512]{3,1,0,2:T(8,128)(2,1)} %copy.174), calls=%async_computation | async-start | bytes 4194304 | tf_op jit(solution)/shard_map/all_to_all | solution.py:210
  75.4 1.7 copy.365
  79.7 2.0 fusion.45
  83.7 2.0 copy-done
  87.3 16.5 %all-to-all-done = bf16[4,32,16,512]{3,1,0,2:T(8,128)(2,1)S(1)} async-done(((bf16[4,32,16,512]{3,1,0,2:T(8,128)(2,1)}), bf16[4,32,16,512]{3,1,0,2:T(8,128)(2,1)S(1)}, u32[]{:S(2)}, u32[]{:S(2)}) %all-to-all-start) | async-done | bytes 2097184 | tf_op jit(solution)/shard_map/all_to_all | solution.py:210
  107.2 2.1 fusion.49
  111.4 2.0 copy-done.1
  116.3 2.8 fusion.41
  126.4 3.1 convert_add_fusion.1
  131.7 2.5 convert_add_fusion
  134.9 1.8 collective-permute-start.15
  138.3 7.0 %collective-permute-done.1 = bf16[4,128,512]{2,1,0:T(8,128)(2,1)S(1)} collective-permute-done((bf16[4,128,512]{2,1,0:T(8,128)(2,1)S(1)}, bf16[4,128,512]{2,1,0:T(8,128)(2,1)S(1)}, u32[]{:S(2)}, u32[]{:S(2)}) %collective-permute-start.1) | collective-permute-done | bytes 524320 | tf_op jit(solution)/shard_map/ppermute | solution.py:21
  147.4 17.5 %collective-permute-done.2 = bf16[4,128,256]{2,1,0:T(8,128)(2,1)S(1)} collective-permute-done((bf16[4,128,256]{2,1,0:T(8,128)(2,1)S(1)}, bf16[4,128,256]{2,1,0:T(8,128)(2,1)S(1)}, u32[]{:S(2)}, u32[]{:S(2)}) %collective-permute-start.2) | collective-permute-done | bytes 262176 | tf_op jit(solution)/shard_map/ppermute | solution.py:21
  165.4 3.5 collective-permute-done.3
  168.9 1.7 collective-permute-done.6
  170.7 2.7 collective-permute-start.7
  174.4 2.2 collective-permute-start.16
  180.2 7.7 %fusion.277 = (f32[4,512]{1,0:T(4,128)S(1)}, f32[4,512,1024]{1,2,0:T(8,128)}) fusion(pred[512,1024]{0,1:T(8,128)(4,1)} %get-tuple-element.70, bf16[512,4,128]{2,1,0:T(4,128)(2,1)} %reshape_reshape_squeeze.19, bf16[512,128]{1,0:T(8,128)(2,1)S(1)} %bitcast.654, bf16[512,128]{1,0:T(8,128)(2,1)} %get-tuple-element.56), kind=kOutput, calls=%fused_computation.405 | convolution fusion | flops 545784832 | bytes 9707520 | tf_op jit(solution)/shard_map/sub | solution.py:106
  187.9 4.8 %fusion.28 = bf16[4,512,1024]{1,2,0:T(8,128)(2,1)S(1)} fusion(f32[4,512,1024]{1,2,0:T(8,128)} %get-tuple-element.76, f32[4,512]{1,0:T(4,128)S(1)} %get-tuple-element.75), kind=kLoop, calls=%fused_computation.46 | loop fusion | flops 4194304 | bytes 12591104 | tf_op jit(solution)/shard_map/convert_element_type | solution.py:112
  194.3 2.3 fusion.9
  196.6 2.1 copy-done.15
  200.8 7.6 %fusion.286 = (f32[4,512]{1,0:T(4,128)S(1)}, f32[4,512,1024]{1,2,0:T(8,128)}) fusion(pred[512,1024]{0,1:T(8,128)(4,1)} %get-tuple-element.67, bf16[512,4,128]{2,1,0:T(4,128)(2,1)S(1)} %copy-done.43, bf16[512,128]{1,0:T(8,128)(2,1)S(1)} %bitcast.655, bf16[512,128]{1,0:T(8,128)(2,1)} %get-tuple-element.54), kind=kOutput, calls=%fused_computation.406 | convolution fusion | flops 545784832 | bytes 9707520 | tf_op jit(solution)/shard_map/sub | solution.py:106
  209.5 1.7 collective-permute-start.17
  212.3 1.8 collective-permute-start.20
  214.9 4.5 %collective-permute-done.20 = bf16[4,128,128]{2,1,0:T(8,128)(2,1)S(1)} collective-permute-done((bf16[4,128,128]{2,1,0:T(8,128)(2,1)S(1)}, bf16[4,128,128]{2,1,0:T(8,128)(2,1)S(1)}, u32[]{:S(2)}, u32[]{:S(2)}) %collective-permute-start.20) | collective-permute-done | bytes 131104 | tf_op jit(solution)/shard_map/ppermute | solution.py:21
  220.4 4.2 %fusion.68 = bf16[512,4,128]{0,2,1:T(8,128)(2,1)S(1)} fusion(f32[4,512,1024]{1,2,0:T(8,128)} %get-tuple-element.78, f32[4,512]{1,0:T(4,128)S(1)} %get-tuple-element.77, bf16[512,128]{1,0:T(8,128)(2,1)S(1)} %bitcast.659, bf16[512,128]{1,0:T(8,128)(2,1)S(1)} %copy-done.64), kind=kOutput, calls=%fused_computation.113 | convolution fusion | flops 541851648 | bytes 9183232 | tf_op jit(solution)/shard_map/gts,sd->tgd/dot_general | solution.py:113
  226.1 6.5 %fusion.295 = (f32[4,512]{1,0:T(4,128)S(1)}, f32[4,512,1024]{1,2,0:T(8,128)}) fusion(pred[512,1024]{0,1:T(8,128)(4,1)S(1)} %copy-done.56, bf16[512,4,128]{2,1,0:T(4,128)(2,1)S(1)} %copy-done.42, bf16[512,128]{1,0:T(8,128)(2,1)S(1)} %bitcast.648, bf16[512,128]{1,0:T(8,128)(2,1)S(1)} %get-tuple-element.60), kind=kOutput, calls=%fused_computation.407 | convolution fusion | flops 545784832 | bytes 9707520 | tf_op jit(solution)/shard_map/sub | solution.py:106
  232.5 4.8 %fusion.29 = bf16[4,512,1024]{1,2,0:T(8,128)(2,1)S(1)} fusion(f32[4,512,1024]{1,2,0:T(8,128)} %get-tuple-element.80, f32[4,512]{1,0:T(4,128)S(1)} %get-tuple-element.79), kind=kLoop, calls=%fused_computation.47 | loop fusion | flops 4194304 | bytes 12591104 | tf_op jit(solution)/shard_map/convert_element_type | solution.py:112
  238.8 2.3 fusion.6
  241.2 1.9 copy-done.14
  248.2 2.3 collective-permute-start.10
  252.6 5.5 %collective-permute-done.10 = bf16[2,2,256,128]{3,2,0,1:T(8,128)(2,1)S(1)} collective-permute-done((bf16[2,2,256,128]{3,2,0,1:T(8,128)(2,1)S(1)}, bf16[2,2,256,128]{3,2,0,1:T(8,128)(2,1)S(1)}, u32[]{:S(2)}, u32[]{:S(2)}) %collective-permute-start.10) | collective-permute-done | bytes 262176 | tf_op jit(solution)/shard_map/ppermute | solution.py:21
  258.1 2.1 collective-permute-start.11
  260.3 2.5 collective-permute-start.24
  262.7 7.7 %fusion.304 = (f32[4,512]{1,0:T(4,128)S(1)}, f32[4,512,1024]{1,2,0:T(8,128)}) fusion(pred[512,1024]{0,1:T(8,128)(4,1)} %get-tuple-element.69, bf16[512,4,128]{2,1,0:T(4,128)(2,1)} %reshape_reshape_squeeze.21, bf16[512,128]{1,0:T(8,128)(2,1)S(1)} %bitcast.649, bf16[512,128]{1,0:T(8,128)(2,1)} %get-tuple-element.58), kind=kOutput, calls=%fused_computation.408 | convolution fusion | flops 545784832 | bytes 9707520 | tf_op jit(solution)/shard_map/sub | solution.py:106
  270.5 2.1 collective-permute-start.25
  272.8 1.8 collective-permute-start.12
  274.5 4.1 %fusion.69 = bf16[512,4,128]{0,2,1:T(8,128)(2,1)S(1)} fusion(f32[4,512,1024]{1,2,0:T(8,128)} %get-tuple-element.82, f32[4,512]{1,0:T(4,128)S(1)} %get-tuple-element.81, bf16[512,128]{1,0:T(8,128)(2,1)S(1)} %bitcast.653, bf16[512,128]{1,0:T(8,128)(2,1)S(1)} %get-tuple-element.57), kind=kOutput, calls=%fused_computation.114 | convolution fusion | flops 541851648 | bytes 9183232 | tf_op jit(solution)/shard_map/gts,sd->tgd/dot_general | solution.py:113
  278.7 5.2 %collective-permute-done.25 = bf16[4,2,256,128]{3,2,0,1:T(8,128)(2,1)S(1)} collective-permute-done((bf16[4,2,256,128]{3,2,0,1:T(8,128)(2,1)S(1)}, bf16[4,2,256,128]{3,2,0,1:T(8,128)(2,1)S(1)}, u32[]{:S(2)}, u32[]{:S(2)}) %collective-permute-start.25) | collective-permute-done | bytes 524320 | tf_op jit(solution)/shard_map/ppermute | solution.py:21
  284.1 2.6 collective-permute-start.26
  290.0 4.3 %all-to-all-start.2 = ((bf16[2,16,32,512]{3,2,0,1:T(8,128)(2,1)}), bf16[2,16,32,512]{3,2,0,1:T(8,128)(2,1)S(1)}, u32[]{:S(2)}, u32[]{:S(2)}) async-start(bf16[2,16,32,512]{3,2,0,1:T(8,128)(2,1)} %copy.205), calls=%async_computation.2 | async-start | bytes 2097152 | tf_op jit(solution)/shard_map/all_to_all | solution.py:282
  294.3 3.9 %fusion.63 = f32[128,4,512]{2,0,1:T(8,128)} fusion(bf16[4,512,1024]{1,2,0:T(8,128)(2,1)} %copy-done.14, bf16[512,128]{1,0:T(8,128)(2,1)S(1)} %bitcast.650, bf16[512,128]{1,0:T(8,128)(2,1)S(1)} %copy-done.46), kind=kOutput, calls=%fused_computation.108 | convolution fusion | flops 537919488 | bytes 5505024 | tf_op jit(solution)/shard_map/gts,sd->tgd/dot_general | solution.py:128
  301.1 2.2 maximum_select_fusion.1
  306.1 5.3 %all-to-all-done.2 = bf16[2,16,32,512]{3,2,0,1:T(8,128)(2,1)S(1)} async-done(((bf16[2,16,32,512]{3,2,0,1:T(8,128)(2,1)}), bf16[2,16,32,512]{3,2,0,1:T(8,128)(2,1)S(1)}, u32[]{:S(2)}, u32[]{:S(2)}) %all-to-all-start.2) | async-done | bytes 1048608 | tf_op jit(solution)/shard_map/all_to_all | solution.py:282
  311.4 5.0 %all-to-all-start.3 = ((bf16[2,16,32,512]{3,2,0,1:T(8,128)(2,1)}), bf16[2,16,32,512]{3,2,0,1:T(8,128)(2,1)}, u32[]{:S(2)}, u32[]{:S(2)}) async-start(bf16[2,16,32,512]{3,2,0,1:T(8,128)(2,1)} %copy.234), calls=%async_computation.3 | async-start | bytes 2097152 | tf_op jit(solution)/shard_map/all_to_all | solution.py:282
  317.3 1.6 copy.288
  318.9 1.6 copy.284
  321.0 12.7 %all-to-all-done.3 = bf16[2,16,32,512]{3,2,0,1:T(8,128)(2,1)} async-done(((bf16[2,16,32,512]{3,2,0,1:T(8,128)(2,1)}), bf16[2,16,32,512]{3,2,0,1:T(8,128)(2,1)}, u32[]{:S(2)}, u32[]{:S(2)}) %all-to-all-start.3) | async-done | bytes 1048608 | tf_op jit(solution)/shard_map/all_to_all | solution.py:282
  333.8 1.9 copy.366
  337.8 7.0 %collective-permute-start.28 = (bf16[32,8192]{1,0:T(8,128)(2,1)S(1)}, bf16[32,8192]{1,0:T(8,128)(2,1)S(1)}, u32[]{:S(2)}, u32[]{:S(2)}) collective-permute-start(bf16[32,8192]{1,0:T(8,128)(2,1)S(1)} %get-tuple-element.12), channel_id=1, source_target_pairs={{0,240},{16,0},{32,16},{48,32},{64,48},{80,64},{96,80},{112,96},{1... | collective-permute-start | bytes 1572872 | tf_op jit(solution)/shard_map/ppermute | solution.py:11
  347.2 26.0 %collective-permute-done.28 = bf16[32,8192]{1,0:T(8,128)(2,1)S(1)} collective-permute-done((bf16[32,8192]{1,0:T(8,128)(2,1)S(1)}, bf16[32,8192]{1,0:T(8,128)(2,1)S(1)}, u32[]{:S(2)}, u32[]{:S(2)}) %collective-permute-start.28) | collective-permute-done | bytes 524320 | tf_op jit(solution)/shard_map/ppermute | solution.py:11
  373.1 11.2 %collective-permute-done.29 = bf16[32,8192]{1,0:T(8,128)(2,1)S(1)} collective-permute-done((bf16[32,8192]{1,0:T(8,128)(2,1)S(1)}, bf16[32,8192]{1,0:T(8,128)(2,1)S(1)}, u32[]{:S(2)}, u32[]{:S(2)}) %collective-permute-start.29) | collective-permute-done | bytes 524320 | tf_op jit(solution)/shard_map/ppermute | solution.py:11
  (363 shorter events, 100.0 us)
Async XLA Ops:
  0.7 6.1 %copy-start.11 = (bf16[1,2,32,8192]{3,2,1,0:T(8,128)(2,1)S(1)}, bf16[1,2,32,8192]{3,2,1,0:T(8,128)(2,1)}, u32[]{:S(2)}) copy-start(bf16[1,2,32,8192]{3,2,1,0:T(8,128)(2,1)} %param.11) | copy-start | bytes 3145732
  8.3 28.2 %copy-start.68 = (f32[32]{0:T(128)}, f32[32]{0:T(128)S(1)}, u32[]{:S(2)}) copy-start(f32[32]{0:T(128)S(1)} %get-tuple-element.90) | copy-start | bytes 388
  11.0 55.6 %all-to-all-start.1 = ((bf16[3,32,16,512]{3,1,0,2:T(8,128)(2,1)}), bf16[3,32,16,512]{3,1,0,2:T(8,128)(2,1)S(1)}, u32[]{:S(2)}, u32[]{:S(2)}) async-start(bf16[3,32,16,512]{3,1,0,2:T(8,128)(2,1)} %copy.177), calls=%async_computation.1 | async-start | bytes 3145728 | tf_op jit(solution)/shard_map/all_to_all | solution.py:210
  23.5 8.7 %copy-start.63 = (bf16[1,2,32,8,128]{4,3,2,1,0:T(8,128)(2,1)S(1)}, bf16[1,2,32,8,128]{4,3,2,1,0:T(8,128)(2,1)}, u32[]{:S(2)}) copy-start(bf16[1,2,32,8,128]{4,3,2,1,0:T(8,128)(2,1)} %param.12) | copy-start | bytes 393220
  26.2 10.3 %copy-start.59 = (f32[16,512]{1,0:T(8,128)}, f32[16,512]{1,0:T(8,128)S(1)}, u32[]{:S(2)}) copy-start(f32[16,512]{1,0:T(8,128)S(1)} %mul.365) | copy-start | bytes 98308
  28.1 10.0 %copy-start.8 = (f32[4,8,16,512]{3,2,1,0:T(8,128)}, f32[4,8,16,512]{3,2,1,0:T(8,128)S(1)}, u32[]{:S(2)}) copy-start(f32[4,8,16,512]{3,2,1,0:T(8,128)S(1)} %copy.277) | copy-start | bytes 3145732
  32.2 5.8 %copy-start.33 = (bf16[4,8,16,512]{3,2,1,0:T(8,128)(2,1)S(1)}, bf16[4,8,16,512]{3,2,1,0:T(8,128)(2,1)}, u32[]{:S(2)}) copy-start(bf16[4,8,16,512]{3,2,1,0:T(8,128)(2,1)} %copy.278) | copy-start | bytes 1572868
  40.9 7.8 %copy-start.70 = (s32[1,2,2]{2,1,0:T(2,128)S(1)}, s32[1,2,2]{2,1,0:T(2,128)}, u32[]{:S(2)}) copy-start(s32[1,2,2]{2,1,0:T(2,128)} %param.17) | copy-start | bytes 52
  40.9 12.3 %copy-start.23 = (bf16[64,8,8,128]{3,1,2,0:T(8,128)(2,1)S(1)}, bf16[64,8,8,128]{3,1,2,0:T(8,128)(2,1)}, u32[]{:S(2)}) copy-start(bf16[64,8,8,128]{3,1,2,0:T(8,128)(2,1)} %get-tuple-element.15) | copy-start | bytes 3145732
  41.7 14.0 %copy-start.19 = (bf16[512,1024]{1,0:T(8,128)(2,1)}, bf16[512,1024]{1,0:T(8,128)(2,1)S(1)}, u32[]{:S(2)}) copy-start(bf16[512,1024]{1,0:T(8,128)(2,1)S(1)} %get-tuple-element.21) | copy-start | bytes 3145732
  43.2 12.6 %copy-start.22 = (bf16[64,8,8,128]{3,1,2,0:T(8,128)(2,1)S(1)}, bf16[64,8,8,128]{3,1,2,0:T(8,128)(2,1)}, u32[]{:S(2)}) copy-start(bf16[64,8,8,128]{3,1,2,0:T(8,128)(2,1)} %get-tuple-element.14) | copy-start | bytes 3145732
  67.8 35.9 %all-to-all-start = ((bf16[4,32,16,512]{3,1,0,2:T(8,128)(2,1)}), bf16[4,32,16,512]{3,1,0,2:T(8,128)(2,1)S(1)}, u32[]{:S(2)}, u32[]{:S(2)}) async-start(bf16[4,32,16,512]{3,1,0,2:T(8,128)(2,1)} %copy.174), calls=%async_computation | async-start | bytes 4194304 | tf_op jit(solution)/shard_map/all_to_all | solution.py:210
  87.2 39.1 %collective-permute-start = (bf16[4,256,1024]{2,1,0:T(8,128)(2,1)}, bf16[4,256,1024]{2,1,0:T(8,128)(2,1)}, u32[]{:S(2)}, u32[]{:S(2)}) collective-permute-start(bf16[4,256,1024]{2,1,0:T(8,128)(2,1)} %constant_dynamic-slice_fusion.1), channel_id=1, source_target_pairs={{0,1},{1,0},{2,3},{3,2},{4,5},{5,4},{6,7},{7,6},{8,9},{9,8},{10,11... | collective-permute-start | bytes 6291464 | tf_op jit(solution)/shard_map/ppermute | solution.py:21
  113.4 7.5 %copy-start.30 = (bf16[1,16,32,1,512]{4,2,1,3,0:T(8,128)(2,1)S(1)}, bf16[1,16,32,1,512]{4,2,1,3,0:T(8,128)(2,1)}, u32[]{:S(2)}) copy-start(bf16[1,16,32,1,512]{4,2,1,3,0:T(8,128)(2,1)} %get-tuple-element.26) | copy-start | bytes 1572868
  114.9 16.6 %collective-permute-start.14 = (bf16[4,256,1024]{2,1,0:T(8,128)(2,1)}, bf16[4,256,1024]{2,1,0:T(8,128)(2,1)}, u32[]{:S(2)}, u32[]{:S(2)}) collective-permute-start(bf16[4,256,1024]{2,1,0:T(8,128)(2,1)} %constant_dynamic-slice_fusion), channel_id=1, source_target_pairs={{0,1},{1,0},{2,3},{3,2},{4,5},{5,4},{6,7},{7,6},{8,9},{9,8},{10,11... | collective-permute-start | bytes 6291464 | tf_op jit(solution)/shard_map/ppermute | solution.py:21
  130.2 15.1 %collective-permute-start.1 = (bf16[4,128,512]{2,1,0:T(8,128)(2,1)S(1)}, bf16[4,128,512]{2,1,0:T(8,128)(2,1)S(1)}, u32[]{:S(2)}, u32[]{:S(2)}) collective-permute-start(bf16[4,128,512]{2,1,0:T(8,128)(2,1)S(1)} %dynamic-slice_convert_fusion.3), channel_id=1, source_target_pairs={{0,8},{1,9},{2,10},{3,11},{4,12},{5,13},{6,14},{7,15},{8,0},{9,1},... | collective-permute-start | bytes 1572872 | tf_op jit(solution)/shard_map/ppermute | solution.py:21
  131.3 14.4 %collective-permute-start.4 = (bf16[4,128,512]{2,1,0:T(8,128)(2,1)S(1)}, bf16[4,128,512]{2,1,0:T(8,128)(2,1)S(1)}, u32[]{:S(2)}, u32[]{:S(2)}) collective-permute-start(bf16[4,128,512]{2,1,0:T(8,128)(2,1)S(1)} %dynamic-slice_convert_fusion.2), channel_id=1, source_target_pairs={{0,2},{1,3},{2,0},{3,1},{4,6},{5,7},{6,4},{7,5},{8,10},{9,11},{10,... | collective-permute-start | bytes 1572872 | tf_op jit(solution)/shard_map/ppermute | solution.py:21
  134.9 38.5 %collective-permute-start.15 = (bf16[4,128,512]{2,1,0:T(8,128)(2,1)S(1)}, bf16[4,128,512]{2,1,0:T(8,128)(2,1)S(1)}, u32[]{:S(2)}, u32[]{:S(2)}) collective-permute-start(bf16[4,128,512]{2,1,0:T(8,128)(2,1)S(1)} %dynamic-slice_convert_fusion.1), channel_id=1, source_target_pairs={{0,8},{1,9},{2,10},{3,11},{4,12},{5,13},{6,14},{7,15},{8,0},{9,1},... | collective-permute-start | bytes 1572872 | tf_op jit(solution)/shard_map/ppermute | solution.py:21
  136.8 39.8 %collective-permute-start.18 = (bf16[4,128,512]{2,1,0:T(8,128)(2,1)S(1)}, bf16[4,128,512]{2,1,0:T(8,128)(2,1)S(1)}, u32[]{:S(2)}, u32[]{:S(2)}) collective-permute-start(bf16[4,128,512]{2,1,0:T(8,128)(2,1)S(1)} %dynamic-slice_convert_fusion), channel_id=1, source_target_pairs={{0,2},{1,3},{2,0},{3,1},{4,6},{5,7},{6,4},{7,5},{8,10},{9,11},{10,... | collective-permute-start | bytes 1572872 | tf_op jit(solution)/shard_map/ppermute | solution.py:21
  145.6 19.3 %collective-permute-start.2 = (bf16[4,128,256]{2,1,0:T(8,128)(2,1)S(1)}, bf16[4,128,256]{2,1,0:T(8,128)(2,1)S(1)}, u32[]{:S(2)}, u32[]{:S(2)}) collective-permute-start(bf16[4,128,256]{2,1,0:T(8,128)(2,1)S(1)} %dynamic-slice_convert_fusion.7), channel_id=1, source_target_pairs={{0,4},{1,5},{2,6},{3,7},{4,0},{5,1},{6,2},{7,3},{8,12},{9,13},{10,... | collective-permute-start | bytes 786440 | tf_op jit(solution)/shard_map/ppermute | solution.py:21
  145.9 19.2 %collective-permute-start.5 = (bf16[4,128,256]{2,1,0:T(8,128)(2,1)S(1)}, bf16[4,128,256]{2,1,0:T(8,128)(2,1)S(1)}, u32[]{:S(2)}, u32[]{:S(2)}) collective-permute-start(bf16[4,128,256]{2,1,0:T(8,128)(2,1)S(1)} %dynamic-slice_convert_fusion.6), channel_id=1, source_target_pairs={{0,8},{1,9},{2,10},{3,11},{4,12},{5,13},{6,14},{7,15},{8,0},{9,1},... | collective-permute-start | bytes 786440 | tf_op jit(solution)/shard_map/ppermute | solution.py:21
  165.0 3.9 %collective-permute-start.3 = (bf16[4,128,128]{2,1,0:T(8,128)(2,1)S(1)}, bf16[4,128,128]{2,1,0:T(8,128)(2,1)S(1)}, u32[]{:S(2)}, u32[]{:S(2)}) collective-permute-start(bf16[4,128,128]{2,1,0:T(8,128)(2,1)S(1)} %dynamic-slice_convert_fusion.11), channel_id=1, source_target_pairs={{0,2},{1,3},{2,0},{3,1},{4,6},{5,7},{6,4},{7,5},{8,10},{9,11},{10,... | collective-permute-start | bytes 393224 | tf_op jit(solution)/shard_map/ppermute | solution.py:21
  165.2 5.4 %collective-permute-start.6 = (bf16[4,128,128]{2,1,0:T(8,128)(2,1)S(1)}, bf16[4,128,128]{2,1,0:T(8,128)(2,1)S(1)}, u32[]{:S(2)}, u32[]{:S(2)}) collective-permute-start(bf16[4,128,128]{2,1,0:T(8,128)(2,1)S(1)} %dynamic-slice_convert_fusion.10), channel_id=1, source_target_pairs={{0,4},{1,5},{2,6},{3,7},{4,0},{5,1},{6,2},{7,3},{8,12},{9,13},{10,... | collective-permute-start | bytes 393224 | tf_op jit(solution)/shard_map/ppermute | solution.py:21
  170.7 7.8 %collective-permute-start.7 = (bf16[4,256,128]{2,1,0:T(8,128)(2,1)S(1)}, bf16[4,256,128]{2,1,0:T(8,128)(2,1)S(1)}, u32[]{:S(2)}, u32[]{:S(2)}) collective-permute-start(bf16[4,256,128]{2,1,0:T(8,128)(2,1)S(1)} %pad_maximum_fusion.22), channel_id=1, source_target_pairs={{0,1},{1,0},{2,3},{3,2},{4,5},{5,4},{6,7},{7,6},{8,9},{9,8},{10,11... | collective-permute-start | bytes 786440 | tf_op jit(solution)/shard_map/ppermute | solution.py:21
  174.4 34.0 %collective-permute-start.16 = (bf16[4,128,256]{2,1,0:T(8,128)(2,1)}, bf16[4,128,256]{2,1,0:T(8,128)(2,1)}, u32[]{:S(2)}, u32[]{:S(2)}) collective-permute-start(bf16[4,128,256]{2,1,0:T(8,128)(2,1)} %dynamic-slice_convert_fusion.5), channel_id=1, source_target_pairs={{0,4},{1,5},{2,6},{3,7},{4,0},{5,1},{6,2},{7,3},{8,12},{9,13},{10,... | collective-permute-start | bytes 786440 | tf_op jit(solution)/shard_map/ppermute | solution.py:21
  177.5 33.7 %collective-permute-start.19 = (bf16[4,128,256]{2,1,0:T(8,128)(2,1)}, bf16[4,128,256]{2,1,0:T(8,128)(2,1)}, u32[]{:S(2)}, u32[]{:S(2)}) collective-permute-start(bf16[4,128,256]{2,1,0:T(8,128)(2,1)} %dynamic-slice_convert_fusion.4), channel_id=1, source_target_pairs={{0,8},{1,9},{2,10},{3,11},{4,12},{5,13},{6,14},{7,15},{8,0},{9,1},... | collective-permute-start | bytes 786440 | tf_op jit(solution)/shard_map/ppermute | solution.py:21
  187.9 6.3 %slice-start = ((s8[8388608]{0:T(1024)(128)(4,1)}), s8[4194304]{0:T(1024)(128)(4,1)S(1)}, s32[]{:S(2)}) async-start(s8[8388608]{0:T(1024)(128)(4,1)} %bitcast.586), calls=%async_computation.4 | async-start | bytes 8388608
  187.9 6.3 %slice-start.1 = ((s8[8388608]{0:T(1024)(128)(4,1)}), s8[4194304]{0:T(1024)(128)(4,1)S(1)}, s32[]{:S(2)}) async-start(s8[8388608]{0:T(1024)(128)(4,1)} %bitcast.586), calls=%async_computation.5 | async-start | bytes 8388608
  193.5 6.0 %copy-start.48 = (bf16[1,512,128]{2,1,0:T(8,128)(2,1)}, bf16[1,512,128]{2,1,0:T(8,128)(2,1)S(1)}, u32[]{:S(2)}) copy-start(bf16[1,512,128]{2,1,0:T(8,128)(2,1)S(1)} %fusion.97) | copy-start | bytes 393220
  200.2 24.4 %collective-permute-start.8 = (bf16[2,512,128]{2,1,0:T(8,128)(2,1)}, bf16[2,512,128]{2,1,0:T(8,128)(2,1)}, u32[]{:S(2)}, u32[]{:S(2)}) collective-permute-start(bf16[2,512,128]{2,1,0:T(8,128)(2,1)} %pad_maximum_fusion.16), channel_id=1, source_target_pairs={{0,1},{1,0},{2,3},{3,2},{4,5},{5,4},{6,7},{7,6},{8,9},{9,8},{10,11... | collective-permute-start | bytes 786440 | tf_op jit(solution)/shard_map/ppermute | solution.py:16
  208.3 12.0 %copy-start.41 = (bf16[512,1,1,128]{3,0,2,1:T(8,128)(2,1)S(1)}, bf16[512,1,1,128]{3,0,2,1:T(8,128)(2,1)}, u32[]{:S(2)}) copy-start(bf16[512,1,1,128]{3,0,2,1:T(8,128)(2,1)} %copy.371) | copy-start | bytes 393220
  208.4 12.0 %copy-start.64 = (bf16[512,128]{1,0:T(8,128)(2,1)S(1)}, bf16[512,128]{1,0:T(8,128)(2,1)}, u32[]{:S(2)}) copy-start(bf16[512,128]{1,0:T(8,128)(2,1)} %get-tuple-element.53) | copy-start | bytes 393220
  209.5 5.4 %collective-permute-start.17 = (bf16[4,128,128]{2,1,0:T(8,128)(2,1)S(1)}, bf16[4,128,128]{2,1,0:T(8,128)(2,1)S(1)}, u32[]{:S(2)}, u32[]{:S(2)}) collective-permute-start(bf16[4,128,128]{2,1,0:T(8,128)(2,1)S(1)} %dynamic-slice_convert_fusion.9), channel_id=1, source_target_pairs={{0,2},{1,3},{2,0},{3,1},{4,6},{5,7},{6,4},{7,5},{8,10},{9,11},{10,... | collective-permute-start | bytes 393224 | tf_op jit(solution)/shard_map/ppermute | solution.py:21
  212.3 7.2 %collective-permute-start.20 = (bf16[4,128,128]{2,1,0:T(8,128)(2,1)S(1)}, bf16[4,128,128]{2,1,0:T(8,128)(2,1)S(1)}, u32[]{:S(2)}, u32[]{:S(2)}) collective-permute-start(bf16[4,128,128]{2,1,0:T(8,128)(2,1)S(1)} %dynamic-slice_convert_fusion.8), channel_id=1, source_target_pairs={{0,4},{1,5},{2,6},{3,7},{4,0},{5,1},{6,2},{7,3},{8,12},{9,13},{10,... | collective-permute-start | bytes 393224 | tf_op jit(solution)/shard_map/ppermute | solution.py:21
  219.5 6.3 %collective-permute-start.21 = (bf16[4,256,128]{2,1,0:T(8,128)(2,1)S(1)}, bf16[4,256,128]{2,1,0:T(8,128)(2,1)S(1)}, u32[]{:S(2)}, u32[]{:S(2)}) collective-permute-start(bf16[4,256,128]{2,1,0:T(8,128)(2,1)S(1)} %pad_maximum_fusion.23), channel_id=1, source_target_pairs={{0,1},{1,0},{2,3},{3,2},{4,5},{5,4},{6,7},{7,6},{8,9},{9,8},{10,11... | collective-permute-start | bytes 786440 | tf_op jit(solution)/shard_map/ppermute | solution.py:21
  225.6 21.5 %collective-permute-start.9 = (bf16[1,2,256,128]{3,2,0,1:T(8,128)(2,1)S(1)}, bf16[1,2,256,128]{3,2,0,1:T(8,128)(2,1)}, u32[]{:S(2)}, u32[]{:S(2)}) collective-permute-start(bf16[1,2,256,128]{3,2,0,1:T(8,128)(2,1)S(1)} %fusion.212), channel_id=1, source_target_pairs={{0,2},{1,3},{2,0},{3,1},{4,6},{5,7},{6,4},{7,5},{8,10},{9,11},{10,... | collective-permute-start | bytes 393224 | tf_op jit(solution)/shard_map/ppermute | solution.py:21
  226.0 6.5 %copy-start.45 = (bf16[512,128]{1,0:T(8,128)(2,1)}, bf16[512,128]{1,0:T(8,128)(2,1)S(1)}, u32[]{:S(2)}) copy-start(bf16[512,128]{1,0:T(8,128)(2,1)S(1)} %get-tuple-element.60) | copy-start | bytes 393220
  232.5 6.3 %slice-start.2 = ((s8[8388608]{0:T(1024)(128)(4,1)}), s8[4194304]{0:T(1024)(128)(4,1)S(1)}, s32[]{:S(2)}) async-start(s8[8388608]{0:T(1024)(128)(4,1)} %bitcast.588), calls=%async_computation.6 | async-start | bytes 8388608
  232.5 6.3 %slice-start.3 = ((s8[8388608]{0:T(1024)(128)(4,1)}), s8[4194304]{0:T(1024)(128)(4,1)S(1)}, s32[]{:S(2)}) async-start(s8[8388608]{0:T(1024)(128)(4,1)} %bitcast.588), calls=%async_computation.7 | async-start | bytes 8388608
  238.0 5.8 %copy-start.52 = (bf16[1,512,128]{2,1,0:T(8,128)(2,1)}, bf16[1,512,128]{2,1,0:T(8,128)(2,1)S(1)}, u32[]{:S(2)}) copy-start(bf16[1,512,128]{2,1,0:T(8,128)(2,1)S(1)} %fusion.103) | copy-start | bytes 393220
  244.6 5.9 %collective-permute-start.22 = (bf16[2,512,128]{2,1,0:T(8,128)(2,1)}, bf16[2,512,128]{2,1,0:T(8,128)(2,1)}, u32[]{:S(2)}, u32[]{:S(2)}) collective-permute-start(bf16[2,512,128]{2,1,0:T(8,128)(2,1)} %pad_maximum_fusion.21), channel_id=1, source_target_pairs={{0,1},{1,0},{2,3},{3,2},{4,5},{5,4},{6,7},{7,6},{8,9},{9,8},{10,11... | collective-permute-start | bytes 786440 | tf_op jit(solution)/shard_map/ppermute | solution.py:16
  248.2 9.9 %collective-permute-start.10 = (bf16[2,2,256,128]{3,2,0,1:T(8,128)(2,1)S(1)}, bf16[2,2,256,128]{3,2,0,1:T(8,128)(2,1)S(1)}, u32[]{:S(2)}, u32[]{:S(2)}) collective-permute-start(bf16[2,2,256,128]{3,2,0,1:T(8,128)(2,1)S(1)} %maximum_select_fusion.8), channel_id=1, source_target_pairs={{0,4},{1,5},{2,6},{3,7},{4,0},{5,1},{6,2},{7,3},{8,12},{9,13},{10,... | collective-permute-start | bytes 786440 | tf_op jit(solution)/shard_map/ppermute | solution.py:21
  251.5 8.7 %collective-permute-start.23 = (bf16[1,2,256,128]{3,2,0,1:T(8,128)(2,1)S(1)}, bf16[1,2,256,128]{3,2,0,1:T(8,128)(2,1)S(1)}, u32[]{:S(2)}, u32[]{:S(2)}) collective-permute-start(bf16[1,2,256,128]{3,2,0,1:T(8,128)(2,1)S(1)} %fusion.213), channel_id=1, source_target_pairs={{0,2},{1,3},{2,0},{3,1},{4,6},{5,7},{6,4},{7,5},{8,10},{9,11},{10,... | collective-permute-start | bytes 393224 | tf_op jit(solution)/shard_map/ppermute | solution.py:21
  258.1 14.5 %collective-permute-start.11 = (bf16[4,2,256,128]{3,2,0,1:T(8,128)(2,1)S(1)}, bf16[4,2,256,128]{3,2,0,1:T(8,128)(2,1)S(1)}, u32[]{:S(2)}, u32[]{:S(2)}) collective-permute-start(bf16[4,2,256,128]{3,2,0,1:T(8,128)(2,1)S(1)} %maximum_select_fusion.6), channel_id=1, source_target_pairs={{0,8},{1,9},{2,10},{3,11},{4,12},{5,13},{6,14},{7,15},{8,0},{9,1},... | collective-permute-start | bytes 1572872 | tf_op jit(solution)/shard_map/ppermute | solution.py:21
  260.3 10.2 %collective-permute-start.24 = (bf16[2,2,256,128]{3,2,0,1:T(8,128)(2,1)S(1)}, bf16[2,2,256,128]{3,2,0,1:T(8,128)(2,1)S(1)}, u32[]{:S(2)}, u32[]{:S(2)}) collective-permute-start(bf16[2,2,256,128]{3,2,0,1:T(8,128)(2,1)S(1)} %maximum_select_fusion.9), channel_id=1, source_target_pairs={{0,4},{1,5},{2,6},{3,7},{4,0},{5,1},{6,2},{7,3},{8,12},{9,13},{10,... | collective-permute-start | bytes 786440 | tf_op jit(solution)/shard_map/ppermute | solution.py:21
  270.5 13.4 %collective-permute-start.25 = (bf16[4,2,256,128]{3,2,0,1:T(8,128)(2,1)S(1)}, bf16[4,2,256,128]{3,2,0,1:T(8,128)(2,1)S(1)}, u32[]{:S(2)}, u32[]{:S(2)}) collective-permute-start(bf16[4,2,256,128]{3,2,0,1:T(8,128)(2,1)S(1)} %maximum_select_fusion.7), channel_id=1, source_target_pairs={{0,8},{1,9},{2,10},{3,11},{4,12},{5,13},{6,14},{7,15},{8,0},{9,1},... | collective-permute-start | bytes 1572872 | tf_op jit(solution)/shard_map/ppermute | solution.py:21
  272.8 13.9 %collective-permute-start.12 = (bf16[8,2,256,128]{3,2,0,1:T(8,128)(2,1)S(1)}, bf16[8,2,256,128]{3,2,0,1:T(8,128)(2,1)S(1)}, u32[]{:S(2)}, u32[]{:S(2)}) collective-permute-start(bf16[8,2,256,128]{3,2,0,1:T(8,128)(2,1)S(1)} %maximum_select_fusion.2), channel_id=1, source_target_pairs={{0,1},{1,0},{2,3},{3,2},{4,5},{5,4},{6,7},{7,6},{8,9},{9,8},{10,11... | collective-permute-start | bytes 3145736 | tf_op jit(solution)/shard_map/ppermute | solution.py:21
  278.7 8.6 %copy-start.39 = (bf16[64,8,8,128]{3,2,1,0:T(8,128)(2,1)S(1)}, bf16[64,8,8,128]{3,2,1,0:T(8,128)(2,1)}, u32[]{:S(2)}) copy-start(bf16[64,8,8,128]{3,2,1,0:T(8,128)(2,1)} %copy.283) | copy-start | bytes 3145732
  284.1 17.0 %collective-permute-start.26 = (bf16[8,2,256,128]{3,2,0,1:T(8,128)(2,1)S(1)}, bf16[8,2,256,128]{3,2,0,1:T(8,128)(2,1)}, u32[]{:S(2)}, u32[]{:S(2)}) collective-permute-start(bf16[8,2,256,128]{3,2,0,1:T(8,128)(2,1)S(1)} %maximum_select_fusion.3), channel_id=1, source_target_pairs={{0,1},{1,0},{2,3},{3,2},{4,5},{5,4},{6,7},{7,6},{8,9},{9,8},{10,11... | collective-permute-start | bytes 3145736 | tf_op jit(solution)/shard_map/ppermute | solution.py:21
  290.0 21.4 %all-to-all-start.2 = ((bf16[2,16,32,512]{3,2,0,1:T(8,128)(2,1)}), bf16[2,16,32,512]{3,2,0,1:T(8,128)(2,1)S(1)}, u32[]{:S(2)}, u32[]{:S(2)}) async-start(bf16[2,16,32,512]{3,2,0,1:T(8,128)(2,1)} %copy.205), calls=%async_computation.2 | async-start | bytes 2097152 | tf_op jit(solution)/shard_map/all_to_all | solution.py:282
  311.4 22.4 %all-to-all-start.3 = ((bf16[2,16,32,512]{3,2,0,1:T(8,128)(2,1)}), bf16[2,16,32,512]{3,2,0,1:T(8,128)(2,1)}, u32[]{:S(2)}, u32[]{:S(2)}) async-start(bf16[2,16,32,512]{3,2,0,1:T(8,128)(2,1)} %copy.234), calls=%async_computation.3 | async-start | bytes 2097152 | tf_op jit(solution)/shard_map/all_to_all | solution.py:282
  318.9 17.0 %copy-start.9 = (f32[4,8,16,512]{3,2,1,0:T(8,128)S(1)}, f32[4,8,16,512]{3,2,1,0:T(8,128)}, u32[]{:S(2)}) copy-start(f32[4,8,16,512]{3,2,1,0:T(8,128)} %copy-done.8) | copy-start | bytes 3145732
  318.9 17.0 %copy-start.60 = (f32[16,512]{1,0:T(8,128)S(1)}, f32[16,512]{1,0:T(8,128)}, u32[]{:S(2)}) copy-start(f32[16,512]{1,0:T(8,128)} %copy-done.59) | copy-start | bytes 98308
  318.9 17.0 %copy-start.69 = (f32[32]{0:T(128)S(1)}, f32[32]{0:T(128)}, u32[]{:S(2)}) copy-start(f32[32]{0:T(128)} %copy-done.68) | copy-start | bytes 388
  321.0 16.0 %copy-start.3 = (bf16[1,2,32,8192]{3,2,1,0:T(8,128)(2,1)S(1)}, bf16[1,2,32,8192]{3,2,1,0:T(8,128)(2,1)}, u32[]{:S(2)}) copy-start(bf16[1,2,32,8192]{3,2,1,0:T(8,128)(2,1)} %param.10) | copy-start | bytes 3145732
  321.0 16.0 %copy-start.12 = (bf16[1,2,32,8192]{3,2,1,0:T(8,128)(2,1)S(1)}, bf16[1,2,32,8192]{3,2,1,0:T(8,128)(2,1)}, u32[]{:S(2)}) copy-start(bf16[1,2,32,8192]{3,2,1,0:T(8,128)(2,1)} %param.11) | copy-start | bytes 3145732
  321.0 16.0 %copy-start.61 = (f32[1,1,8192]{2,1,0:T(1,128)S(1)}, f32[1,1,8192]{2,1,0:T(1,128)}, u32[]{:S(2)}) copy-start(f32[1,1,8192]{2,1,0:T(1,128)} %get-tuple-element.61) | copy-start | bytes 98308
  321.0 16.0 %copy-start.62 = (f32[1,1,8192]{2,1,0:T(1,128)S(1)}, f32[1,1,8192]{2,1,0:T(1,128)}, u32[]{:S(2)}) copy-start(f32[1,1,8192]{2,1,0:T(1,128)} %get-tuple-element.62) | copy-start | bytes 98308
  337.0 8.4 %copy-start.5 = (bf16[1,2,32,8192]{3,2,1,0:T(8,128)(2,1)S(1)}, bf16[1,2,32,8192]{3,2,1,0:T(8,128)(2,1)}, u32[]{:S(2)}) copy-start(bf16[1,2,32,8192]{3,2,1,0:T(8,128)(2,1)} %param.9) | copy-start | bytes 3145732
  337.0 8.4 %copy-start.24 = (f32[4,8,16,512]{3,1,2,0:T(8,128)S(1)}, f32[4,8,16,512]{3,1,2,0:T(8,128)}, u32[]{:S(2)}) copy-start(f32[4,8,16,512]{3,1,2,0:T(8,128)} %copy.284) | copy-start | bytes 3145732
  337.8 35.4 %collective-permute-start.28 = (bf16[32,8192]{1,0:T(8,128)(2,1)S(1)}, bf16[32,8192]{1,0:T(8,128)(2,1)S(1)}, u32[]{:S(2)}, u32[]{:S(2)}) collective-permute-start(bf16[32,8192]{1,0:T(8,128)(2,1)S(1)} %get-tuple-element.12), channel_id=1, source_target_pairs={{0,240},{16,0},{32,16},{48,32},{64,48},{80,64},{96,80},{112,96},{1... | collective-permute-start | bytes 1572872 | tf_op jit(solution)/shard_map/ppermute | solution.py:11
  344.7 39.6 %collective-permute-start.29 = (bf16[32,8192]{1,0:T(8,128)(2,1)S(1)}, bf16[32,8192]{1,0:T(8,128)(2,1)S(1)}, u32[]{:S(2)}, u32[]{:S(2)}) collective-permute-start(bf16[32,8192]{1,0:T(8,128)(2,1)S(1)} %get-tuple-element.13), channel_id=1, source_target_pairs={{0,240},{16,0},{32,16},{48,32},{64,48},{80,64},{96,80},{112,96},{1... | collective-permute-start | bytes 1572872 | tf_op jit(solution)/shard_map/ppermute | solution.py:11
  345.6 39.9 %collective-permute-start.27 = (bf16[32,8192]{1,0:T(8,128)(2,1)S(1)}, bf16[32,8192]{1,0:T(8,128)(2,1)S(1)}, u32[]{:S(2)}, u32[]{:S(2)}) collective-permute-start(bf16[32,8192]{1,0:T(8,128)(2,1)S(1)} %get-tuple-element.34), channel_id=1, source_target_pairs={{0,16},{16,32},{32,48},{48,64},{64,80},{80,96},{96,112},{112,128},... | collective-permute-start | bytes 1572872 | tf_op jit(solution)/shard_map/ppermute | solution.py:11
  347.1 38.6 %collective-permute-start.13 = (bf16[32,8192]{1,0:T(8,128)(2,1)S(1)}, bf16[32,8192]{1,0:T(8,128)(2,1)S(1)}, u32[]{:S(2)}, u32[]{:S(2)}) collective-permute-start(bf16[32,8192]{1,0:T(8,128)(2,1)S(1)} %get-tuple-element.33), channel_id=1, source_target_pairs={{0,16},{16,32},{32,48},{48,64},{64,80},{80,96},{96,112},{112,128},... | collective-permute-start | bytes 1572872 | tf_op jit(solution)/shard_map/ppermute | solution.py:11
  (45 other events, 124.5 us)

commit v3 on v2

--- a/solution.py
+++ b/solution.py
@@ -244,6 +244,10 @@
         forward_value_list = jnp.concatenate([cached_v, new_kv[0, 1]], axis=0)
         backward_key_list = jnp.concatenate([cached_k, new_kv[1, 0]], axis=0)
         backward_value_list = jnp.concatenate([cached_v, new_kv[1, 1]], axis=0)
+        if stretch > 0:
+            (forward_slice, backward_slice, grad_slice, new_kv), _ = lax.optimization_barrier(
+                ((forward_slice, backward_slice, grad_slice, new_kv), previous_outs)
+            )
         attended = attend(
             forward_slice.reshape(seg_len, local_heads, head_size),
             forward_key_list,
@@ -293,6 +297,7 @@
         section_grad = input_grad(
             backward_rows, gain_row, returned[1].reshape(local_rows, model_width), grad_rows
         )
+        previous_outs = (section_out, section_grad)
         forward_outs.append(passed_along(section_out, "pipe", 1))
         backward_outs.append(passed_along(section_grad, "pipe", -1))
     pipe_rank = lax.axis_index("pipe")

time: 393 us -> 425 us (1.081)
  waiting for transfers between devices: 118 us -> 127 us
  local copies, waits for them, and re-layouts: 90 us -> 98.1 us
  other arithmetic: 44.4 us -> 49.6 us
  matrix products: 62.9 us -> 67.8 us
    ppermute x4, waiting for transfers between devices: 37.4 us -> 18.5 us  [passed_along(): lax.ppermute(array, axis, [(i, (i + by) % count) for i in range(count)])]
    all_to_all x2, waiting for transfers between devices: 18.1 us -> 33.1 us  [on_device(): lax.all_to_all(jnp.stack([attended.reshape(ctx_size, local_rows, -1), gra...]
    ppermute x24, waiting for transfers between devices: 45.7 us -> 57.8 us  [swapped_with(): return lax.ppermute(array, axis, [(i, i ^ mask) for i in range(count)])]
    unnamed x198 -> x202, local copies, waits for them, and re-layouts: 49.1 us -> 42 us
    ppermute x4, starting transfers between devices: 8.58 us -> 15.6 us  [passed_along(): lax.ppermute(array, axis, [(i, (i + by) % count) for i in range(count)])]
  transfers between devices with their start and end apart: 34 -> 34, of which waited for: 14 -> 16; matrix products, arithmetic and copies ran while one was open for 44% -> 38% of each run, Pallas kernels for 0% -> 0%
where the time goes in v3:
time: 425 us; the launch traced here: 419 us
  waiting for transfers between devices  127 us (30%)
  local copies, waits for them, and re-layouts  98.1 us (23%)
  starting transfers between devices  71 us (17%)
  matrix products  67.8 us (16%)
  other arithmetic  49.6 us (12%)
  between operations  5.35 us (1%)
    ppermute x24, waiting for transfers between devices, swapped_with(): return lax.ppermute(array, axis, [(i, i ^ mask) for i in range(count)])  57.8 us
    unnamed x202, local copies, waits for them, and re-layouts  42 us
    all_to_all x2, waiting for transfers between devices, on_device(): lax.all_to_all(jnp.stack([attended.reshape(ctx_size, local_rows, -1), gra...  33.1 us
    sub x4, matrix products, probabilities(): lifted = jnp.exp(scores - row_max)  30.9 us
    ppermute x24, starting transfers between devices, swapped_with(): return lax.ppermute(array, axis, [(i, i ^ mask) for i in range(count)])  29.3 us
    ppermute x4, waiting for transfers between devices, passed_along(): lax.ppermute(array, axis, [(i, (i + by) % count) for i in range(count)])  18.5 us
    all_to_all x2, waiting for transfers between devices, on_device(): lax.all_to_all(jnp.stack(outgoing), 'ctx', split_axis=2, concat_axis=1, t...  16.8 us
    all_to_all x2, starting transfers between devices, on_device(): lax.all_to_all(jnp.stack(outgoing), 'ctx', split_axis=2, concat_axis=1, t...  16 us
  transfers between devices with their start and end apart: 34, of which 16 were waited for; matrix products, arithmetic and copies ran while one was open for 38% of the time, Pallas kernels for 0%

profile of v3, /device:TPU:1, one launch (start us, length us, event | category | flops | bytes accessed | tf_op | source)
XLA Modules:
  0.0 419.2 jit_solution(5282627117604223555)
XLA Ops:
  2.3 2.3 slice_convert_fusion.4
  7.1 1.8 copy.293
  8.9 2.2 copy.292
  12.7 2.0 copy.183
  14.7 8.8 %all-to-all-start.1 = ((bf16[3,32,16,512]{3,1,0,2:T(8,128)(2,1)}), bf16[3,32,16,512]{3,1,0,2:T(8,128)(2,1)}, u32[]{:S(2)}, u32[]{:S(2)}) async-start(bf16[3,32,16,512]{3,1,0,2:T(8,128)(2,1)} %copy.183), calls=%async_computation.1 | async-start | bytes 3145728 | tf_op jit(solution)/shard_map/all_to_all | solution.py:210
  23.6 3.7 slice_bitcast_fusion.14
  33.2 2.0 slice_bitcast_fusion.12
  38.5 1.8 copy.289
  40.3 2.0 copy.291
  47.3 2.5 copy.180
  61.9 7.2 %all-to-all-start = ((bf16[4,32,16,512]{3,1,0,2:T(8,128)(2,1)}), bf16[4,32,16,512]{3,1,0,2:T(8,128)(2,1)}, u32[]{:S(2)}, u32[]{:S(2)}) async-start(bf16[4,32,16,512]{3,1,0,2:T(8,128)(2,1)} %copy.180), calls=%async_computation | async-start | bytes 4194304 | tf_op jit(solution)/shard_map/all_to_all | solution.py:210
  76.8 2.0 copy-done
  80.9 16.8 %all-to-all-done = bf16[4,32,16,512]{3,1,0,2:T(8,128)(2,1)} async-done(((bf16[4,32,16,512]{3,1,0,2:T(8,128)(2,1)}), bf16[4,32,16,512]{3,1,0,2:T(8,128)(2,1)}, u32[]{:S(2)}, u32[]{:S(2)}) %all-to-all-start) | async-done | bytes 2097184 | tf_op jit(solution)/shard_map/all_to_all | solution.py:210
  97.7 2.0 copy.351
  101.6 1.9 fusion.47
  107.1 2.0 copy-done.1
  111.6 2.7 fusion.41
  120.2 3.1 convert_add_fusion.1
  125.5 2.5 convert_add_fusion
  128.7 1.9 collective-permute-start.9
  132.3 6.8 %collective-permute-done.1 = bf16[4,128,512]{2,1,0:T(8,128)(2,1)S(1)} collective-permute-done((bf16[4,128,512]{2,1,0:T(8,128)(2,1)S(1)}, bf16[4,128,512]{2,1,0:T(8,128)(2,1)S(1)}, u32[]{:S(2)}, u32[]{:S(2)}) %collective-permute-start.1) | collective-permute-done | bytes 524320 | tf_op jit(solution)/shard_map/ppermute | solution.py:21
  141.8 8.5 %collective-permute-done.9 = bf16[4,128,512]{2,1,0:T(8,128)(2,1)S(1)} collective-permute-done((bf16[4,128,512]{2,1,0:T(8,128)(2,1)S(1)}, bf16[4,128,512]{2,1,0:T(8,128)(2,1)S(1)}, u32[]{:S(2)}, u32[]{:S(2)}) %collective-permute-start.9) | collective-permute-done | bytes 524320 | tf_op jit(solution)/shard_map/ppermute | solution.py:21
  152.5 11.8 %collective-permute-done.10 = bf16[4,128,256]{2,1,0:T(8,128)(2,1)S(1)} collective-permute-done((bf16[4,128,256]{2,1,0:T(8,128)(2,1)S(1)}, bf16[4,128,256]{2,1,0:T(8,128)(2,1)S(1)}, u32[]{:S(2)}, u32[]{:S(2)}) %collective-permute-start.10) | collective-permute-done | bytes 262176 | tf_op jit(solution)/shard_map/ppermute | solution.py:21
  164.7 3.6 collective-permute-done.11
  170.1 2.7 collective-permute-start.15
  177.0 7.7 %fusion.268 = (f32[4,512]{1,0:T(4,128)S(1)}, f32[4,512,1024]{1,2,0:T(8,128)}) fusion(pred[512,1024]{0,1:T(8,128)(4,1)} %get-tuple-element.71, bf16[512,4,128]{2,1,0:T(4,128)(2,1)} %reshape_reshape_squeeze.10, bf16[512,128]{1,0:T(8,128)(2,1)S(1)} %bitcast.655, bf16[512,128]{1,0:T(8,128)(2,1)S(1)} %get-tuple-element.62), kind=kOutput, calls=%fused_computation.400 | convolution fusion | flops 545784832 | bytes 9707520 | tf_op jit(solution)/shard_map/sub | solution.py:106
  184.7 4.8 %fusion.28 = bf16[4,512,1024]{1,2,0:T(8,128)(2,1)S(1)} fusion(f32[4,512,1024]{1,2,0:T(8,128)} %get-tuple-element.78, f32[4,512]{1,0:T(4,128)S(1)} %get-tuple-element.77), kind=kLoop, calls=%fused_computation.46 | loop fusion | flops 4194304 | bytes 12591104 | tf_op jit(solution)/shard_map/convert_element_type | solution.py:112
  190.7 2.3 fusion.9
  196.0 2.5 collective-permute-start.6
  199.7 5.0 %collective-permute-done.17 = bf16[1,2,256,128]{3,2,0,1:T(8,128)(2,1)S(1)} collective-permute-done((bf16[1,2,256,128]{3,2,0,1:T(8,128)(2,1)S(1)}, bf16[1,2,256,128]{3,2,0,1:T(8,128)(2,1)S(1)}, u32[]{:S(2)}, u32[]{:S(2)}) %collective-permute-start.17) | collective-permute-done | bytes 131104 | tf_op jit(solution)/shard_map/ppermute | solution.py:21
  208.5 4.7 %collective-permute-done.18 = bf16[2,2,256,128]{3,2,0,1:T(8,128)(2,1)S(1)} collective-permute-done((bf16[2,2,256,128]{3,2,0,1:T(8,128)(2,1)S(1)}, bf16[2,2,256,128]{3,2,0,1:T(8,128)(2,1)S(1)}, u32[]{:S(2)}, u32[]{:S(2)}) %collective-permute-start.18) | collective-permute-done | bytes 262176 | tf_op jit(solution)/shard_map/ppermute | solution.py:21
  215.3 7.7 %fusion.277 = (f32[4,512]{1,0:T(4,128)S(1)}, f32[4,512,1024]{1,2,0:T(8,128)}) fusion(pred[512,1024]{0,1:T(8,128)(4,1)} %get-tuple-element.72, bf16[512,4,128]{2,1,0:T(4,128)(2,1)} %reshape_reshape_squeeze.9, bf16[512,128]{1,0:T(8,128)(2,1)S(1)} %bitcast.656, bf16[512,128]{1,0:T(8,128)(2,1)S(1)} %get-tuple-element.60), kind=kOutput, calls=%fused_computation.401 | convolution fusion | flops 545784832 | bytes 9707520 | tf_op jit(solution)/shard_map/sub | solution.py:106
  222.9 3.9 collective-permute-done.19
  228.5 2.9 collective-permute-start.20
  231.4 5.1 %fusion.68 = bf16[512,4,128]{0,2,1:T(8,128)(2,1)} fusion(f32[4,512,1024]{1,2,0:T(8,128)} %get-tuple-element.80, f32[4,512]{1,0:T(4,128)S(1)} %get-tuple-element.79, bf16[512,128]{1,0:T(8,128)(2,1)} %bitcast.660, bf16[512,128]{1,0:T(8,128)(2,1)} %get-tuple-element.59), kind=kOutput, calls=%fused_computation.113 | convolution fusion | flops 541851648 | bytes 9183232 | tf_op jit(solution)/shard_map/gts,sd->tgd/dot_general | solution.py:113
  236.5 2.1 copy.209
  238.6 2.0 stack_reshape.8
  240.6 4.0 fusion.59
  244.6 2.5 copy.221
  247.2 2.2 maximum_select_fusion
  252.1 4.4 %all-to-all-start.2 = ((bf16[2,16,32,512]{3,2,0,1:T(8,128)(2,1)}), bf16[2,16,32,512]{3,2,0,1:T(8,128)(2,1)S(1)}, u32[]{:S(2)}, u32[]{:S(2)}) async-start(bf16[2,16,32,512]{3,2,0,1:T(8,128)(2,1)} %copy.222), calls=%async_computation.2 | async-start | bytes 2097152 | tf_op jit(solution)/shard_map/all_to_all | solution.py:286
  261.1 12.5 %all-to-all-done.2 = bf16[2,16,32,512]{3,2,0,1:T(8,128)(2,1)S(1)} async-done(((bf16[2,16,32,512]{3,2,0,1:T(8,128)(2,1)}), bf16[2,16,32,512]{3,2,0,1:T(8,128)(2,1)S(1)}, u32[]{:S(2)}, u32[]{:S(2)}) %all-to-all-start.2) | async-done | bytes 1048608 | tf_op jit(solution)/shard_map/all_to_all | solution.py:286
  279.6 7.7 %fusion.286 = (f32[4,512]{1,0:T(4,128)S(1)}, f32[4,512,1024]{1,2,0:T(8,128)}) fusion(pred[512,1024]{0,1:T(8,128)(4,1)} %get-tuple-element.70, bf16[512,4,128]{0,2,1:T(8,128)(2,1)} %bitcast.667, bf16[512,128]{1,0:T(8,128)(2,1)S(1)} %bitcast.661, bf16[512,128]{1,0:T(8,128)(2,1)} %get-tuple-element.58), kind=kOutput, calls=%fused_computation.402 | convolution fusion | flops 545784832 | bytes 9707520 | tf_op jit(solution)/shard_map/sub | solution.py:106
  287.3 4.8 %fusion.29 = bf16[4,512,1024]{1,2,0:T(8,128)(2,1)S(1)} fusion(f32[4,512,1024]{1,2,0:T(8,128)} %get-tuple-element.82, f32[4,512]{1,0:T(4,128)S(1)} %get-tuple-element.81), kind=kLoop, calls=%fused_computation.47 | loop fusion | flops 4194304 | bytes 12591104 | tf_op jit(solution)/shard_map/convert_element_type | solution.py:112
  293.7 2.3 fusion.6
  299.1 4.7 %collective-permute-done.22 = bf16[1,2,256,128]{3,2,0,1:T(8,128)(2,1)S(1)} collective-permute-done((bf16[1,2,256,128]{3,2,0,1:T(8,128)(2,1)S(1)}, bf16[1,2,256,128]{3,2,0,1:T(8,128)(2,1)S(1)}, u32[]{:S(2)}, u32[]{:S(2)}) %collective-permute-start.22) | collective-permute-done | bytes 131104 | tf_op jit(solution)/shard_map/ppermute | solution.py:21
  308.2 4.0 collective-permute-done.23
  314.5 7.8 %fusion.291 = (f32[4,512]{1,0:T(4,128)S(1)}, f32[4,512,1024]{1,2,0:T(8,128)}) fusion(pred[512,1024]{0,1:T(8,128)(4,1)} %get-tuple-element.69, bf16[512,4,128]{0,2,1:T(8,128)(2,1)} %bitcast.669, bf16[512,128]{1,0:T(8,128)(2,1)S(1)} %bitcast.662, bf16[512,128]{1,0:T(8,128)(2,1)} %get-tuple-element.56), kind=kOutput, calls=%fused_computation.403 | convolution fusion | flops 545784832 | bytes 9707520 | tf_op jit(solution)/shard_map/sub | solution.py:106
  322.3 3.0 collective-permute-done.24
  327.0 3.1 collective-permute-start.25
  330.1 5.0 %fusion.69 = bf16[512,4,128]{0,2,1:T(8,128)(2,1)} fusion(f32[4,512,1024]{1,2,0:T(8,128)} %get-tuple-element.84, f32[4,512]{1,0:T(4,128)S(1)} %get-tuple-element.83, bf16[512,128]{1,0:T(8,128)(2,1)S(1)} %bitcast.666, bf16[512,128]{1,0:T(8,128)(2,1)} %get-tuple-element.55), kind=kOutput, calls=%fused_computation.114 | convolution fusion | flops 541851648 | bytes 9183232 | tf_op jit(solution)/shard_map/gts,sd->tgd/dot_general | solution.py:113
  335.2 2.1 copy.228
  337.3 2.0 stack_reshape.10
  339.3 3.9 fusion.63
  343.2 2.5 copy.241
  345.8 2.2 maximum_select_fusion.1
  350.7 4.4 %all-to-all-start.3 = ((bf16[2,16,32,512]{3,2,0,1:T(8,128)(2,1)}), bf16[2,16,32,512]{3,2,0,1:T(8,128)(2,1)}, u32[]{:S(2)}, u32[]{:S(2)}) async-start(bf16[2,16,32,512]{3,2,0,1:T(8,128)(2,1)} %copy.242), calls=%async_computation.3 | async-start | bytes 2097152 | tf_op jit(solution)/shard_map/all_to_all | solution.py:286
  355.1 7.6 %collective-permute-start.29 = (bf16[32,8192]{1,0:T(8,128)(2,1)}, bf16[32,8192]{1,0:T(8,128)(2,1)}, u32[]{:S(2)}, u32[]{:S(2)}) collective-permute-start(bf16[32,8192]{1,0:T(8,128)(2,1)} %fusion.115), channel_id=1, source_target_pairs={{0,240},{16,0},{32,16},{48,32},{64,48},{80,64},{96,80},{112,96},{1... | collective-permute-start | bytes 1572872 | tf_op jit(solution)/shard_map/ppermute | solution.py:11
  363.0 20.6 %all-to-all-done.3 = bf16[2,16,32,512]{3,2,0,1:T(8,128)(2,1)} async-done(((bf16[2,16,32,512]{3,2,0,1:T(8,128)(2,1)}), bf16[2,16,32,512]{3,2,0,1:T(8,128)(2,1)}, u32[]{:S(2)}, u32[]{:S(2)}) %all-to-all-start.3) | async-done | bytes 1048608 | tf_op jit(solution)/shard_map/all_to_all | solution.py:286
  383.6 1.9 copy.353
  387.3 7.6 %collective-permute-start.28 = (bf16[32,8192]{1,0:T(8,128)(2,1)S(1)}, bf16[32,8192]{1,0:T(8,128)(2,1)S(1)}, u32[]{:S(2)}, u32[]{:S(2)}) collective-permute-start(bf16[32,8192]{1,0:T(8,128)(2,1)S(1)} %fusion.114), channel_id=1, source_target_pairs={{0,240},{16,0},{32,16},{48,32},{64,48},{80,64},{96,80},{112,96},{1... | collective-permute-start | bytes 1572872 | tf_op jit(solution)/shard_map/ppermute | solution.py:11
  395.8 18.5 %collective-permute-done.28 = bf16[32,8192]{1,0:T(8,128)(2,1)S(1)} collective-permute-done((bf16[32,8192]{1,0:T(8,128)(2,1)S(1)}, bf16[32,8192]{1,0:T(8,128)(2,1)S(1)}, u32[]{:S(2)}, u32[]{:S(2)}) %collective-permute-start.28) | collective-permute-done | bytes 524320 | tf_op jit(solution)/shard_map/ppermute | solution.py:11
  414.3 2.3 maximum_select_fusion.5
  416.6 2.3 maximum_select_fusion.4
  (369 shorter events, 112.2 us)
Async XLA Ops:
  0.6 5.7 %copy-start.69 = (f32[1,2,8192]{2,1,0:T(2,128)S(1)}, f32[1,2,8192]{2,1,0:T(2,128)}, u32[]{:S(2)}) copy-start(f32[1,2,8192]{2,1,0:T(2,128)} %param.14) | copy-start | bytes 196612
  4.6 6.6 %copy-start.11 = (bf16[1,2,32,8192]{3,2,1,0:T(8,128)(2,1)S(1)}, bf16[1,2,32,8192]{3,2,1,0:T(8,128)(2,1)}, u32[]{:S(2)}) copy-start(bf16[1,2,32,8192]{3,2,1,0:T(8,128)(2,1)} %param.11) | copy-start | bytes 3145732
  14.7 47.2 %all-to-all-start.1 = ((bf16[3,32,16,512]{3,1,0,2:T(8,128)(2,1)}), bf16[3,32,16,512]{3,1,0,2:T(8,128)(2,1)}, u32[]{:S(2)}, u32[]{:S(2)}) async-start(bf16[3,32,16,512]{3,1,0,2:T(8,128)(2,1)} %copy.183), calls=%async_computation.1 | async-start | bytes 3145728 | tf_op jit(solution)/shard_map/all_to_all | solution.py:210
  23.6 9.5 %copy-start.31 = (bf16[1,2,512,1024]{3,2,1,0:T(8,128)(2,1)S(1)}, bf16[1,2,512,1024]{3,2,1,0:T(8,128)(2,1)}, u32[]{:S(2)}) copy-start(bf16[1,2,512,1024]{3,2,1,0:T(8,128)(2,1)} %param.16) | copy-start | bytes 6291460
  27.4 7.8 %copy-start.16 = (bf16[512,1024]{1,0:T(8,128)(2,1)}, bf16[512,1024]{1,0:T(8,128)(2,1)S(1)}, u32[]{:S(2)}) copy-start(bf16[512,1024]{1,0:T(8,128)(2,1)S(1)} %get-tuple-element.20) | copy-start | bytes 3145732
  27.4 7.8 %copy-start.17 = (bf16[512,1024]{1,0:T(8,128)(2,1)}, bf16[512,1024]{1,0:T(8,128)(2,1)S(1)}, u32[]{:S(2)}) copy-start(bf16[512,1024]{1,0:T(8,128)(2,1)S(1)} %get-tuple-element.21) | copy-start | bytes 3145732
  35.2 7.2 %copy-start.68 = (bf16[1,2,32,8,128]{4,3,2,1,0:T(8,128)(2,1)S(1)}, bf16[1,2,32,8,128]{4,3,2,1,0:T(8,128)(2,1)}, u32[]{:S(2)}) copy-start(bf16[1,2,32,8,128]{4,3,2,1,0:T(8,128)(2,1)} %param.12) | copy-start | bytes 393220
  37.9 8.8 %copy-start.64 = (f32[16,512]{1,0:T(8,128)}, f32[16,512]{1,0:T(8,128)S(1)}, u32[]{:S(2)}) copy-start(f32[16,512]{1,0:T(8,128)S(1)} %mul.365) | copy-start | bytes 98308
  47.0 6.0 %copy-start.25 = (bf16[64,8,8,128]{3,1,2,0:T(8,128)(2,1)S(1)}, bf16[64,8,8,128]{3,1,2,0:T(8,128)(2,1)}, u32[]{:S(2)}) copy-start(bf16[64,8,8,128]{3,1,2,0:T(8,128)(2,1)} %get-tuple-element.23) | copy-start | bytes 3145732
  47.3 7.0 %copy-start.24 = (bf16[64,8,8,128]{3,1,2,0:T(8,128)(2,1)S(1)}, bf16[64,8,8,128]{3,1,2,0:T(8,128)(2,1)}, u32[]{:S(2)}) copy-start(bf16[64,8,8,128]{3,1,2,0:T(8,128)(2,1)} %get-tuple-element.19) | copy-start | bytes 3145732
  47.3 8.3 %copy-start.19 = (bf16[512,1024]{1,0:T(8,128)(2,1)S(1)}, bf16[512,1024]{1,0:T(8,128)(2,1)}, u32[]{:S(2)}) copy-start(bf16[512,1024]{1,0:T(8,128)(2,1)} %copy-done.18) | copy-start | bytes 3145732
  61.9 35.8 %all-to-all-start = ((bf16[4,32,16,512]{3,1,0,2:T(8,128)(2,1)}), bf16[4,32,16,512]{3,1,0,2:T(8,128)(2,1)}, u32[]{:S(2)}, u32[]{:S(2)}) async-start(bf16[4,32,16,512]{3,1,0,2:T(8,128)(2,1)} %copy.180), calls=%async_computation | async-start | bytes 4194304 | tf_op jit(solution)/shard_map/all_to_all | solution.py:210
  80.4 39.8 %collective-permute-start = (bf16[4,256,1024]{2,1,0:T(8,128)(2,1)}, bf16[4,256,1024]{2,1,0:T(8,128)(2,1)}, u32[]{:S(2)}, u32[]{:S(2)}) collective-permute-start(bf16[4,256,1024]{2,1,0:T(8,128)(2,1)} %constant_dynamic-slice_fusion.1), channel_id=1, source_target_pairs={{0,1},{1,0},{2,3},{3,2},{4,5},{5,4},{6,7},{7,6},{8,9},{9,8},{10,11... | collective-permute-start | bytes 6291464 | tf_op jit(solution)/shard_map/ppermute | solution.py:21
  110.6 14.7 %collective-permute-start.8 = (bf16[4,256,1024]{2,1,0:T(8,128)(2,1)}, bf16[4,256,1024]{2,1,0:T(8,128)(2,1)}, u32[]{:S(2)}, u32[]{:S(2)}) collective-permute-start(bf16[4,256,1024]{2,1,0:T(8,128)(2,1)} %constant_dynamic-slice_fusion), channel_id=1, source_target_pairs={{0,1},{1,0},{2,3},{3,2},{4,5},{5,4},{6,7},{7,6},{8,9},{9,8},{10,11... | collective-permute-start | bytes 6291464 | tf_op jit(solution)/shard_map/ppermute | solution.py:21
  118.9 71.4 %copy-start.53 = (bf16[512,1,1,128]{3,0,2,1:T(8,128)(2,1)}, bf16[512,1,1,128]{3,0,2,1:T(8,128)(2,1)S(1)}, u32[]{:S(2)}) copy-start(bf16[512,1,1,128]{3,0,2,1:T(8,128)(2,1)S(1)} %copy.356) | copy-start | bytes 393220
  124.0 15.1 %collective-permute-start.1 = (bf16[4,128,512]{2,1,0:T(8,128)(2,1)S(1)}, bf16[4,128,512]{2,1,0:T(8,128)(2,1)S(1)}, u32[]{:S(2)}, u32[]{:S(2)}) collective-permute-start(bf16[4,128,512]{2,1,0:T(8,128)(2,1)S(1)} %dynamic-slice_convert_fusion.3), channel_id=1, source_target_pairs={{0,8},{1,9},{2,10},{3,11},{4,12},{5,13},{6,14},{7,15},{8,0},{9,1},... | collective-permute-start | bytes 1572872 | tf_op jit(solution)/shard_map/ppermute | solution.py:21
  125.1 14.4 %collective-permute-start.4 = (bf16[4,128,512]{2,1,0:T(8,128)(2,1)S(1)}, bf16[4,128,512]{2,1,0:T(8,128)(2,1)S(1)}, u32[]{:S(2)}, u32[]{:S(2)}) collective-permute-start(bf16[4,128,512]{2,1,0:T(8,128)(2,1)S(1)} %dynamic-slice_convert_fusion.2), channel_id=1, source_target_pairs={{0,2},{1,3},{2,0},{3,1},{4,6},{5,7},{6,4},{7,5},{8,10},{9,11},{10,... | collective-permute-start | bytes 1572872 | tf_op jit(solution)/shard_map/ppermute | solution.py:21
  128.7 21.7 %collective-permute-start.9 = (bf16[4,128,512]{2,1,0:T(8,128)(2,1)S(1)}, bf16[4,128,512]{2,1,0:T(8,128)(2,1)S(1)}, u32[]{:S(2)}, u32[]{:S(2)}) collective-permute-start(bf16[4,128,512]{2,1,0:T(8,128)(2,1)S(1)} %dynamic-slice_convert_fusion.1), channel_id=1, source_target_pairs={{0,8},{1,9},{2,10},{3,11},{4,12},{5,13},{6,14},{7,15},{8,0},{9,1},... | collective-permute-start | bytes 1572872 | tf_op jit(solution)/shard_map/ppermute | solution.py:21
  130.6 20.1 %collective-permute-start.12 = (bf16[4,128,512]{2,1,0:T(8,128)(2,1)S(1)}, bf16[4,128,512]{2,1,0:T(8,128)(2,1)S(1)}, u32[]{:S(2)}, u32[]{:S(2)}) collective-permute-start(bf16[4,128,512]{2,1,0:T(8,128)(2,1)S(1)} %dynamic-slice_convert_fusion), channel_id=1, source_target_pairs={{0,2},{1,3},{2,0},{3,1},{4,6},{5,7},{6,4},{7,5},{8,10},{9,11},{10,... | collective-permute-start | bytes 1572872 | tf_op jit(solution)/shard_map/ppermute | solution.py:21
  139.4 33.4 %collective-permute-start.2 = (bf16[4,128,256]{2,1,0:T(8,128)(2,1)S(1)}, bf16[4,128,256]{2,1,0:T(8,128)(2,1)S(1)}, u32[]{:S(2)}, u32[]{:S(2)}) collective-permute-start(bf16[4,128,256]{2,1,0:T(8,128)(2,1)S(1)} %dynamic-slice_convert_fusion.7), channel_id=1, source_target_pairs={{0,4},{1,5},{2,6},{3,7},{4,0},{5,1},{6,2},{7,3},{8,12},{9,13},{10,... | collective-permute-start | bytes 786440 | tf_op jit(solution)/shard_map/ppermute | solution.py:21
  140.5 54.5 %collective-permute-start.5 = (bf16[4,128,256]{2,1,0:T(8,128)(2,1)}, bf16[4,128,256]{2,1,0:T(8,128)(2,1)}, u32[]{:S(2)}, u32[]{:S(2)}) collective-permute-start(bf16[4,128,256]{2,1,0:T(8,128)(2,1)} %dynamic-slice_convert_fusion.6), channel_id=1, source_target_pairs={{0,8},{1,9},{2,10},{3,11},{4,12},{5,13},{6,14},{7,15},{8,0},{9,1},... | collective-permute-start | bytes 786440 | tf_op jit(solution)/shard_map/ppermute | solution.py:21
  150.6 13.6 %collective-permute-start.10 = (bf16[4,128,256]{2,1,0:T(8,128)(2,1)S(1)}, bf16[4,128,256]{2,1,0:T(8,128)(2,1)S(1)}, u32[]{:S(2)}, u32[]{:S(2)}) collective-permute-start(bf16[4,128,256]{2,1,0:T(8,128)(2,1)S(1)} %dynamic-slice_convert_fusion.5), channel_id=1, source_target_pairs={{0,4},{1,5},{2,6},{3,7},{4,0},{5,1},{6,2},{7,3},{8,12},{9,13},{10,... | collective-permute-start | bytes 786440 | tf_op jit(solution)/shard_map/ppermute | solution.py:21
  151.0 13.5 %collective-permute-start.13 = (bf16[4,128,256]{2,1,0:T(8,128)(2,1)S(1)}, bf16[4,128,256]{2,1,0:T(8,128)(2,1)S(1)}, u32[]{:S(2)}, u32[]{:S(2)}) collective-permute-start(bf16[4,128,256]{2,1,0:T(8,128)(2,1)S(1)} %dynamic-slice_convert_fusion.4), channel_id=1, source_target_pairs={{0,8},{1,9},{2,10},{3,11},{4,12},{5,13},{6,14},{7,15},{8,0},{9,1},... | collective-permute-start | bytes 786440 | tf_op jit(solution)/shard_map/ppermute | solution.py:21
  164.4 3.9 collective-permute-start.11
  164.6 5.4 %collective-permute-start.14 = (bf16[4,128,128]{2,1,0:T(8,128)(2,1)S(1)}, bf16[4,128,128]{2,1,0:T(8,128)(2,1)S(1)}, u32[]{:S(2)}, u32[]{:S(2)}) collective-permute-start(bf16[4,128,128]{2,1,0:T(8,128)(2,1)S(1)} %dynamic-slice_convert_fusion.8), channel_id=1, source_target_pairs={{0,4},{1,5},{2,6},{3,7},{4,0},{5,1},{6,2},{7,3},{8,12},{9,13},{10,... | collective-permute-start | bytes 393224 | tf_op jit(solution)/shard_map/ppermute | solution.py:21
  170.1 5.2 %collective-permute-start.15 = (bf16[4,256,128]{2,1,0:T(8,128)(2,1)S(1)}, bf16[4,256,128]{2,1,0:T(8,128)(2,1)S(1)}, u32[]{:S(2)}, u32[]{:S(2)}) collective-permute-start(bf16[4,256,128]{2,1,0:T(8,128)(2,1)S(1)} %pad_maximum_fusion.23), channel_id=1, source_target_pairs={{0,1},{1,0},{2,3},{3,2},{4,5},{5,4},{6,7},{7,6},{8,9},{9,8},{10,11... | collective-permute-start | bytes 786440 | tf_op jit(solution)/shard_map/ppermute | solution.py:21
  173.6 25.1 %collective-permute-start.3 = (bf16[4,128,128]{2,1,0:T(8,128)(2,1)}, bf16[4,128,128]{2,1,0:T(8,128)(2,1)}, u32[]{:S(2)}, u32[]{:S(2)}) collective-permute-start(bf16[4,128,128]{2,1,0:T(8,128)(2,1)} %dynamic-slice_convert_fusion.11), channel_id=1, source_target_pairs={{0,2},{1,3},{2,0},{3,1},{4,6},{5,7},{6,4},{7,5},{8,10},{9,11},{10,... | collective-permute-start | bytes 393224 | tf_op jit(solution)/shard_map/ppermute | solution.py:21
  177.0 7.7 %copy-start.59 = (bf16[512,128]{1,0:T(8,128)(2,1)}, bf16[512,128]{1,0:T(8,128)(2,1)S(1)}, u32[]{:S(2)}) copy-start(bf16[512,128]{1,0:T(8,128)(2,1)S(1)} %get-tuple-element.62) | copy-start | bytes 393220
  184.7 5.6 %slice-start.2 = ((s8[8388608]{0:T(1024)(128)(4,1)}), s8[4194304]{0:T(1024)(128)(4,1)S(1)}, s32[]{:S(2)}) async-start(s8[8388608]{0:T(1024)(128)(4,1)} %bitcast.591), calls=%async_computation.6 | async-start | bytes 8388608
  184.7 6.0 %slice-start.3 = ((s8[8388608]{0:T(1024)(128)(4,1)}), s8[4194304]{0:T(1024)(128)(4,1)S(1)}, s32[]{:S(2)}) async-start(s8[8388608]{0:T(1024)(128)(4,1)} %bitcast.591), calls=%async_computation.7 | async-start | bytes 8388608
  193.1 5.6 %copy-start.43 = (f32[4,128,256]{2,1,0:T(8,128)S(1)}, f32[4,128,256]{2,1,0:T(8,128)}, u32[]{:S(2)}) copy-start(f32[4,128,256]{2,1,0:T(8,128)} %copy-done.42) | copy-start | bytes 1572868
  193.8 20.8 %copy-start.52 = (bf16[1,2,512,128]{3,2,1,0:T(8,128)(2,1)S(1)}, bf16[1,2,512,128]{3,2,1,0:T(8,128)(2,1)}, u32[]{:S(2)}) copy-start(bf16[1,2,512,128]{3,2,1,0:T(8,128)(2,1)} %get-tuple-element.51) | copy-start | bytes 786436
  194.5 4.0 collective-permute-start.16
  196.0 10.4 %collective-permute-start.6 = (bf16[4,128,128]{2,1,0:T(8,128)(2,1)S(1)}, bf16[4,128,128]{2,1,0:T(8,128)(2,1)S(1)}, u32[]{:S(2)}, u32[]{:S(2)}) collective-permute-start(bf16[4,128,128]{2,1,0:T(8,128)(2,1)S(1)} %dynamic-slice_convert_fusion.10), channel_id=1, source_target_pairs={{0,4},{1,5},{2,6},{3,7},{4,0},{5,1},{6,2},{7,3},{8,12},{9,13},{10,... | collective-permute-start | bytes 393224 | tf_op jit(solution)/shard_map/ppermute | solution.py:21
  198.6 6.0 %collective-permute-start.17 = (bf16[1,2,256,128]{3,2,0,1:T(8,128)(2,1)S(1)}, bf16[1,2,256,128]{3,2,0,1:T(8,128)(2,1)S(1)}, u32[]{:S(2)}, u32[]{:S(2)}) collective-permute-start(bf16[1,2,256,128]{3,2,0,1:T(8,128)(2,1)S(1)} %fusion.200), channel_id=1, source_target_pairs={{0,2},{1,3},{2,0},{3,1},{4,6},{5,7},{6,4},{7,5},{8,10},{9,11},{10,... | collective-permute-start | bytes 393224 | tf_op jit(solution)/shard_map/ppermute | solution.py:21
  204.7 8.5 %collective-permute-start.18 = (bf16[2,2,256,128]{3,2,0,1:T(8,128)(2,1)S(1)}, bf16[2,2,256,128]{3,2,0,1:T(8,128)(2,1)S(1)}, u32[]{:S(2)}, u32[]{:S(2)}) collective-permute-start(bf16[2,2,256,128]{3,2,0,1:T(8,128)(2,1)S(1)} %maximum_select_fusion.8), channel_id=1, source_target_pairs={{0,4},{1,5},{2,6},{3,7},{4,0},{5,1},{6,2},{7,3},{8,12},{9,13},{10,... | collective-permute-start | bytes 786440 | tf_op jit(solution)/shard_map/ppermute | solution.py:21
  207.2 51.9 %collective-permute-start.7 = (bf16[4,256,128]{2,1,0:T(8,128)(2,1)}, bf16[4,256,128]{2,1,0:T(8,128)(2,1)}, u32[]{:S(2)}, u32[]{:S(2)}) collective-permute-start(bf16[4,256,128]{2,1,0:T(8,128)(2,1)} %pad_maximum_fusion.22), channel_id=1, source_target_pairs={{0,1},{1,0},{2,3},{3,2},{4,5},{5,4},{6,7},{7,6},{8,9},{9,8},{10,11... | collective-permute-start | bytes 786440 | tf_op jit(solution)/shard_map/ppermute | solution.py:21
  213.2 9.8 %copy-start.36 = (bf16[4,2,256,128]{3,2,0,1:T(8,128)(2,1)}, bf16[4,2,256,128]{3,2,0,1:T(8,128)(2,1)S(1)}, u32[]{:S(2)}) copy-start(bf16[4,2,256,128]{3,2,0,1:T(8,128)(2,1)S(1)} %maximum_select_fusion.6) | copy-start | bytes 1572868
  213.2 13.7 %collective-permute-start.19 = (bf16[4,2,256,128]{3,2,0,1:T(8,128)(2,1)S(1)}, bf16[4,2,256,128]{3,2,0,1:T(8,128)(2,1)}, u32[]{:S(2)}, u32[]{:S(2)}) collective-permute-start(bf16[4,2,256,128]{3,2,0,1:T(8,128)(2,1)S(1)} %maximum_select_fusion.6), channel_id=1, source_target_pairs={{0,8},{1,9},{2,10},{3,11},{4,12},{5,13},{6,14},{7,15},{8,0},{9,1},... | collective-permute-start | bytes 1572872 | tf_op jit(solution)/shard_map/ppermute | solution.py:21
  228.5 18.6 %collective-permute-start.20 = (bf16[8,2,256,128]{3,2,0,1:T(8,128)(2,1)S(1)}, bf16[8,2,256,128]{3,2,0,1:T(8,128)(2,1)}, u32[]{:S(2)}, u32[]{:S(2)}) collective-permute-start(bf16[8,2,256,128]{3,2,0,1:T(8,128)(2,1)S(1)} %maximum_select_fusion.2), channel_id=1, source_target_pairs={{0,1},{1,0},{2,3},{3,2},{4,5},{5,4},{6,7},{7,6},{8,9},{9,8},{10,11... | collective-permute-start | bytes 3145736 | tf_op jit(solution)/shard_map/ppermute | solution.py:21
  252.1 21.5 %all-to-all-start.2 = ((bf16[2,16,32,512]{3,2,0,1:T(8,128)(2,1)}), bf16[2,16,32,512]{3,2,0,1:T(8,128)(2,1)S(1)}, u32[]{:S(2)}, u32[]{:S(2)}) async-start(bf16[2,16,32,512]{3,2,0,1:T(8,128)(2,1)} %copy.222), calls=%async_computation.2 | async-start | bytes 2097152 | tf_op jit(solution)/shard_map/all_to_all | solution.py:286
  287.3 6.3 %slice-start = ((s8[8388608]{0:T(1024)(128)(4,1)}), s8[4194304]{0:T(1024)(128)(4,1)S(1)}, s32[]{:S(2)}) async-start(s8[8388608]{0:T(1024)(128)(4,1)} %bitcast.589), calls=%async_computation.4 | async-start | bytes 8388608
  287.3 6.3 %slice-start.1 = ((s8[8388608]{0:T(1024)(128)(4,1)}), s8[4194304]{0:T(1024)(128)(4,1)S(1)}, s32[]{:S(2)}) async-start(s8[8388608]{0:T(1024)(128)(4,1)} %bitcast.589), calls=%async_computation.5 | async-start | bytes 8388608
  296.0 12.2 %copy-start.15 = (bf16[4,512,1024]{1,2,0:T(8,128)(2,1)}, bf16[4,512,1024]{1,2,0:T(8,128)(2,1)S(1)}, u32[]{:S(2)}) copy-start(bf16[4,512,1024]{1,2,0:T(8,128)(2,1)S(1)} %fusion.6) | copy-start | bytes 12582916
  296.1 9.6 %copy-start.22 = (bf16[64,8,8,128]{3,1,2,0:T(8,128)(2,1)S(1)}, bf16[64,8,8,128]{3,1,2,0:T(8,128)(2,1)}, u32[]{:S(2)}) copy-start(bf16[64,8,8,128]{3,1,2,0:T(8,128)(2,1)} %get-tuple-element.22) | copy-start | bytes 3145732
  296.1 10.9 %copy-start.21 = (bf16[64,8,8,128]{3,1,2,0:T(8,128)(2,1)S(1)}, bf16[64,8,8,128]{3,1,2,0:T(8,128)(2,1)}, u32[]{:S(2)}) copy-start(bf16[64,8,8,128]{3,1,2,0:T(8,128)(2,1)} %get-tuple-element.18) | copy-start | bytes 3145732
  296.8 16.7 %copy-start.8 = (bf16[1,16,32,1,512]{4,2,1,3,0:T(8,128)(2,1)S(1)}, bf16[1,16,32,1,512]{4,2,1,3,0:T(8,128)(2,1)}, u32[]{:S(2)}) copy-start(bf16[1,16,32,1,512]{4,2,1,3,0:T(8,128)(2,1)} %copy-done.7) | copy-start | bytes 1572868
  296.8 2.2 collective-permute-start.21
  299.0 4.8 %collective-permute-start.22 = (bf16[1,2,256,128]{3,2,0,1:T(8,128)(2,1)S(1)}, bf16[1,2,256,128]{3,2,0,1:T(8,128)(2,1)S(1)}, u32[]{:S(2)}, u32[]{:S(2)}) collective-permute-start(bf16[1,2,256,128]{3,2,0,1:T(8,128)(2,1)S(1)} %fusion.201), channel_id=1, source_target_pairs={{0,2},{1,3},{2,0},{3,1},{4,6},{5,7},{6,4},{7,5},{8,10},{9,11},{10,... | collective-permute-start | bytes 393224 | tf_op jit(solution)/shard_map/ppermute | solution.py:21
  303.9 8.4 %collective-permute-start.23 = (bf16[2,2,256,128]{3,2,0,1:T(8,128)(2,1)S(1)}, bf16[2,2,256,128]{3,2,0,1:T(8,128)(2,1)S(1)}, u32[]{:S(2)}, u32[]{:S(2)}) collective-permute-start(bf16[2,2,256,128]{3,2,0,1:T(8,128)(2,1)S(1)} %maximum_select_fusion.9), channel_id=1, source_target_pairs={{0,4},{1,5},{2,6},{3,7},{4,0},{5,1},{6,2},{7,3},{8,12},{9,13},{10,... | collective-permute-start | bytes 786440 | tf_op jit(solution)/shard_map/ppermute | solution.py:21
  312.3 10.0 %copy-start.35 = (bf16[4,2,256,128]{3,2,0,1:T(8,128)(2,1)}, bf16[4,2,256,128]{3,2,0,1:T(8,128)(2,1)S(1)}, u32[]{:S(2)}) copy-start(bf16[4,2,256,128]{3,2,0,1:T(8,128)(2,1)S(1)} %maximum_select_fusion.7) | copy-start | bytes 1572868
  312.3 13.0 %collective-permute-start.24 = (bf16[4,2,256,128]{3,2,0,1:T(8,128)(2,1)S(1)}, bf16[4,2,256,128]{3,2,0,1:T(8,128)(2,1)}, u32[]{:S(2)}, u32[]{:S(2)}) collective-permute-start(bf16[4,2,256,128]{3,2,0,1:T(8,128)(2,1)S(1)} %maximum_select_fusion.7), channel_id=1, source_target_pairs={{0,8},{1,9},{2,10},{3,11},{4,12},{5,13},{6,14},{7,15},{8,0},{9,1},... | collective-permute-start | bytes 1572872 | tf_op jit(solution)/shard_map/ppermute | solution.py:21
  314.5 15.6 %copy-start.55 = (bf16[512,1,1,128]{3,0,2,1:T(8,128)(2,1)S(1)}, bf16[512,1,1,128]{3,0,2,1:T(8,128)(2,1)}, u32[]{:S(2)}) copy-start(bf16[512,1,1,128]{3,0,2,1:T(8,128)(2,1)} %copy.358) | copy-start | bytes 393220
  327.0 18.7 %collective-permute-start.25 = (bf16[8,2,256,128]{3,2,0,1:T(8,128)(2,1)S(1)}, bf16[8,2,256,128]{3,2,0,1:T(8,128)(2,1)}, u32[]{:S(2)}, u32[]{:S(2)}) collective-permute-start(bf16[8,2,256,128]{3,2,0,1:T(8,128)(2,1)S(1)} %maximum_select_fusion.3), channel_id=1, source_target_pairs={{0,1},{1,0},{2,3},{3,2},{4,5},{5,4},{6,7},{7,6},{8,9},{9,8},{10,11... | collective-permute-start | bytes 3145736 | tf_op jit(solution)/shard_map/ppermute | solution.py:21
  330.1 9.2 %copy-start.58 = (bf16[512,128]{1,0:T(8,128)(2,1)S(1)}, bf16[512,128]{1,0:T(8,128)(2,1)}, u32[]{:S(2)}) copy-start(bf16[512,128]{1,0:T(8,128)(2,1)} %get-tuple-element.58) | copy-start | bytes 393220
  350.7 35.1 %copy-start.6 = (f32[4,8,16,512]{3,2,1,0:T(8,128)S(1)}, f32[4,8,16,512]{3,2,1,0:T(8,128)}, u32[]{:S(2)}) copy-start(f32[4,8,16,512]{3,2,1,0:T(8,128)} %copy-done.5) | copy-start | bytes 3145732
  350.7 35.1 %copy-start.63 = (f32[16,512]{1,0:T(8,128)S(1)}, f32[16,512]{1,0:T(8,128)}, u32[]{:S(2)}) copy-start(f32[16,512]{1,0:T(8,128)} %copy-done.62) | copy-start | bytes 98308
  350.7 35.1 %copy-start.71 = (f32[32]{0:T(128)S(1)}, f32[32]{0:T(128)}, u32[]{:S(2)}) copy-start(f32[32]{0:T(128)} %copy-done.70) | copy-start | bytes 388
  350.7 32.9 %all-to-all-start.3 = ((bf16[2,16,32,512]{3,2,0,1:T(8,128)(2,1)}), bf16[2,16,32,512]{3,2,0,1:T(8,128)(2,1)}, u32[]{:S(2)}, u32[]{:S(2)}) async-start(bf16[2,16,32,512]{3,2,0,1:T(8,128)(2,1)} %copy.242), calls=%async_computation.3 | async-start | bytes 2097152 | tf_op jit(solution)/shard_map/all_to_all | solution.py:286
  355.1 31.8 %copy-start.66 = (f32[1,1,8192]{2,1,0:T(1,128)S(1)}, f32[1,1,8192]{2,1,0:T(1,128)}, u32[]{:S(2)}) copy-start(f32[1,1,8192]{2,1,0:T(1,128)} %get-tuple-element.63) | copy-start | bytes 98308
  355.1 40.6 %collective-permute-start.29 = (bf16[32,8192]{1,0:T(8,128)(2,1)}, bf16[32,8192]{1,0:T(8,128)(2,1)}, u32[]{:S(2)}, u32[]{:S(2)}) collective-permute-start(bf16[32,8192]{1,0:T(8,128)(2,1)} %fusion.115), channel_id=1, source_target_pairs={{0,240},{16,0},{32,16},{48,32},{64,48},{80,64},{96,80},{112,96},{1... | collective-permute-start | bytes 1572872 | tf_op jit(solution)/shard_map/ppermute | solution.py:11
  362.7 53.9 %collective-permute-start.27 = (bf16[32,8192]{1,0:T(8,128)(2,1)}, bf16[32,8192]{1,0:T(8,128)(2,1)}, u32[]{:S(2)}, u32[]{:S(2)}) collective-permute-start(bf16[32,8192]{1,0:T(8,128)(2,1)} %fusion.133), channel_id=1, source_target_pairs={{0,16},{16,32},{32,48},{48,64},{64,80},{80,96},{96,112},{112,128},... | collective-permute-start | bytes 1572872 | tf_op jit(solution)/shard_map/ppermute | solution.py:11
  387.3 27.0 %collective-permute-start.28 = (bf16[32,8192]{1,0:T(8,128)(2,1)S(1)}, bf16[32,8192]{1,0:T(8,128)(2,1)S(1)}, u32[]{:S(2)}, u32[]{:S(2)}) collective-permute-start(bf16[32,8192]{1,0:T(8,128)(2,1)S(1)} %fusion.114), channel_id=1, source_target_pairs={{0,240},{16,0},{32,16},{48,32},{64,48},{80,64},{96,80},{112,96},{1... | collective-permute-start | bytes 1572872 | tf_op jit(solution)/shard_map/ppermute | solution.py:11
  395.6 21.0 %collective-permute-start.26 = (bf16[32,8192]{1,0:T(8,128)(2,1)S(1)}, bf16[32,8192]{1,0:T(8,128)(2,1)S(1)}, u32[]{:S(2)}, u32[]{:S(2)}) collective-permute-start(bf16[32,8192]{1,0:T(8,128)(2,1)S(1)} %fusion.135), channel_id=1, source_target_pairs={{0,16},{16,32},{32,48},{48,64},{64,80},{80,96},{96,112},{112,128},... | collective-permute-start | bytes 1572872 | tf_op jit(solution)/shard_map/ppermute | solution.py:11
  (47 other events, 133.4 us)
